TPU v7x, 256 devices: a whole 4x4x8 slice. The times are simulated.
256 devices in a mesh: seq: 32 (over x, y, core), chan: 4 (over z_hi), rep: 2 (over z_lo).
Axes of the slice: x: 4, y: 4, z: 8 (z_hi: 4, z_lo: 2; z = z_hi * 2 + z_lo), core: 2. Of those that a mesh axis runs over, the one named last changes fastest.
Arguments:
- tokens: bfloat16 [24576, 8192], P(('rep', 'seq'), 'chan'), parts along dimension 0, may hold values from -6 to 6
- w_in: bfloat16 [1024, 3, 8192], P('chan', None, 'seq'), may hold values from -0.0625 to 0.0625
- short_taps: float32 [3, 3, 1024], P(None, None, 'chan'), may hold values from -3 to 3
- decay: float32 [16, 1024], P(None, 'chan'), may hold values from 2.0345053e-05 to 0.03
- residue: float32 [16, 1024], P(None, 'chan'), may hold values from -2 to 2
- skip: float32 [1024], P('chan'), may hold values from -2.5 to 2.5
- w_out: bfloat16 [1024, 8192], P(None, 'chan'), may hold values from -0.1875 to 0.1875
Outputs:
- mixed: bfloat16 [24576, 8192], P(('rep', 'seq'), 'chan'), parts along dimension 0
There are 2 independent parts, one for each index of `rep`. A program takes and returns all parts, laid end to end along the dimension named above; an argument that names none is the same for every part. Nothing has to cross between parts.
All inputs are finite; a program needn't handle non-finite values.
Results may differ from a plain program's by a relative error of at most 0.0079.
Values may be sent and summed in bfloat16 or wider, within the bound.
No kernel may reach another device: no remote copies, remote signals or barrier semaphores. Data moves between devices by JAX's collectives and lax.ppermute only.
A program may use at most 128 MiB of HBM per device.

v0:
```python
import math

import jax
import jax.numpy as jnp
from jax import lax
from jax.sharding import PartitionSpec as P


def from_behind(value, axis, steps):
    count = lax.axis_size(axis)
    leading, last = (max(0, -steps), min(count, count - steps))
    return lax.ppermute(value, axis, [(source, source + steps) for source in range(leading, last)])


def hidot(form, left, right):
    return jnp.einsum(
        form, left, right, precision=lax.Precision.HIGHEST, preferred_element_type=jnp.float32
    )


def make_tables(rows_a, cols_b, total_n):
    idx_a = jnp.arange(rows_a, dtype=jnp.int32)
    idx_b = jnp.arange(cols_b, dtype=jnp.int32)
    prod_a = idx_a[:, None] * idx_a[None, :] % rows_a
    ang_a = 2.0 * math.pi / rows_a * prod_a.astype(jnp.float32)
    prod_b = idx_b[:, None] * idx_b[None, :] % cols_b
    ang_b = 2.0 * math.pi / cols_b * prod_b.astype(jnp.float32)
    prod_t = idx_a[:, None] * idx_b[None, :]
    ang_t = 2.0 * math.pi / total_n * prod_t.astype(jnp.float32)
    return (
        jnp.cos(ang_a),
        jnp.sin(ang_a),
        jnp.cos(ang_b),
        jnp.sin(ang_b),
        jnp.cos(ang_t),
        -jnp.sin(ang_t),
    )


def forward_dft(signal, tables):
    cos_a, sin_a, cos_b, sin_b, tw_c, tw_s = tables
    half = signal.shape[1]
    re_one = hidot("ka,pab->pkb", cos_a[:, :half], signal)
    im_one = -hidot("ka,pab->pkb", sin_a[:, :half], signal)
    re_two = re_one * tw_c - im_one * tw_s
    im_two = re_one * tw_s + im_one * tw_c
    spec_re = hidot("pkb,bq->pkq", re_two, cos_b) + hidot("pkb,bq->pkq", im_two, sin_b)
    spec_im = hidot("pkb,bq->pkq", im_two, cos_b) - hidot("pkb,bq->pkq", re_two, sin_b)
    return (spec_re, spec_im)


def inverse_dft(spec_re, spec_im, tables, half, total_n):
    cos_a, sin_a, cos_b, sin_b, tw_c, tw_s = tables
    re_one = hidot("pkq,qb->pkb", spec_re, cos_b) - hidot("pkq,qb->pkb", spec_im, sin_b)
    im_one = hidot("pkq,qb->pkb", spec_re, sin_b) + hidot("pkq,qb->pkb", spec_im, cos_b)
    re_two = re_one * tw_c + im_one * tw_s
    im_two = im_one * tw_c - re_one * tw_s
    out_rows = hidot("ak,pkb->pab", cos_a[:half, :], re_two) - hidot(
        "ak,pkb->pab", sin_a[:half, :], im_two
    )
    return out_rows / total_n


def ring_shift(value, axis, steps):
    count = lax.axis_size(axis)
    return lax.ppermute(value, axis, [(source, (source + steps) % count) for source in range(count)])


def chan_pieces(tokens):
    count = lax.axis_size("chan")
    width = tokens.shape[1]
    if count != 4:
        return [(step, 0, width, ring_shift(tokens, "chan", step)) for step in range(1, count)]
    half = width // 2
    ahead_lo = ring_shift(tokens[:, :half], "chan", 1)
    behind_hi = ring_shift(tokens[:, half:], "chan", -1)
    far_lo = ring_shift(ahead_lo, "chan", 1)
    far_hi = ring_shift(behind_hi, "chan", -1)
    ahead_hi = ring_shift(tokens[:, half:], "chan", 1)
    behind_lo = ring_shift(tokens[:, :half], "chan", -1)
    return [
        (1, 0, half, ahead_lo),
        (-1, half, width, behind_hi),
        (1, half, width, ahead_hi),
        (-1, 0, half, behind_lo),
        (2, 0, half, far_lo),
        (2, half, width, far_hi),
    ]


def on_device(tokens, w_in, short_taps, decay, residue, skip, w_out):
    seq_count = lax.axis_size("seq")
    seq_rank = lax.axis_index("seq")
    chan_count = lax.axis_size("chan")
    chan_rank = lax.axis_index("chan")
    tok_rows = tokens.shape[0]
    width = tokens.shape[1]
    ch_dev = w_in.shape[0]
    per_dev = ch_dev // seq_count
    w_full = lax.all_gather(w_in, "seq", axis=2, tiled=True)

    def block_of(step, lo, hi):
        index = (chan_rank - step) % chan_count
        return lax.dynamic_slice_in_dim(w_full, index * width + lo, hi - lo, axis=2)

    qkv = jnp.einsum("cgd,td->cgt", block_of(0, 0, width), tokens, preferred_element_type=jnp.float32)
    for step, lo, hi, piece in chan_pieces(tokens):
        qkv = qkv + jnp.einsum(
            "cgd,td->cgt", block_of(step, lo, hi), piece, preferred_element_type=jnp.float32
        )
    qkv_b = qkv.astype(jnp.bfloat16)
    taps_n = short_taps.shape[0]
    rim_rows = qkv_b[:, :, tok_rows - (taps_n - 1) :]
    prior = from_behind(rim_rows, "seq", 1)
    extended = lax.optimization_barrier(jnp.concatenate([prior, qkv_b], axis=2)).astype(jnp.float32)
    taps = short_taps.transpose(2, 1, 0)
    feat = jnp.zeros((ch_dev, 3, tok_rows), jnp.float32)
    for j in range(taps_n):
        feat = (
            feat
            + taps[:, :, j : j + 1] * extended[:, :, taps_n - 1 - j : taps_n - 1 - j + tok_rows]
        )
    query = feat[:, 0]
    zprod = (feat[:, 1] * feat[:, 2]).astype(jnp.bfloat16)
    whole_seq = lax.all_to_all(
        zprod.reshape(seq_count, per_dev, tok_rows), "seq", split_axis=0, concat_axis=0, tiled=True
    )
    length = tok_rows * seq_count
    total_n = 2 * length
    rows_a = 2 * seq_count
    z_f = lax.optimization_barrier(whole_seq).astype(jnp.float32).transpose(1, 0, 2)
    rates = lax.dynamic_slice_in_dim(decay, seq_rank * per_dev, per_dev, 1)
    weights = lax.dynamic_slice_in_dim(residue, seq_rank * per_dev, per_dev, 1)
    direct = lax.dynamic_slice_in_dim(skip, seq_rank * per_dev, per_dev, 0)
    tables = make_tables(rows_a, tok_rows, total_n)
    z_re, z_im = forward_dft(z_f, tables)
    times = jnp.arange(length, dtype=jnp.float32)
    filt = jnp.zeros((per_dev, length), jnp.float32)
    for m in range(rates.shape[0]):
        rate = rates[m][:, None]
        filt = filt + weights[m][:, None] * jnp.sqrt(rate) * jnp.exp(-rate * times[None, :])
    h_re, h_im = forward_dft(filt.reshape(per_dev, seq_count, tok_rows), tables)
    prod_re = z_re * h_re - z_im * h_im
    prod_im = z_re * h_im + z_im * h_re
    conv = inverse_dft(prod_re, prod_im, tables, seq_count, total_n)
    longc = (conv + direct[:, None, None] * z_f).astype(jnp.bfloat16)
    returned = lax.all_to_all(
        longc.transpose(1, 0, 2), "seq", split_axis=0, concat_axis=0, tiled=True
    )
    long_f = lax.optimization_barrier(returned.reshape(ch_dev, tok_rows)).astype(jnp.float32)
    gated = (query * long_f).astype(jnp.bfloat16)
    def rows_of(step):
        index = (chan_rank - step) % chan_count
        return lax.dynamic_slice_in_dim(w_out, index * ch_dev, ch_dev, axis=0)

    shifts = [step if step <= chan_count // 2 else step - chan_count for step in range(1, chan_count)]
    arrived = [(step, ring_shift(gated, "chan", step)) for step in shifts]
    mixed = jnp.einsum("ct,ce->te", gated, rows_of(0), preferred_element_type=jnp.float32)
    for step, piece in arrived:
        mixed = mixed + jnp.einsum(
            "ct,ce->te", piece, rows_of(step), preferred_element_type=jnp.float32
        )
    return mixed.astype(jnp.bfloat16)


def solution(mesh):
    placed = (
        P(("rep", "seq"), "chan"),
        P("chan", None, "seq"),
        P(None, None, "chan"),
        P(None, "chan"),
        P(None, "chan"),
        P("chan"),
        P(None, "chan"),
    )
    return jax.shard_map(
        on_device, mesh=mesh, in_specs=placed, out_specs=P(("rep", "seq"), "chan"), check_vma=False
    )
```

profile of v0, /device:TPU:1, one launch (start us, length us, event | category | flops | bytes accessed | tf_op | source)
XLA Modules:
  0.0 235.0 jit_solution(8011731295941108)
XLA Ops:
  6.5 0.7 all-gather.2.cloned.1.call-update
  7.3 2.6 %fusion.222 = (bf16[384,1024]{1,0:T(8,128)(2,1)}, bf16[384,1024]{1,0:T(8,128)(2,1)}) fusion(bf16[384,2048]{1,0:T(8,128)(2,1)} %param.7), kind=kLoop, calls=%fused_computation.255 | loop fusion | bytes 3145728 | tf_op jit(solution)/shard_map/slice | solution.py:75
  9.9 6.8 %collective-permute-start.1 = (bf16[384,1024]{1,0:T(8,128)(2,1)}, bf16[384,1024]{1,0:T(8,128)(2,1)}, u32[]{:S(2)}, u32[]{:S(2)}) collective-permute-start(bf16[384,1024]{1,0:T(8,128)(2,1)} %get-tuple-element.8), channel_id=1, source_target_pairs={{0,6},{2,0},{4,2},{6,4},{1,7},{3,1},{5,3},{7,5},{8,14},{10,8},{12,... | collective-permute-start | bytes 2359304 | tf_op jit(solution)/shard_map/ppermute | solution.py:66
  16.8 3.6 %collective-permute-start.3 = (bf16[384,1024]{1,0:T(8,128)(2,1)}, bf16[384,1024]{1,0:T(8,128)(2,1)}, u32[]{:S(2)}, u32[]{:S(2)}) collective-permute-start(bf16[384,1024]{1,0:T(8,128)(2,1)} %get-tuple-element.7), channel_id=1, source_target_pairs={{0,6},{2,0},{4,2},{6,4},{1,7},{3,1},{5,3},{7,5},{8,14},{10,8},{12,... | collective-permute-start | bytes 2359304 | tf_op jit(solution)/shard_map/ppermute | solution.py:66
  20.3 0.2 collective-permute-start
  20.6 0.2 fusion.182
  20.8 0.1 fusion.157
  21.0 0.1 fusion.156
  21.1 0.4 sine_negate_fusion
  21.5 1.9 convolution_bitcast_fusion
  23.4 1.9 fusion.36
  25.4 3.9 %fusion.82 = f32[8,64,384]{2,1,0:T(8,128)S(1)} fusion(f32[8,64,384]{2,1,0:T(8,128)S(1)} %fusion.36, f32[8,64,384]{2,1,0:T(8,128)S(1)} %convolution_bitcast_fusion, f32[64,384]{1,0:T(8,128)S(1)} %get-tuple-element.44, f32[64,384]{1,0:T(8,128)S(1)} %get-tuple-element.45), kind=kOutput, calls=%fused_computation.89 | convolution fusion | flops 907886592 | bytes 2555904 | tf_op jit(solution)/shard_map/pkb,bq->pkq/dot_general | solution.py:16
  29.3 5.3 %convolution_add_fusion.1 = f32[8,64,384]{2,1,0:T(8,128)} fusion(f32[8,64,384]{2,1,0:T(8,128)S(1)} %fusion.82, f32[8,64,384]{2,1,0:T(8,128)S(1)} %fusion.36, f32[8,64,384]{2,1,0:T(8,128)S(1)} %convolution_bitcast_fusion, f32[64,384]{1,0:T(8,128)S(1)} %get-tuple-element.44, f32[64,384]{1,0:T(8,128)S(1)} %get-tuple-element.45), kind=kOutput, calls=%fused_computation.27 | convolution fusion | flops 908083200 | bytes 3342336 | tf_op jit(solution)/shard_map/pkb,bq->pkq/dot_general | solution.py:16
  34.6 4.8 %fusion.78 = f32[8,64,384]{2,1,0:T(8,128)} fusion(f32[8,64,384]{2,1,0:T(8,128)S(1)} %fusion.36, f32[8,64,384]{2,1,0:T(8,128)S(1)} %convolution_bitcast_fusion, f32[64,384]{1,0:T(8,128)S(1)} %get-tuple-element.44, f32[64,384]{1,0:T(8,128)S(1)} %get-tuple-element.45), kind=kOutput, calls=%fused_computation.85 | convolution fusion | flops 907886592 | bytes 2555904 | tf_op jit(solution)/shard_map/pkb,bq->pkq/dot_general | solution.py:16
  39.3 20.6 %collective-permute-done.1 = bf16[384,1024]{1,0:T(8,128)(2,1)} collective-permute-done((bf16[384,1024]{1,0:T(8,128)(2,1)}, bf16[384,1024]{1,0:T(8,128)(2,1)}, u32[]{:S(2)}, u32[]{:S(2)}) %collective-permute-start.1) | collective-permute-done | bytes 786464 | tf_op jit(solution)/shard_map/ppermute | solution.py:66
  59.9 5.9 %collective-permute-start.5 = (bf16[384,1024]{1,0:T(8,128)(2,1)}, bf16[384,1024]{1,0:T(8,128)(2,1)}, u32[]{:S(2)}, u32[]{:S(2)}) collective-permute-start(bf16[384,1024]{1,0:T(8,128)(2,1)} %collective-permute-done.1), channel_id=1, source_target_pairs={{0,6},{2,0},{4,2},{6,4},{1,7},{3,1},{5,3},{7,5},{8,14},{10,8},{12,... | collective-permute-start | bytes 2359304 | tf_op jit(solution)/shard_map/ppermute | solution.py:66
  65.8 22.5 %all-gather.2.cloned.1.call-done = bf16[256,3,8192]{2,0,1:T(8,128)(2,1)} async-done(((bf16[256,3,256]{2,0,1:T(8,128)(2,1)}), bf16[256,3,8192]{2,0,1:T(8,128)(2,1)}) %all-gather.2.cloned.1.call-update) | async-done | bytes 12582928 | tf_op jit(solution)/shard_map/all_gather | solution.py:100
  88.3 2.8 %fusion.11 = f32[256,3,384]{2,0,1:T(8,128)S(1)} fusion(bf16[256,3,8192]{2,0,1:T(8,128)(2,1)} %all-gather.2.cloned.1.call-done, s32[]{:T(128)S(6)} %select_n.120, bf16[384,1024]{1,0:T(8,128)(2,1)} %collective-permute-done.1), kind=kOutput, calls=%fused_computation.12 | convolution fusion | flops 603979776 | bytes 3538948 | tf_op jit(solution)/shard_map/cgd,td->cgt/dot_general | solution.py:108
  91.0 3.2 %fusion.9 = f32[256,3,384]{2,0,1:T(8,128)S(1)} fusion(bf16[256,3,8192]{2,0,1:T(8,128)(2,1)} %all-gather.2.cloned.1.call-done, s32[]{:T(128)S(6)} %select_n.121, bf16[384,1024]{1,0:T(8,128)(2,1)} %collective-permute-done.2), kind=kOutput, calls=%fused_computation.10 | convolution fusion | flops 603979776 | bytes 3538948 | tf_op jit(solution)/shard_map/cgd,td->cgt/dot_general | solution.py:108
  94.3 4.6 %collective-permute-done.3 = bf16[384,1024]{1,0:T(8,128)(2,1)} collective-permute-done((bf16[384,1024]{1,0:T(8,128)(2,1)}, bf16[384,1024]{1,0:T(8,128)(2,1)}, u32[]{:S(2)}, u32[]{:S(2)}) %collective-permute-start.3) | collective-permute-done | bytes 786464 | tf_op jit(solution)/shard_map/ppermute | solution.py:66
  98.9 2.6 %fusion.7 = f32[256,3,384]{2,0,1:T(8,128)S(1)} fusion(bf16[256,3,8192]{2,0,1:T(8,128)(2,1)} %all-gather.2.cloned.1.call-done, s32[]{:T(128)S(6)} %select_n.122, bf16[384,1024]{1,0:T(8,128)(2,1)} %collective-permute-done.3), kind=kOutput, calls=%fused_computation.8 | convolution fusion | flops 603979776 | bytes 3538948 | tf_op jit(solution)/shard_map/cgd,td->cgt/dot_general | solution.py:108
  101.5 0.0 copy-start.3
  101.5 14.2 %collective-permute-done.5 = bf16[384,1024]{1,0:T(8,128)(2,1)} collective-permute-done((bf16[384,1024]{1,0:T(8,128)(2,1)}, bf16[384,1024]{1,0:T(8,128)(2,1)}, u32[]{:S(2)}, u32[]{:S(2)}) %collective-permute-start.5) | collective-permute-done | bytes 786464 | tf_op jit(solution)/shard_map/ppermute | solution.py:66
  115.7 2.6 %fusion.3 = f32[256,3,384]{2,0,1:T(8,128)S(1)} fusion(bf16[256,3,8192]{2,0,1:T(8,128)(2,1)} %all-gather.2.cloned.1.call-done, s32[]{:T(128)S(6)} %select_n.125, bf16[384,1024]{1,0:T(8,128)(2,1)} %collective-permute-done.5), kind=kOutput, calls=%fused_computation.4 | convolution fusion | flops 603979776 | bytes 3538948 | tf_op jit(solution)/shard_map/cgd,td->cgt/dot_general | solution.py:108
  118.3 1.8 fusion
  120.2 2.2 fusion.30
  122.4 0.0 copy-start.8
  122.4 2.2 fusion.33
  124.6 0.1 slice.201
  124.7 6.5 %collective-permute-start.6 = (bf16[256,3,2]{2,0,1:T(8,128)(2,1)S(1)}, bf16[256,3,2]{2,0,1:T(8,128)(2,1)S(1)}, u32[]{:S(2)}, u32[]{:S(2)}) collective-permute-start(bf16[256,3,2]{2,0,1:T(8,128)(2,1)S(1)} %slice.201), channel_id=1, source_target_pairs={{0,8},{8,16},{16,24},{24,32},{32,40},{40,48},{48,56},{56,64},{64,7... | collective-permute-start | bytes 9224 | tf_op jit(solution)/shard_map/ppermute | solution.py:12
  131.3 0.1 dynamic_slice.51
  131.4 2.5 %collective-permute-done.6 = bf16[256,3,2]{2,0,1:T(8,128)(2,1)S(1)} collective-permute-done((bf16[256,3,2]{2,0,1:T(8,128)(2,1)S(1)}, bf16[256,3,2]{2,0,1:T(8,128)(2,1)S(1)}, u32[]{:S(2)}, u32[]{:S(2)}) %collective-permute-start.6) | collective-permute-done | bytes 3104 | tf_op jit(solution)/shard_map/ppermute | solution.py:12
  133.8 0.4 pad_maximum_fusion
  134.2 0.2 convert_element_type.100
  134.4 1.1 fusion.40
  135.5 0.7 fusion.146
  136.2 8.6 %all-to-all-start = ((bf16[32,8,384]{2,1,0:T(8,128)(2,1)}), bf16[32,8,384]{2,1,0:T(8,128)(2,1)S(1)}, u32[]{:S(2)}, u32[]{:S(2)}) async-start(bf16[32,8,384]{2,1,0:T(8,128)(2,1)} %fusion.146), calls=%async_computation | async-start | bytes 393216 | tf_op jit(solution)/shard_map/all_to_all | solution.py:125
  144.8 5.9 %convolution_subtract_fusion.1 = f32[8,64,384]{2,1,0:T(8,128)} fusion(f32[8,64,384]{2,1,0:T(8,128)} %fusion.78, f32[8,64,384]{2,1,0:T(8,128)S(1)} %fusion.36, f32[8,64,384]{2,1,0:T(8,128)S(1)} %convolution_bitcast_fusion, f32[64,384]{1,0:T(8,128)S(1)} %get-tuple-element.44, f32[64,384]{1,0:T(8,128)S(1)} %get-tuple-element.45), kind=kOutput, calls=%fused_computation.25 | convolution fusion | flops 908083200 | bytes 3342336 | tf_op jit(solution)/shard_map/pkb,bq->pkq/dot_general | solution.py:16
  150.7 2.2 all-to-all-done
  152.9 0.5 convolution_bitcast_fusion.1
  153.5 0.5 fusion.37
  154.0 3.9 %fusion.80 = f32[8,64,384]{2,1,0:T(8,128)S(1)} fusion(f32[8,64,384]{2,1,0:T(8,128)S(1)} %fusion.37, f32[8,64,384]{2,1,0:T(8,128)S(1)} %convolution_bitcast_fusion.1, f32[64,384]{1,0:T(8,128)S(1)} %get-tuple-element.44, f32[64,384]{1,0:T(8,128)S(1)} %get-tuple-element.45), kind=kOutput, calls=%fused_computation.87 | convolution fusion | flops 907886592 | bytes 2555904 | tf_op jit(solution)/shard_map/pkb,bq->pkq/dot_general | solution.py:16
  157.9 4.1 %fusion.84 = f32[8,64,384]{2,1,0:T(8,128)S(1)} fusion(f32[8,64,384]{2,1,0:T(8,128)S(1)} %fusion.37, f32[8,64,384]{2,1,0:T(8,128)S(1)} %convolution_bitcast_fusion.1, f32[64,384]{1,0:T(8,128)S(1)} %get-tuple-element.44, f32[64,384]{1,0:T(8,128)S(1)} %get-tuple-element.45), kind=kOutput, calls=%fused_computation.91 | convolution fusion | flops 907886592 | bytes 2555904 | tf_op jit(solution)/shard_map/pkb,bq->pkq/dot_general | solution.py:16
  162.0 0.0 copy-start.2
  162.0 3.9 %convolution_add_fusion.2 = f32[8,64,384]{2,1,0:T(8,128)S(1)} fusion(f32[8,64,384]{2,1,0:T(8,128)S(1)} %fusion.84, f32[8,64,384]{2,1,0:T(8,128)S(1)} %fusion.37, f32[8,64,384]{2,1,0:T(8,128)S(1)} %convolution_bitcast_fusion.1, f32[64,384]{1,0:T(8,128)S(1)} %get-tuple-element.44, f32[64,384]{1,0:T(8,128)S(1)} %get-tuple-element.45), kind=kOutput, calls=%fused_computation.31 | convolution fusion | flops 908083200 | bytes 3342336 | tf_op jit(solution)/shard_map/pkb,bq->pkq/dot_general | solution.py:16
  165.9 4.0 %multiply_add_fusion = (f32[8,64,384]{2,1,0:T(8,128)S(1)}, f32[8,64,384]{2,1,0:T(8,128)S(1)}) fusion(f32[8,64,384]{2,1,0:T(8,128)S(1)} %copy-done.1, f32[8,64,384]{2,1,0:T(8,128)S(1)} %convolution_add_fusion.2, f32[8,64,384]{2,1,0:T(8,128)S(1)} %copy-done.2, f32[8,64,384]{2,1,0:T(8,128)S(1)} %fusion.80, f32[8,64,384]{2,1,0:T(8,128)S(1)} %fusion.37, ...), kind=kOutput, calls=%fused_computation.67 | convolution fusion | flops 909262848 | bytes 6488064 | tf_op jit(solution)/shard_map/pkb,bq->pkq/dot_general | solution.py:16
  169.9 4.3 %fusion.76 = f32[8,64,384]{2,1,0:T(8,128)S(1)} fusion(f32[8,64,384]{2,1,0:T(8,128)S(1)} %get-tuple-element.6), kind=kOutput, calls=%fused_computation.83 | convolution fusion | flops 907296768 | bytes 1572864 | tf_op jit(solution)/shard_map/pkq,qb->pkb/dot_general | solution.py:16
  174.2 3.9 %fusion.68 = f32[8,64,384]{2,1,0:T(8,128)S(1)} fusion(f32[8,64,384]{2,1,0:T(8,128)S(1)} %get-tuple-element.6), kind=kOutput, calls=%fused_computation.75 | convolution fusion | flops 907296768 | bytes 1572864 | tf_op jit(solution)/shard_map/pkq,qb->pkb/dot_general | solution.py:16
  178.1 3.8 %convolution_subtract_fusion = f32[8,64,384]{2,1,0:T(8,128)S(1)} fusion(f32[8,64,384]{2,1,0:T(8,128)S(1)} %fusion.76, f32[8,64,384]{2,1,0:T(8,128)S(1)} %get-tuple-element.5), kind=kOutput, calls=%fused_computation.24 | convolution fusion | flops 907493376 | bytes 2359296 | tf_op jit(solution)/shard_map/pkq,qb->pkb/dot_general | solution.py:16
  182.0 4.0 %convolution_add_fusion = f32[8,64,384]{2,1,0:T(8,128)S(1)} fusion(f32[8,64,384]{2,1,0:T(8,128)S(1)} %fusion.68, f32[8,64,384]{2,1,0:T(8,128)S(1)} %get-tuple-element.5), kind=kOutput, calls=%fused_computation.23 | convolution fusion | flops 907493376 | bytes 2359296 | tf_op jit(solution)/shard_map/pkq,qb->pkb/dot_general | solution.py:16
  186.0 0.6 fusion.62
  186.6 0.6 fusion.42
  187.2 0.7 copy.17
  188.0 5.2 %all-to-all-start.1 = ((bf16[32,8,384]{2,1,0:T(8,128)(2,1)}), bf16[32,8,384]{2,1,0:T(8,128)(2,1)S(1)}, u32[]{:S(2)}, u32[]{:S(2)}) async-start(bf16[32,8,384]{2,1,0:T(8,128)(2,1)} %copy.17), calls=%async_computation.1 | async-start | bytes 393216 | tf_op jit(solution)/shard_map/all_to_all | solution.py:147
  193.2 8.3 %all-to-all-done.1 = bf16[32,8,384]{2,1,0:T(8,128)(2,1)S(1)} async-done(((bf16[32,8,384]{2,1,0:T(8,128)(2,1)}), bf16[32,8,384]{2,1,0:T(8,128)(2,1)S(1)}, u32[]{:S(2)}, u32[]{:S(2)}) %all-to-all-start.1) | async-done | bytes 196640 | tf_op jit(solution)/shard_map/all_to_all | solution.py:147
  201.5 1.9 collective-permute-start.7
  203.5 4.5 %collective-permute-start.8 = (bf16[256,384]{1,0:T(8,128)(2,1)S(1)}, bf16[256,384]{1,0:T(8,128)(2,1)S(1)}, u32[]{:S(2)}, u32[]{:S(2)}) collective-permute-start(bf16[256,384]{1,0:T(8,128)(2,1)S(1)} %fusion.105), channel_id=1, source_target_pairs={{0,4},{2,6},{4,0},{6,2},{1,5},{3,7},{5,1},{7,3},{8,12},{10,14},{12... | collective-permute-start | bytes 589832 | tf_op jit(solution)/shard_map/ppermute | solution.py:66
  208.0 1.2 collective-permute-start.9
  209.1 1.8 fusion.51
  211.0 4.1 %collective-permute-done.7 = bf16[256,384]{1,0:T(8,128)(2,1)S(1)} collective-permute-done((bf16[256,384]{1,0:T(8,128)(2,1)S(1)}, bf16[256,384]{1,0:T(8,128)(2,1)S(1)}, u32[]{:S(2)}, u32[]{:S(2)}) %collective-permute-start.7) | collective-permute-done | bytes 196640 | tf_op jit(solution)/shard_map/ppermute | solution.py:66
  215.0 0.6 fusion.49
  215.6 10.0 %collective-permute-done.8 = bf16[256,384]{1,0:T(8,128)(2,1)S(1)} collective-permute-done((bf16[256,384]{1,0:T(8,128)(2,1)S(1)}, bf16[256,384]{1,0:T(8,128)(2,1)S(1)}, u32[]{:S(2)}, u32[]{:S(2)}) %collective-permute-start.8) | collective-permute-done | bytes 196640 | tf_op jit(solution)/shard_map/ppermute | solution.py:66
  225.6 0.6 fusion.47
  226.2 1.8 add_convert_fusion
  (25 shorter events, 0.1 us)
Async XLA Ops:
  6.5 81.7 %all-gather.2.cloned.1.call-start = ((), (), s32[]{:S(2)}) async-start(), calls=%async_computation.2 | async-start | bytes 12976128 | tf_op jit(solution)/shard_map/all_gather | solution.py:100
  7.3 13.4 %copy-start.6 = (f32[16,256]{1,0:T(8,128)S(1)}, f32[16,256]{1,0:T(8,128)}, u32[]{:S(2)}) copy-start(f32[16,256]{1,0:T(8,128)} %param.11) | copy-start | bytes 49156
  7.3 13.4 %copy-start.7 = (f32[16,256]{1,0:T(8,128)S(1)}, f32[16,256]{1,0:T(8,128)}, u32[]{:S(2)}) copy-start(f32[16,256]{1,0:T(8,128)} %param.10) | copy-start | bytes 49156
  9.9 50.0 %collective-permute-start.1 = (bf16[384,1024]{1,0:T(8,128)(2,1)}, bf16[384,1024]{1,0:T(8,128)(2,1)}, u32[]{:S(2)}, u32[]{:S(2)}) collective-permute-start(bf16[384,1024]{1,0:T(8,128)(2,1)} %get-tuple-element.8), channel_id=1, source_target_pairs={{0,6},{2,0},{4,2},{6,4},{1,7},{3,1},{5,3},{7,5},{8,14},{10,8},{12,... | collective-permute-start | bytes 2359304 | tf_op jit(solution)/shard_map/ppermute | solution.py:66
  16.8 74.3 %collective-permute-start.2 = (bf16[384,1024]{1,0:T(8,128)(2,1)}, bf16[384,1024]{1,0:T(8,128)(2,1)}, u32[]{:S(2)}, u32[]{:S(2)}) collective-permute-start(bf16[384,1024]{1,0:T(8,128)(2,1)} %get-tuple-element.8), channel_id=1, source_target_pairs={{0,2},{2,4},{4,6},{6,0},{1,3},{3,5},{5,7},{7,1},{8,10},{10,12},{12... | collective-permute-start | bytes 2359304 | tf_op jit(solution)/shard_map/ppermute | solution.py:66
  16.8 82.2 %collective-permute-start.3 = (bf16[384,1024]{1,0:T(8,128)(2,1)}, bf16[384,1024]{1,0:T(8,128)(2,1)}, u32[]{:S(2)}, u32[]{:S(2)}) collective-permute-start(bf16[384,1024]{1,0:T(8,128)(2,1)} %get-tuple-element.7), channel_id=1, source_target_pairs={{0,6},{2,0},{4,2},{6,4},{1,7},{3,1},{5,3},{7,5},{8,14},{10,8},{12,... | collective-permute-start | bytes 2359304 | tf_op jit(solution)/shard_map/ppermute | solution.py:66
  20.3 45.4 %collective-permute-start = (bf16[384,1024]{1,0:T(8,128)(2,1)}, bf16[384,1024]{1,0:T(8,128)(2,1)}, u32[]{:S(2)}, u32[]{:S(2)}) collective-permute-start(bf16[384,1024]{1,0:T(8,128)(2,1)} %get-tuple-element.7), channel_id=1, source_target_pairs={{0,2},{2,4},{4,6},{6,0},{1,3},{3,5},{5,7},{7,1},{8,10},{10,12},{12... | collective-permute-start | bytes 2359304 | tf_op jit(solution)/shard_map/ppermute | solution.py:66
  59.9 55.8 %collective-permute-start.5 = (bf16[384,1024]{1,0:T(8,128)(2,1)}, bf16[384,1024]{1,0:T(8,128)(2,1)}, u32[]{:S(2)}, u32[]{:S(2)}) collective-permute-start(bf16[384,1024]{1,0:T(8,128)(2,1)} %collective-permute-done.1), channel_id=1, source_target_pairs={{0,6},{2,0},{4,2},{6,4},{1,7},{3,1},{5,3},{7,5},{8,14},{10,8},{12,... | collective-permute-start | bytes 2359304 | tf_op jit(solution)/shard_map/ppermute | solution.py:66
  65.8 56.7 %collective-permute-start.4 = (bf16[384,1024]{1,0:T(8,128)(2,1)}, bf16[384,1024]{1,0:T(8,128)(2,1)}, u32[]{:S(2)}, u32[]{:S(2)}) collective-permute-start(bf16[384,1024]{1,0:T(8,128)(2,1)} %collective-permute-done), channel_id=1, source_target_pairs={{0,2},{2,4},{4,6},{6,0},{1,3},{3,5},{5,7},{7,1},{8,10},{10,12},{12... | collective-permute-start | bytes 2359304 | tf_op jit(solution)/shard_map/ppermute | solution.py:66
  88.3 30.1 %copy-start.4 = (bf16[256,3,8192]{2,0,1:T(8,128)(2,1)S(1)}, bf16[256,3,8192]{2,0,1:T(8,128)(2,1)}, u32[]{:S(2)}) copy-start(bf16[256,3,8192]{2,0,1:T(8,128)(2,1)} %all-gather.2.cloned.1.call-done) | copy-start | bytes 37748740
  101.5 16.8 %copy-start.3 = (bf16[384,2048]{1,0:T(8,128)(2,1)S(1)}, bf16[384,2048]{1,0:T(8,128)(2,1)}, u32[]{:S(2)}) copy-start(bf16[384,2048]{1,0:T(8,128)(2,1)} %param.7) | copy-start | bytes 4718596
  122.4 8.8 %copy-start.5 = (f32[3,3,256]{2,1,0:T(4,128)S(1)}, f32[3,3,256]{2,1,0:T(4,128)}, u32[]{:S(2)}) copy-start(f32[3,3,256]{2,1,0:T(4,128)} %param.9) | copy-start | bytes 27652
  122.4 8.9 %copy-start.8 = (f32[256]{0:T(256)S(1)}, f32[256]{0:T(256)}, u32[]{:S(2)}) copy-start(f32[256]{0:T(256)} %param.12) | copy-start | bytes 3076
  124.7 9.1 %collective-permute-start.6 = (bf16[256,3,2]{2,0,1:T(8,128)(2,1)S(1)}, bf16[256,3,2]{2,0,1:T(8,128)(2,1)S(1)}, u32[]{:S(2)}, u32[]{:S(2)}) collective-permute-start(bf16[256,3,2]{2,0,1:T(8,128)(2,1)S(1)} %slice.201), channel_id=1, source_target_pairs={{0,8},{8,16},{16,24},{24,32},{32,40},{40,48},{48,56},{56,64},{64,7... | collective-permute-start | bytes 9224 | tf_op jit(solution)/shard_map/ppermute | solution.py:12
  136.2 16.7 %all-to-all-start = ((bf16[32,8,384]{2,1,0:T(8,128)(2,1)}), bf16[32,8,384]{2,1,0:T(8,128)(2,1)S(1)}, u32[]{:S(2)}, u32[]{:S(2)}) async-start(bf16[32,8,384]{2,1,0:T(8,128)(2,1)} %fusion.146), calls=%async_computation | async-start | bytes 393216 | tf_op jit(solution)/shard_map/all_to_all | solution.py:125
  162.0 3.9 %copy-start.1 = (f32[8,64,384]{2,1,0:T(8,128)S(1)}, f32[8,64,384]{2,1,0:T(8,128)}, u32[]{:S(2)}) copy-start(f32[8,64,384]{2,1,0:T(8,128)} %convolution_add_fusion.1) | copy-start | bytes 2359300
  162.0 3.9 %copy-start.2 = (f32[8,64,384]{2,1,0:T(8,128)S(1)}, f32[8,64,384]{2,1,0:T(8,128)}, u32[]{:S(2)}) copy-start(f32[8,64,384]{2,1,0:T(8,128)} %convolution_subtract_fusion.1) | copy-start | bytes 2359300
  188.0 13.5 %all-to-all-start.1 = ((bf16[32,8,384]{2,1,0:T(8,128)(2,1)}), bf16[32,8,384]{2,1,0:T(8,128)(2,1)S(1)}, u32[]{:S(2)}, u32[]{:S(2)}) async-start(bf16[32,8,384]{2,1,0:T(8,128)(2,1)} %copy.17), calls=%async_computation.1 | async-start | bytes 393216 | tf_op jit(solution)/shard_map/all_to_all | solution.py:147
  201.5 13.5 %copy-start = (bf16[1024,2048]{1,0:T(8,128)(2,1)S(1)}, bf16[1024,2048]{1,0:T(8,128)(2,1)}, u32[]{:S(2)}) copy-start(bf16[1024,2048]{1,0:T(8,128)(2,1)} %param.13) | copy-start | bytes 12582916
  201.5 13.5 %collective-permute-start.7 = (bf16[256,384]{1,0:T(8,128)(2,1)S(1)}, bf16[256,384]{1,0:T(8,128)(2,1)S(1)}, u32[]{:S(2)}, u32[]{:S(2)}) collective-permute-start(bf16[256,384]{1,0:T(8,128)(2,1)S(1)} %fusion.105), channel_id=1, source_target_pairs={{0,2},{2,4},{4,6},{6,0},{1,3},{3,5},{5,7},{7,1},{8,10},{10,12},{12... | collective-permute-start | bytes 589832 | tf_op jit(solution)/shard_map/ppermute | solution.py:66
  203.5 22.1 %collective-permute-start.8 = (bf16[256,384]{1,0:T(8,128)(2,1)S(1)}, bf16[256,384]{1,0:T(8,128)(2,1)S(1)}, u32[]{:S(2)}, u32[]{:S(2)}) collective-permute-start(bf16[256,384]{1,0:T(8,128)(2,1)S(1)} %fusion.105), channel_id=1, source_target_pairs={{0,4},{2,6},{4,0},{6,2},{1,5},{3,7},{5,1},{7,3},{8,12},{10,14},{12... | collective-permute-start | bytes 589832 | tf_op jit(solution)/shard_map/ppermute | solution.py:66
  208.0 18.3 %collective-permute-start.9 = (bf16[256,384]{1,0:T(8,128)(2,1)S(1)}, bf16[256,384]{1,0:T(8,128)(2,1)S(1)}, u32[]{:S(2)}, u32[]{:S(2)}) collective-permute-start(bf16[256,384]{1,0:T(8,128)(2,1)S(1)} %fusion.105), channel_id=1, source_target_pairs={{0,6},{2,0},{4,2},{6,4},{1,7},{3,1},{5,3},{7,5},{8,14},{10,8},{12,... | collective-permute-start | bytes 589832 | tf_op jit(solution)/shard_map/ppermute | solution.py:66
Sparse Core Ops, SparseCore 0:
  9.8 78.4 all-gather.1
where the time goes:
time: 239 us; the launch traced here: 235 us
  waiting for transfers between devices  89.6 us (37%)
  matrix products  80.1 us (34%)
  starting transfers between devices  44.3 us (19%)
  between operations  14.1 us (6%)
  local copies, waits for them, and re-layouts  3.64 us (2%)
  other arithmetic  3.27 us (1%)
    dot_general x18, matrix products, hidot(): jnp.einsum(form, left, right, precision=lax.Precision.HIGHEST, preferred_...  57.9 us
    ppermute x9, waiting for transfers between devices, ring_shift(): lax.ppermute(value, axis, [(source, (source + steps) % count) for source...  53.4 us
    ppermute x9, starting transfers between devices, ring_shift(): lax.ppermute(value, axis, [(source, (source + steps) % count) for source...  24.1 us
    all_gather x1, waiting for transfers between devices, on_device(): w_full = lax.all_gather(w_in, 'seq', axis=2, tiled=True)  22.5 us
    dot_general x6, matrix products, on_device(): jnp.einsum('cgd,td->cgt', block_of(step, lo, hi), piece, preferred_elemen...  15.6 us
    all_to_all x1, starting transfers between devices, on_device(): lax.all_to_all(zprod.reshape(seq_count, per_dev, tok_rows), 'seq', split_...  8.56 us
    all_to_all x1, waiting for transfers between devices, on_device(): lax.all_to_all(longc.transpose(1, 0, 2), 'seq', split_axis=0, concat_axis...  8.27 us
    ppermute x1, starting transfers between devices, from_behind(): lax.ppermute(value, axis, [(source, source + steps) for source in range(l...  6.51 us
  transfers between devices with their start and end apart: 13, of which 9 were waited for; matrix products, arithmetic and copies ran while one was open for 19% of the time, Pallas kernels for 0%

commit v1 on v0

v1 whole, which is shorter than its diff:
```python
import jax
import jax.numpy as jnp
from jax import lax
from jax.sharding import PartitionSpec as P


def from_behind(value, axis, steps):
    count = lax.axis_size(axis)
    leading, last = (max(0, -steps), min(count, count - steps))
    return lax.ppermute(value, axis, [(source, source + steps) for source in range(leading, last)])


def hidot(form, left, right):
    return jnp.einsum(
        form, left, right, precision=lax.Precision.HIGHEST, preferred_element_type=jnp.float32
    )


def ring_shift(value, axis, steps):
    count = lax.axis_size(axis)
    return lax.ppermute(value, axis, [(source, (source + steps) % count) for source in range(count)])


def chan_pieces(tokens):
    count = lax.axis_size("chan")
    width = tokens.shape[1]
    if count != 4:
        return [(step, 0, width, ring_shift(tokens, "chan", step)) for step in range(1, count)]
    half = width // 2
    ahead_lo = ring_shift(tokens[:, :half], "chan", 1)
    behind_hi = ring_shift(tokens[:, half:], "chan", -1)
    far_lo = ring_shift(ahead_lo, "chan", 1)
    far_hi = ring_shift(behind_hi, "chan", -1)
    ahead_hi = ring_shift(tokens[:, half:], "chan", 1)
    behind_lo = ring_shift(tokens[:, :half], "chan", -1)
    return [
        (1, 0, half, ahead_lo),
        (-1, half, width, behind_hi),
        (1, half, width, ahead_hi),
        (-1, 0, half, behind_lo),
        (2, 0, half, far_lo),
        (2, half, width, far_hi),
    ]


def on_device(tokens, w_in, short_taps, decay, residue, skip, w_out):
    seq_count = lax.axis_size("seq")
    seq_rank = lax.axis_index("seq")
    chan_count = lax.axis_size("chan")
    chan_rank = lax.axis_index("chan")
    tok_rows = tokens.shape[0]
    width = tokens.shape[1]
    ch_dev = w_in.shape[0]
    w_full = lax.all_gather(w_in, "seq", axis=2, tiled=True)

    def block_of(step, lo, hi):
        index = (chan_rank - step) % chan_count
        return lax.dynamic_slice_in_dim(w_full, index * width + lo, hi - lo, axis=2)

    qkv = jnp.einsum("cgd,td->cgt", block_of(0, 0, width), tokens, preferred_element_type=jnp.float32)
    for step, lo, hi, piece in chan_pieces(tokens):
        qkv = qkv + jnp.einsum(
            "cgd,td->cgt", block_of(step, lo, hi), piece, preferred_element_type=jnp.float32
        )
    qkv_b = qkv.astype(jnp.bfloat16)
    taps_n = short_taps.shape[0]
    rim_rows = qkv_b[:, :, tok_rows - (taps_n - 1) :]
    prior = from_behind(rim_rows, "seq", 1)
    extended = lax.optimization_barrier(jnp.concatenate([prior, qkv_b], axis=2)).astype(jnp.float32)
    taps = short_taps.transpose(2, 1, 0)
    feat = jnp.zeros((ch_dev, 3, tok_rows), jnp.float32)
    for j in range(taps_n):
        feat = (
            feat
            + taps[:, :, j : j + 1] * extended[:, :, taps_n - 1 - j : taps_n - 1 - j + tok_rows]
        )
    query = feat[:, 0]
    zprod = (feat[:, 1] * feat[:, 2]).astype(jnp.bfloat16)
    z_f = lax.optimization_barrier(zprod).astype(jnp.float32)
    gains = residue * jnp.sqrt(decay)
    tau = jnp.arange(tok_rows, dtype=jnp.float32)
    grow = jnp.exp(decay[:, :, None] * tau)
    fall = jnp.exp(-decay[:, :, None] * tau)
    upper = (tau[:, None] <= tau[None, :]).astype(jnp.float32)
    prefix = hidot("mcs,st->mct", grow * z_f[None], upper)
    intra = fall * prefix
    states = lax.all_gather(intra[:, :, -1], "seq", axis=0, tiled=False)
    blocks = jnp.arange(seq_count)
    lag = jnp.maximum(seq_rank - 1 - blocks, 0).astype(jnp.float32)
    carry = jnp.where(
        (blocks < seq_rank)[:, None, None],
        jnp.exp(-decay[None] * (tok_rows * lag)[:, None, None]),
        0.0,
    )
    incoming = jnp.sum(carry * states, axis=0)
    inter = jnp.exp(-decay[:, :, None] * (tau + 1.0)) * incoming[:, :, None]
    conv = jnp.einsum("mc,mct->ct", gains, intra + inter, precision=lax.Precision.HIGHEST)
    longc = (conv + skip[:, None] * z_f).astype(jnp.bfloat16)
    long_f = lax.optimization_barrier(longc).astype(jnp.float32)
    gated = (query * long_f).astype(jnp.bfloat16)
    def rows_of(step):
        index = (chan_rank - step) % chan_count
        return lax.dynamic_slice_in_dim(w_out, index * ch_dev, ch_dev, axis=0)

    shifts = [step if step <= chan_count // 2 else step - chan_count for step in range(1, chan_count)]
    arrived = [(step, ring_shift(gated, "chan", step)) for step in shifts]
    mixed = jnp.einsum("ct,ce->te", gated, rows_of(0), preferred_element_type=jnp.float32)
    for step, piece in arrived:
        mixed = mixed + jnp.einsum(
            "ct,ce->te", piece, rows_of(step), preferred_element_type=jnp.float32
        )
    return mixed.astype(jnp.bfloat16)


def solution(mesh):
    placed = (
        P(("rep", "seq"), "chan"),
        P("chan", None, "seq"),
        P(None, None, "chan"),
        P(None, "chan"),
        P(None, "chan"),
        P("chan"),
        P(None, "chan"),
    )
    return jax.shard_map(
        on_device, mesh=mesh, in_specs=placed, out_specs=P(("rep", "seq"), "chan"), check_vma=False
    )
```

time: 239 us -> 217 us (0.908); the launches traced: 235 us -> 216 us
  matrix products: 80.1 us -> 33.2 us
  blocking collectives: 0 us -> 27.9 us
  starting transfers between devices: 44.3 us -> 29.7 us
  waiting for transfers between devices: 89.6 us -> 99.1 us
  other arithmetic: 3.27 us -> 6.28 us
  local copies, waits for them, and re-layouts: 3.64 us -> 6.32 us
    dot_general x18 -> x1, matrix products: 57.9 us -> 7.19 us  [hidot(): jnp.einsum(form, left, right, precision=lax.Precision.HIGHEST, preferred_...]
    all_gather x0 -> x1, blocking collectives: none -> 27.9 us  [on_device(): states = lax.all_gather(intra[:, :, -1], 'seq', axis=0, tiled=False)]
    ppermute x9, waiting for transfers between devices: 53.4 us -> 73.1 us  [ring_shift(): lax.ppermute(value, axis, [(source, (source + steps) % count) for source...]
    all_to_all x2 -> x0, starting transfers between devices: 13.7 us -> none  [the longest x1 8.56 us: on_device(): lax.all_to_all(zprod.reshape(seq_count, per_dev, tok_rows), 'seq', split_...]
    all_to_all x2 -> x0, waiting for transfers between devices: 10.5 us -> none  [the longest x1 8.27 us: on_device(): lax.all_to_all(longc.transpose(1, 0, 2), 'seq', split_axis=0, concat_axis...]
    dot_general x0 -> x1, matrix products: none -> 7.34 us  [on_device(): jnp.einsum('mc,mct->ct', gains, intra + inter, precision=lax.Precision.HI...]
    add x0 -> x2, other arithmetic: none -> 4.2 us  [the longest x1 4.19 us: on_device(): intra + inter]
    unnamed x18 -> x19, local copies, waits for them, and re-layouts: 0.05 us -> 2.72 us
  transfers between devices with their start and end apart: 13 -> 11, of which waited for: 9 -> 8; matrix products, arithmetic and copies ran while one was open for 19% -> 8% of each run, Pallas kernels for 0% -> 0%
where the time goes in v1:
time: 217 us; the launch traced here: 216 us
  waiting for transfers between devices  99.1 us (46%)
  matrix products  33.2 us (15%)
  starting transfers between devices  29.7 us (14%)
  blocking collectives  27.9 us (13%)
  between operations  13.8 us (6%)
  local copies, waits for them, and re-layouts  6.32 us (3%)
  other arithmetic  6.28 us (3%)
    ppermute x9, waiting for transfers between devices, ring_shift(): lax.ppermute(value, axis, [(source, (source + steps) % count) for source...  73.1 us
    all_gather x1, blocking collectives, on_device(): states = lax.all_gather(intra[:, :, -1], 'seq', axis=0, tiled=False)  27.9 us
    ppermute x9, starting transfers between devices, ring_shift(): lax.ppermute(value, axis, [(source, (source + steps) % count) for source...  24.1 us
    all_gather x1, waiting for transfers between devices, on_device(): w_full = lax.all_gather(w_in, 'seq', axis=2, tiled=True)  23.7 us
    dot_general x6, matrix products, on_device(): jnp.einsum('cgd,td->cgt', block_of(step, lo, hi), piece, preferred_elemen...  13.3 us
    dot_general x1, matrix products, on_device(): jnp.einsum('mc,mct->ct', gains, intra + inter, precision=lax.Precision.HI...  7.34 us
    dot_general x1, matrix products, hidot(): jnp.einsum(form, left, right, precision=lax.Precision.HIGHEST, preferred_...  7.19 us
    ppermute x1, starting transfers between devices, from_behind(): lax.ppermute(value, axis, [(source, source + steps) for source in range(l...  5.56 us
  transfers between devices with their start and end apart: 11, of which 8 were waited for; matrix products, arithmetic and copies ran while one was open for 8% of the time, Pallas kernels for 0%

profile of v1, /device:TPU:1, one launch (start us, length us, event | category | flops | bytes accessed | tf_op | source)
XLA Modules:
  0.0 216.3 jit_solution(14029778157932556777)
XLA Ops:
  6.5 0.0 copy-start.7
  6.5 0.0 copy-start.6
  6.5 0.0 all-gather.3.cloned.1.call-start
  6.5 0.7 all-gather.3.cloned.1.call-update
  7.3 1.5 fusion.83
  8.8 6.9 %collective-permute-start.1 = (bf16[384,1024]{1,0:T(8,128)(2,1)S(1)}, bf16[384,1024]{1,0:T(8,128)(2,1)}, u32[]{:S(2)}, u32[]{:S(2)}) collective-permute-start(bf16[384,1024]{1,0:T(8,128)(2,1)S(1)} %get-tuple-element.6), channel_id=1, source_target_pairs={{0,6},{2,0},{4,2},{6,4},{1,7},{3,1},{5,3},{7,5},{8,14},{10,8},{12,... | collective-permute-start | bytes 2359304 | tf_op jit(solution)/shard_map/ppermute | solution.py:21
  15.7 0.0 collective-permute-start
  15.7 1.3 collective-permute-start.2
  16.9 2.3 %collective-permute-start.3 = (bf16[384,1024]{1,0:T(8,128)(2,1)S(1)}, bf16[384,1024]{1,0:T(8,128)(2,1)}, u32[]{:S(2)}, u32[]{:S(2)}) collective-permute-start(bf16[384,1024]{1,0:T(8,128)(2,1)S(1)} %get-tuple-element.5), channel_id=1, source_target_pairs={{0,6},{2,0},{4,2},{6,4},{1,7},{3,1},{5,3},{7,5},{8,14},{10,8},{12,... | collective-permute-start | bytes 2359304 | tf_op jit(solution)/shard_map/ppermute | solution.py:21
  19.3 0.0 copy-done.7
  19.4 0.0 copy-done.6
  19.4 0.0 copy-done.5
  19.4 39.2 %collective-permute-done.1 = bf16[384,1024]{1,0:T(8,128)(2,1)} collective-permute-done((bf16[384,1024]{1,0:T(8,128)(2,1)S(1)}, bf16[384,1024]{1,0:T(8,128)(2,1)}, u32[]{:S(2)}, u32[]{:S(2)}) %collective-permute-start.1) | collective-permute-done | bytes 786464 | tf_op jit(solution)/shard_map/ppermute | solution.py:21
  58.6 6.0 %collective-permute-start.5 = (bf16[384,1024]{1,0:T(8,128)(2,1)}, bf16[384,1024]{1,0:T(8,128)(2,1)}, u32[]{:S(2)}, u32[]{:S(2)}) collective-permute-start(bf16[384,1024]{1,0:T(8,128)(2,1)} %collective-permute-done.1), channel_id=1, source_target_pairs={{0,6},{2,0},{4,2},{6,4},{1,7},{3,1},{5,3},{7,5},{8,14},{10,8},{12,... | collective-permute-start | bytes 2359304 | tf_op jit(solution)/shard_map/ppermute | solution.py:21
  64.6 0.0 collective-permute-done
  64.6 0.0 collective-permute-start.4
  64.6 23.7 %all-gather.3.cloned.1.call-done = bf16[256,3,8192]{2,0,1:T(8,128)(2,1)} async-done(((bf16[256,3,256]{2,0,1:T(8,128)(2,1)}), bf16[256,3,8192]{2,0,1:T(8,128)(2,1)}) %all-gather.3.cloned.1.call-update) | async-done | bytes 12582928 | tf_op jit(solution)/shard_map/all_gather | solution.py:54
  88.3 2.8 %fusion.22 = f32[256,3,384]{2,0,1:T(8,128)S(1)} fusion(bf16[256,3,8192]{2,0,1:T(8,128)(2,1)} %all-gather.3.cloned.1.call-done, s32[]{:T(128)S(6)} %select_n.75, bf16[384,1024]{1,0:T(8,128)(2,1)} %collective-permute-done.1), kind=kOutput, calls=%fused_computation.23 | convolution fusion | flops 603979776 | bytes 3538948 | tf_op jit(solution)/shard_map/cgd,td->cgt/dot_general | solution.py:62
  91.1 0.0 collective-permute-done.2
  91.1 3.2 %fusion.20 = f32[256,3,384]{2,0,1:T(8,128)S(1)} fusion(bf16[256,3,8192]{2,0,1:T(8,128)(2,1)} %all-gather.3.cloned.1.call-done, s32[]{:T(128)S(6)} %select_n.76, bf16[384,1024]{1,0:T(8,128)(2,1)} %collective-permute-done.2), kind=kOutput, calls=%fused_computation.21 | convolution fusion | flops 603979776 | bytes 3538948 | tf_op jit(solution)/shard_map/cgd,td->cgt/dot_general | solution.py:62
  94.3 0.0 copy-start.2
  94.3 3.1 %collective-permute-done.3 = bf16[384,1024]{1,0:T(8,128)(2,1)} collective-permute-done((bf16[384,1024]{1,0:T(8,128)(2,1)S(1)}, bf16[384,1024]{1,0:T(8,128)(2,1)}, u32[]{:S(2)}, u32[]{:S(2)}) %collective-permute-start.3) | collective-permute-done | bytes 786464 | tf_op jit(solution)/shard_map/ppermute | solution.py:21
  97.4 2.6 %fusion.18 = f32[256,3,384]{2,0,1:T(8,128)S(1)} fusion(bf16[256,3,8192]{2,0,1:T(8,128)(2,1)} %all-gather.3.cloned.1.call-done, s32[]{:T(128)S(6)} %select_n.77, bf16[384,1024]{1,0:T(8,128)(2,1)} %collective-permute-done.3), kind=kOutput, calls=%fused_computation.19 | convolution fusion | flops 603979776 | bytes 3538948 | tf_op jit(solution)/shard_map/cgd,td->cgt/dot_general | solution.py:62
  100.0 14.3 %collective-permute-done.5 = bf16[384,1024]{1,0:T(8,128)(2,1)} collective-permute-done((bf16[384,1024]{1,0:T(8,128)(2,1)}, bf16[384,1024]{1,0:T(8,128)(2,1)}, u32[]{:S(2)}, u32[]{:S(2)}) %collective-permute-start.5) | collective-permute-done | bytes 786464 | tf_op jit(solution)/shard_map/ppermute | solution.py:21
  114.3 2.6 %fusion.14 = f32[256,3,384]{2,0,1:T(8,128)S(1)} fusion(bf16[256,3,8192]{2,0,1:T(8,128)(2,1)} %all-gather.3.cloned.1.call-done, s32[]{:T(128)S(6)} %select_n.80, bf16[384,1024]{1,0:T(8,128)(2,1)} %collective-permute-done.5), kind=kOutput, calls=%fused_computation.15 | convolution fusion | flops 603979776 | bytes 3538948 | tf_op jit(solution)/shard_map/cgd,td->cgt/dot_general | solution.py:62
  116.9 0.0 copy-done.3
  116.9 0.0 copy-done.2
  116.9 1.8 fusion.9
  118.8 1.0 fusion.41
  119.8 1.2 collective-permute-done.4
  121.0 1.0 fusion.44
  122.1 0.1 slice.55
  122.2 5.6 %collective-permute-start.6 = (bf16[256,3,2]{2,0,1:T(8,128)(2,1)S(1)}, bf16[256,3,2]{2,0,1:T(8,128)(2,1)S(1)}, u32[]{:S(2)}, u32[]{:S(2)}) collective-permute-start(bf16[256,3,2]{2,0,1:T(8,128)(2,1)S(1)} %slice.55), channel_id=1, source_target_pairs={{0,8},{8,16},{16,24},{24,32},{32,40},{40,48},{48,56},{56,64},{64,7... | collective-permute-start | bytes 9224 | tf_op jit(solution)/shard_map/ppermute | solution.py:10
  127.8 0.8 copy.9
  128.6 1.6 collective-permute-done.6
  130.2 0.4 pad_maximum_fusion
  130.6 0.2 convert_element_type.36
  130.8 1.1 fusion.47
  131.9 7.2 %exponential_multiply_fusion = f32[16,256,384]{2,1,0:T(8,128)S(1)} fusion(f32[16,256]{1,0:T(8,128)S(1)} %get-tuple-element.7, f32[256,384]{1,0:T(8,128)S(1)} %convert_element_type.39, f32[16,256]{1,0:T(8,128)S(1)} %copy-done.6), kind=kOutput, calls=%fused_computation.8 | convolution fusion | flops 7254196224 | bytes 6717440 | tf_op jit(solution)/shard_map/mcs,st->mct/dot_general | solution.py:14
  139.1 0.0 copy-start
  139.1 2.6 %copy-done = f32[16,256,384]{2,1,0:T(8,128)} copy-done((f32[16,256,384]{2,1,0:T(8,128)}, f32[16,256,384]{2,1,0:T(8,128)S(1)}, u32[]{:S(2)}) %copy-start) | copy-done | bytes 6291480
  141.8 0.6 slice.64
  142.4 0.6 copy.8
  143.0 27.9 %all-gather = f32[512,256,1]{1,2,0:T(1,128)S(1)} all-gather(f32[16,256,1]{1,2,0:T(1,128)S(1)} %copy.8), channel_id=2, replica_groups=mesh['seq'=32,'chan'=4,'rep'=2] {'seq'}, dimensions={0}, use_global_device_ids=true | all-gather | bytes 540672 | tf_op jit(solution)/shard_map/all_gather | solution.py:87
  171.0 0.2 multiply_reduce_fusion
  171.2 0.0 copy-start.4
  171.2 4.2 %multiply_add_fusion = f32[16,256,384]{2,1,0:T(8,128)S(1)} fusion(f32[16,256,384]{2,1,0:T(8,128)} %copy-done, f32[16,256]{1,0:T(8,128)S(1)} %multiply_reduce_fusion, f32[384]{0:T(512)S(1)} %iota_add_fusion, f32[16,256]{1,0:T(8,128)S(1)} %get-tuple-element.7), kind=kLoop, calls=%fused_computation.2 | loop fusion | flops 4718592 | bytes 12617216 | tf_op jit(solution)/shard_map/add | solution.py:97
  175.4 0.0 copy-done.4
  175.4 0.0 copy-start.8
  175.4 0.0 copy-start.1
  175.4 7.3 %fusion = f32[256,1,384]{2,1,0:T(1,128)S(1)} fusion(f32[16,256,1]{0,2,1:T(1,128)S(1)} %copy-done.4, f32[16,256,384]{2,1,0:T(8,128)S(1)} %multiply_add_fusion), kind=kOutput, calls=%fused_computation | convolution fusion | flops 18874368 | bytes 6701056 | tf_op jit(solution)/shard_map/mc,mct->ct/dot_general | solution.py:97
  182.8 0.0 copy-done.8
  182.8 0.1 fusion.70
  182.9 2.0 collective-permute-start.7
  184.9 4.5 %collective-permute-start.8 = (bf16[256,384]{1,0:T(8,128)(2,1)S(1)}, bf16[256,384]{1,0:T(8,128)(2,1)S(1)}, u32[]{:S(2)}, u32[]{:S(2)}) collective-permute-start(bf16[256,384]{1,0:T(8,128)(2,1)S(1)} %fusion.69), channel_id=1, source_target_pairs={{0,4},{2,6},{4,0},{6,2},{1,5},{3,7},{5,1},{7,3},{8,12},{10,14},{12... | collective-permute-start | bytes 589832 | tf_op jit(solution)/shard_map/ppermute | solution.py:21
  189.4 1.2 collective-permute-start.9
  190.6 0.0 copy-done.1
  190.6 0.6 fusion.57
  191.2 4.4 %collective-permute-done.7 = bf16[256,384]{1,0:T(8,128)(2,1)S(1)} collective-permute-done((bf16[256,384]{1,0:T(8,128)(2,1)S(1)}, bf16[256,384]{1,0:T(8,128)(2,1)S(1)}, u32[]{:S(2)}, u32[]{:S(2)}) %collective-permute-start.7) | collective-permute-done | bytes 196640 | tf_op jit(solution)/shard_map/ppermute | solution.py:21
  195.6 0.6 fusion.55
  196.1 10.9 %collective-permute-done.8 = bf16[256,384]{1,0:T(8,128)(2,1)S(1)} collective-permute-done((bf16[256,384]{1,0:T(8,128)(2,1)S(1)}, bf16[256,384]{1,0:T(8,128)(2,1)S(1)}, u32[]{:S(2)}, u32[]{:S(2)}) %collective-permute-start.8) | collective-permute-done | bytes 196640 | tf_op jit(solution)/shard_map/ppermute | solution.py:21
  207.1 0.6 fusion.53
  207.7 0.0 collective-permute-done.9
  207.7 1.8 add_convert_fusion
  (11 shorter events, 0.2 us)
Async XLA Ops:
  6.5 12.7 %copy-start.7 = (f32[3,3,256]{2,1,0:T(4,128)S(1)}, f32[3,3,256]{2,1,0:T(4,128)}, u32[]{:S(2)}) copy-start(f32[3,3,256]{2,1,0:T(4,128)} %param.9) | copy-start | bytes 27652
  6.5 12.9 %copy-start.6 = (f32[16,256]{1,0:T(8,128)S(1)}, f32[16,256]{1,0:T(8,128)}, u32[]{:S(2)}) copy-start(f32[16,256]{1,0:T(8,128)} %param.10) | copy-start | bytes 49156
  6.5 12.9 %copy-start.5 = (f32[16,256]{1,0:T(8,128)S(1)}, f32[16,256]{1,0:T(8,128)}, u32[]{:S(2)}) copy-start(f32[16,256]{1,0:T(8,128)} %param.11) | copy-start | bytes 49156
  6.5 81.8 %all-gather.3.cloned.1.call-start = ((), (), s32[]{:S(2)}) async-start(), calls=%async_computation | async-start | bytes 12976128 | tf_op jit(solution)/shard_map/all_gather | solution.py:54
  8.8 49.8 %collective-permute-start.1 = (bf16[384,1024]{1,0:T(8,128)(2,1)S(1)}, bf16[384,1024]{1,0:T(8,128)(2,1)}, u32[]{:S(2)}, u32[]{:S(2)}) collective-permute-start(bf16[384,1024]{1,0:T(8,128)(2,1)S(1)} %get-tuple-element.6), channel_id=1, source_target_pairs={{0,6},{2,0},{4,2},{6,4},{1,7},{3,1},{5,3},{7,5},{8,14},{10,8},{12,... | collective-permute-start | bytes 2359304 | tf_op jit(solution)/shard_map/ppermute | solution.py:21
  15.7 48.9 %collective-permute-start = (bf16[384,1024]{1,0:T(8,128)(2,1)S(1)}, bf16[384,1024]{1,0:T(8,128)(2,1)S(1)}, u32[]{:S(2)}, u32[]{:S(2)}) collective-permute-start(bf16[384,1024]{1,0:T(8,128)(2,1)S(1)} %get-tuple-element.5), channel_id=1, source_target_pairs={{0,2},{2,4},{4,6},{6,0},{1,3},{3,5},{5,7},{7,1},{8,10},{10,12},{12... | collective-permute-start | bytes 2359304 | tf_op jit(solution)/shard_map/ppermute | solution.py:21
  15.7 75.4 %collective-permute-start.2 = (bf16[384,1024]{1,0:T(8,128)(2,1)S(1)}, bf16[384,1024]{1,0:T(8,128)(2,1)}, u32[]{:S(2)}, u32[]{:S(2)}) collective-permute-start(bf16[384,1024]{1,0:T(8,128)(2,1)S(1)} %get-tuple-element.6), channel_id=1, source_target_pairs={{0,2},{2,4},{4,6},{6,0},{1,3},{3,5},{5,7},{7,1},{8,10},{10,12},{12... | collective-permute-start | bytes 2359304 | tf_op jit(solution)/shard_map/ppermute | solution.py:21
  16.9 80.5 %collective-permute-start.3 = (bf16[384,1024]{1,0:T(8,128)(2,1)S(1)}, bf16[384,1024]{1,0:T(8,128)(2,1)}, u32[]{:S(2)}, u32[]{:S(2)}) collective-permute-start(bf16[384,1024]{1,0:T(8,128)(2,1)S(1)} %get-tuple-element.5), channel_id=1, source_target_pairs={{0,6},{2,0},{4,2},{6,4},{1,7},{3,1},{5,3},{7,5},{8,14},{10,8},{12,... | collective-permute-start | bytes 2359304 | tf_op jit(solution)/shard_map/ppermute | solution.py:21
  58.6 55.7 %collective-permute-start.5 = (bf16[384,1024]{1,0:T(8,128)(2,1)}, bf16[384,1024]{1,0:T(8,128)(2,1)}, u32[]{:S(2)}, u32[]{:S(2)}) collective-permute-start(bf16[384,1024]{1,0:T(8,128)(2,1)} %collective-permute-done.1), channel_id=1, source_target_pairs={{0,6},{2,0},{4,2},{6,4},{1,7},{3,1},{5,3},{7,5},{8,14},{10,8},{12,... | collective-permute-start | bytes 2359304 | tf_op jit(solution)/shard_map/ppermute | solution.py:21
  64.6 56.5 %collective-permute-start.4 = (bf16[384,1024]{1,0:T(8,128)(2,1)S(1)}, bf16[384,1024]{1,0:T(8,128)(2,1)S(1)}, u32[]{:S(2)}, u32[]{:S(2)}) collective-permute-start(bf16[384,1024]{1,0:T(8,128)(2,1)S(1)} %collective-permute-done), channel_id=1, source_target_pairs={{0,2},{2,4},{4,6},{6,0},{1,3},{3,5},{5,7},{7,1},{8,10},{10,12},{12... | collective-permute-start | bytes 2359304 | tf_op jit(solution)/shard_map/ppermute | solution.py:21
  88.3 28.6 %copy-start.3 = (bf16[256,3,8192]{2,0,1:T(8,128)(2,1)S(1)}, bf16[256,3,8192]{2,0,1:T(8,128)(2,1)}, u32[]{:S(2)}) copy-start(bf16[256,3,8192]{2,0,1:T(8,128)(2,1)} %all-gather.3.cloned.1.call-done) | copy-start | bytes 37748740
  94.3 22.6 %copy-start.2 = (bf16[384,2048]{1,0:T(8,128)(2,1)S(1)}, bf16[384,2048]{1,0:T(8,128)(2,1)}, u32[]{:S(2)}) copy-start(bf16[384,2048]{1,0:T(8,128)(2,1)} %param.7) | copy-start | bytes 4718596
  122.2 8.0 %collective-permute-start.6 = (bf16[256,3,2]{2,0,1:T(8,128)(2,1)S(1)}, bf16[256,3,2]{2,0,1:T(8,128)(2,1)S(1)}, u32[]{:S(2)}, u32[]{:S(2)}) collective-permute-start(bf16[256,3,2]{2,0,1:T(8,128)(2,1)S(1)} %slice.55), channel_id=1, source_target_pairs={{0,8},{8,16},{16,24},{24,32},{32,40},{40,48},{48,56},{56,64},{64,7... | collective-permute-start | bytes 9224 | tf_op jit(solution)/shard_map/ppermute | solution.py:10
  139.1 2.7 %copy-start = (f32[16,256,384]{2,1,0:T(8,128)}, f32[16,256,384]{2,1,0:T(8,128)S(1)}, u32[]{:S(2)}) copy-start(f32[16,256,384]{2,1,0:T(8,128)S(1)} %exponential_multiply_fusion) | copy-start | bytes 18874372
  171.2 4.2 %copy-start.4 = (f32[16,256,1]{0,2,1:T(1,128)S(1)}, f32[16,256,1]{0,2,1:T(1,128)}, u32[]{:S(2)}) copy-start(f32[16,256,1]{0,2,1:T(1,128)} %copy.9) | copy-start | bytes 49156
  175.4 7.4 %copy-start.8 = (f32[256]{0:T(256)S(1)}, f32[256]{0:T(256)}, u32[]{:S(2)}) copy-start(f32[256]{0:T(256)} %param.12) | copy-start | bytes 3076
  175.4 15.1 %copy-start.1 = (bf16[1024,2048]{1,0:T(8,128)(2,1)S(1)}, bf16[1024,2048]{1,0:T(8,128)(2,1)}, u32[]{:S(2)}) copy-start(bf16[1024,2048]{1,0:T(8,128)(2,1)} %param.13) | copy-start | bytes 12582916
  182.9 12.6 %collective-permute-start.7 = (bf16[256,384]{1,0:T(8,128)(2,1)S(1)}, bf16[256,384]{1,0:T(8,128)(2,1)S(1)}, u32[]{:S(2)}, u32[]{:S(2)}) collective-permute-start(bf16[256,384]{1,0:T(8,128)(2,1)S(1)} %fusion.69), channel_id=1, source_target_pairs={{0,2},{2,4},{4,6},{6,0},{1,3},{3,5},{5,7},{7,1},{8,10},{10,12},{12... | collective-permute-start | bytes 589832 | tf_op jit(solution)/shard_map/ppermute | solution.py:21
  184.9 22.1 %collective-permute-start.8 = (bf16[256,384]{1,0:T(8,128)(2,1)S(1)}, bf16[256,384]{1,0:T(8,128)(2,1)S(1)}, u32[]{:S(2)}, u32[]{:S(2)}) collective-permute-start(bf16[256,384]{1,0:T(8,128)(2,1)S(1)} %fusion.69), channel_id=1, source_target_pairs={{0,4},{2,6},{4,0},{6,2},{1,5},{3,7},{5,1},{7,3},{8,12},{10,14},{12... | collective-permute-start | bytes 589832 | tf_op jit(solution)/shard_map/ppermute | solution.py:21
  189.4 18.3 %collective-permute-start.9 = (bf16[256,384]{1,0:T(8,128)(2,1)S(1)}, bf16[256,384]{1,0:T(8,128)(2,1)S(1)}, u32[]{:S(2)}, u32[]{:S(2)}) collective-permute-start(bf16[256,384]{1,0:T(8,128)(2,1)S(1)} %fusion.69), channel_id=1, source_target_pairs={{0,6},{2,0},{4,2},{6,4},{1,7},{3,1},{5,3},{7,5},{8,14},{10,8},{12,... | collective-permute-start | bytes 589832 | tf_op jit(solution)/shard_map/ppermute | solution.py:21
Sparse Core Ops, SparseCore 0:
  9.8 78.4 all-gather.2

commit v2 on v1

--- a/solution.py
+++ b/solution.py
@@ -82,17 +82,18 @@
     grow = jnp.exp(decay[:, :, None] * tau)
     fall = jnp.exp(-decay[:, :, None] * tau)
     upper = (tau[:, None] <= tau[None, :]).astype(jnp.float32)
-    prefix = hidot("mcs,st->mct", grow * z_f[None], upper)
-    intra = fall * prefix
-    states = lax.all_gather(intra[:, :, -1], "seq", axis=0, tiled=False)
+    tail = jnp.exp(-decay[:, :, None] * (tok_rows - 1.0 - tau))
+    ending = jnp.sum(tail * z_f[None], axis=2)
     blocks = jnp.arange(seq_count)
-    lag = jnp.maximum(seq_rank - 1 - blocks, 0).astype(jnp.float32)
+    lag = jnp.maximum(blocks - 1 - seq_rank, 0).astype(jnp.float32)
     carry = jnp.where(
-        (blocks < seq_rank)[:, None, None],
+        (blocks > seq_rank)[:, None, None],
         jnp.exp(-decay[None] * (tok_rows * lag)[:, None, None]),
         0.0,
     )
-    incoming = jnp.sum(carry * states, axis=0)
+    incoming = lax.psum_scatter(carry * ending[None], "seq", scatter_dimension=0, tiled=True)[0]
+    prefix = hidot("mcs,st->mct", grow * z_f[None], upper)
+    intra = fall * prefix
     inter = jnp.exp(-decay[:, :, None] * (tau + 1.0)) * incoming[:, :, None]
     conv = jnp.einsum("mc,mct->ct", gains, intra + inter, precision=lax.Precision.HIGHEST)
     longc = (conv + skip[:, None] * z_f).astype(jnp.bfloat16)

time: 217 us -> 269 us (1.24)
  waiting for transfers between devices: 99.1 us -> 183 us
  blocking collectives: 27.9 us -> 0 us
  local copies, waits for them, and re-layouts: 6.32 us -> 1.75 us
    reduce_scatter x0 -> x1, waiting for transfers between devices: none -> 84.1 us  [on_device(): lax.psum_scatter(carry * ending[None], 'seq', scatter_dimension=0, tiled=...]
    all_gather x1 -> x0, blocking collectives: 27.9 us -> none  [on_device(): states = lax.all_gather(intra[:, :, -1], 'seq', axis=0, tiled=False)]
    add x1 -> x0, other arithmetic: 4.19 us -> none  [on_device(): intra + inter]
    unnamed x19 -> x14, local copies, waits for them, and re-layouts: 2.72 us -> 0.03 us
  transfers between devices with their start and end apart: 11 -> 12, of which waited for: 8 -> 9; matrix products, arithmetic and copies ran while one was open for 8% -> 7% of each run, Pallas kernels for 0% -> 0%
where the time goes in v2:
time: 269 us
  waiting for transfers between devices  183 us (68%)
  matrix products  34.7 us (13%)
  starting transfers between devices  31.2 us (12%)
  between operations  13.8 us (5%)
  other arithmetic  4.75 us (2%)
    reduce_scatter x1, waiting for transfers between devices, on_device(): lax.psum_scatter(carry * ending[None], 'seq', scatter_dimension=0, tiled=...  84.1 us
    ppermute x9, waiting for transfers between devices, ring_shift(): lax.ppermute(value, axis, [(source, (source + steps) % count) for source...  71.6 us
    ppermute x9, starting transfers between devices, ring_shift(): lax.ppermute(value, axis, [(source, (source + steps) % count) for source...  25.6 us
    all_gather x1, waiting for transfers between devices, on_device(): w_full = lax.all_gather(w_in, 'seq', axis=2, tiled=True)  23.7 us
    dot_general x6, matrix products, on_device(): jnp.einsum('cgd,td->cgt', block_of(step, lo, hi), piece, preferred_elemen...  13.3 us
    dot_general x1, matrix products, hidot(): jnp.einsum(form, left, right, precision=lax.Precision.HIGHEST, preferred_...  8.47 us
    dot_general x1, matrix products, on_device(): jnp.einsum('mc,mct->ct', gains, intra + inter, precision=lax.Precision.HI...  7.56 us
    ppermute x1, starting transfers between devices, from_behind(): lax.ppermute(value, axis, [(source, source + steps) for source in range(l...  5.57 us
  transfers between devices with their start and end apart: 12, of which 9 were waited for; matrix products, arithmetic and copies ran while one was open for 7% of the time, Pallas kernels for 0%

profile of v2, /device:TPU:1, one launch (start us, length us, event | category | flops | bytes accessed | tf_op | source)
XLA Modules:
  0.0 268.8 jit_solution(18231795943514949731)
XLA Ops:
  6.5 0.0 copy-start.5
  6.5 0.0 copy-start.4
  6.5 0.0 copy-start.3
  6.5 0.0 all-gather.2.cloned.1.call-start
  6.5 0.7 all-gather.2.cloned.1.call-update
  7.3 0.0 reduce-scatter.2.cloned.1.call-start
  7.3 1.5 fusion.83
  8.8 6.9 %collective-permute-start.1 = (bf16[384,1024]{1,0:T(8,128)(2,1)S(1)}, bf16[384,1024]{1,0:T(8,128)(2,1)}, u32[]{:S(2)}, u32[]{:S(2)}) collective-permute-start(bf16[384,1024]{1,0:T(8,128)(2,1)S(1)} %get-tuple-element.6), channel_id=1, source_target_pairs={{0,6},{2,0},{4,2},{6,4},{1,7},{3,1},{5,3},{7,5},{8,14},{10,8},{12,... | collective-permute-start | bytes 2359304 | tf_op jit(solution)/shard_map/ppermute | solution.py:21
  15.7 0.0 collective-permute-start
  15.7 1.3 collective-permute-start.2
  17.0 2.3 collective-permute-start.3
  19.3 0.0 copy-done.5
  19.4 0.0 copy-done.4
  19.4 0.0 copy-done.3
  19.5 39.2 %collective-permute-done.1 = bf16[384,1024]{1,0:T(8,128)(2,1)} collective-permute-done((bf16[384,1024]{1,0:T(8,128)(2,1)S(1)}, bf16[384,1024]{1,0:T(8,128)(2,1)}, u32[]{:S(2)}, u32[]{:S(2)}) %collective-permute-start.1) | collective-permute-done | bytes 786464 | tf_op jit(solution)/shard_map/ppermute | solution.py:21
  58.6 6.0 %collective-permute-start.5 = (bf16[384,1024]{1,0:T(8,128)(2,1)}, bf16[384,1024]{1,0:T(8,128)(2,1)}, u32[]{:S(2)}, u32[]{:S(2)}) collective-permute-start(bf16[384,1024]{1,0:T(8,128)(2,1)} %collective-permute-done.1), channel_id=1, source_target_pairs={{0,6},{2,0},{4,2},{6,4},{1,7},{3,1},{5,3},{7,5},{8,14},{10,8},{12,... | collective-permute-start | bytes 2359304 | tf_op jit(solution)/shard_map/ppermute | solution.py:21
  64.6 0.0 collective-permute-done
  64.6 0.0 collective-permute-start.4
  64.6 23.7 %all-gather.2.cloned.1.call-done = bf16[256,3,8192]{2,0,1:T(8,128)(2,1)} async-done(((bf16[256,3,256]{2,0,1:T(8,128)(2,1)}), bf16[256,3,8192]{2,0,1:T(8,128)(2,1)}) %all-gather.2.cloned.1.call-update) | async-done | bytes 12582928 | tf_op jit(solution)/shard_map/all_gather | solution.py:54
  88.3 0.0 copy-start.2
  88.3 2.8 %fusion.22 = f32[256,3,384]{2,0,1:T(8,128)S(1)} fusion(bf16[256,3,8192]{2,0,1:T(8,128)(2,1)} %all-gather.2.cloned.1.call-done, s32[]{:T(128)S(6)} %select_n.75, bf16[384,1024]{1,0:T(8,128)(2,1)} %collective-permute-done.1), kind=kOutput, calls=%fused_computation.23 | convolution fusion | flops 603979776 | bytes 3538948 | tf_op jit(solution)/shard_map/cgd,td->cgt/dot_general | solution.py:62
  91.1 0.0 collective-permute-done.2
  91.1 3.2 %fusion.20 = f32[256,3,384]{2,0,1:T(8,128)S(1)} fusion(bf16[256,3,8192]{2,0,1:T(8,128)(2,1)} %all-gather.2.cloned.1.call-done, s32[]{:T(128)S(6)} %select_n.76, bf16[384,1024]{1,0:T(8,128)(2,1)} %collective-permute-done.2), kind=kOutput, calls=%fused_computation.21 | convolution fusion | flops 603979776 | bytes 3538948 | tf_op jit(solution)/shard_map/cgd,td->cgt/dot_general | solution.py:62
  94.3 0.0 copy-start.1
  94.3 3.1 %collective-permute-done.3 = bf16[384,1024]{1,0:T(8,128)(2,1)} collective-permute-done((bf16[384,1024]{1,0:T(8,128)(2,1)S(1)}, bf16[384,1024]{1,0:T(8,128)(2,1)}, u32[]{:S(2)}, u32[]{:S(2)}) %collective-permute-start.3) | collective-permute-done | bytes 786464 | tf_op jit(solution)/shard_map/ppermute | solution.py:21
  97.5 2.6 fusion.18
  100.1 14.3 %collective-permute-done.5 = bf16[384,1024]{1,0:T(8,128)(2,1)} collective-permute-done((bf16[384,1024]{1,0:T(8,128)(2,1)}, bf16[384,1024]{1,0:T(8,128)(2,1)}, u32[]{:S(2)}, u32[]{:S(2)}) %collective-permute-start.5) | collective-permute-done | bytes 786464 | tf_op jit(solution)/shard_map/ppermute | solution.py:21
  114.4 2.6 fusion.14
  117.0 0.0 copy-done.2
  117.0 0.0 copy-done.1
  117.0 1.8 fusion.9
  118.8 1.0 fusion.41
  119.8 1.2 collective-permute-done.4
  121.1 1.0 fusion.44
  122.1 0.1 slice.51
  122.2 5.6 %collective-permute-start.6 = (bf16[256,3,2]{2,0,1:T(8,128)(2,1)S(1)}, bf16[256,3,2]{2,0,1:T(8,128)(2,1)S(1)}, u32[]{:S(2)}, u32[]{:S(2)}) collective-permute-start(bf16[256,3,2]{2,0,1:T(8,128)(2,1)S(1)} %slice.51), channel_id=1, source_target_pairs={{0,8},{8,16},{16,24},{24,32},{32,40},{40,48},{48,56},{56,64},{64,7... | collective-permute-start | bytes 9224 | tf_op jit(solution)/shard_map/ppermute | solution.py:10
  127.8 2.4 collective-permute-done.6
  130.2 0.4 pad_maximum_fusion
  130.6 0.2 convert_element_type.36
  130.8 1.1 fusion.47
  132.0 1.9 multiply_reduce_fusion
  133.9 1.0 select_multiply_fusion
  134.8 0.0 reduce-scatter.2.cloned.1.call-update
  134.9 0.1 copy.8
  135.0 84.1 %reduce-scatter.2.cloned.1.call-done = f32[1,16,256]{2,1,0:T(8,128)} async-done(((f32[32,16,256]{2,1,0:T(8,128)}), f32[1,16,256]{2,1,0:T(8,128)}) %reduce-scatter.2.cloned.1.call-update) | async-done | bytes 16400 | tf_op jit(solution)/shard_map/reduce_scatter | solution.py:94
  219.1 8.5 %multiply_add_fusion = f32[16,256,384]{2,1,0:T(8,128)S(1)} fusion(f32[16,256]{1,0:T(8,128)} %bitcast.52, f32[384]{0:T(512)S(1)} %iota_add_fusion, f32[16,256]{1,0:T(8,128)S(1)} %get-tuple-element.7, f32[256,384]{1,0:T(8,128)S(1)} %convert_element_type.39, f32[16,256]{1,0:T(8,128)S(1)} %copy-done.4), kind=kOutput, calls=%fused_computation.2 | convolution fusion | flops 7258914816 | bytes 6735360 | tf_op jit(solution)/shard_map/mcs,st->mct/dot_general | solution.py:14
  227.6 0.0 copy-start.6
  227.6 0.0 copy-start
  227.6 7.6 %fusion = f32[256,1,384]{2,1,0:T(1,128)S(1)} fusion(f32[16,256,1]{0,2,1:T(1,128)S(1)} %copy.8, f32[16,256,384]{2,1,0:T(8,128)S(1)} %multiply_add_fusion), kind=kOutput, calls=%fused_computation | convolution fusion | flops 18874368 | bytes 6701056 | tf_op jit(solution)/shard_map/mc,mct->ct/dot_general | solution.py:98
  235.2 0.0 copy-done.6
  235.2 0.1 fusion.70
  235.4 2.4 collective-permute-start.7
  237.7 3.6 %collective-permute-start.8 = (bf16[256,384]{1,0:T(8,128)(2,1)S(1)}, bf16[256,384]{1,0:T(8,128)(2,1)S(1)}, u32[]{:S(2)}, u32[]{:S(2)}) collective-permute-start(bf16[256,384]{1,0:T(8,128)(2,1)S(1)} %fusion.69), channel_id=1, source_target_pairs={{0,4},{2,6},{4,0},{6,2},{1,5},{3,7},{5,1},{7,3},{8,12},{10,14},{12... | collective-permute-start | bytes 589832 | tf_op jit(solution)/shard_map/ppermute | solution.py:21
  241.4 3.1 %collective-permute-start.9 = (bf16[256,384]{1,0:T(8,128)(2,1)S(1)}, bf16[256,384]{1,0:T(8,128)(2,1)S(1)}, u32[]{:S(2)}, u32[]{:S(2)}) collective-permute-start(bf16[256,384]{1,0:T(8,128)(2,1)S(1)} %fusion.69), channel_id=1, source_target_pairs={{0,6},{2,0},{4,2},{6,4},{1,7},{3,1},{5,3},{7,5},{8,14},{10,8},{12,... | collective-permute-start | bytes 589832 | tf_op jit(solution)/shard_map/ppermute | solution.py:21
  244.5 0.0 copy-done
  244.5 0.6 fusion.57
  245.1 0.0 collective-permute-done.7
  245.1 0.6 fusion.55
  245.7 7.5 %collective-permute-done.8 = bf16[256,384]{1,0:T(8,128)(2,1)S(1)} collective-permute-done((bf16[256,384]{1,0:T(8,128)(2,1)S(1)}, bf16[256,384]{1,0:T(8,128)(2,1)S(1)}, u32[]{:S(2)}, u32[]{:S(2)}) %collective-permute-start.8) | collective-permute-done | bytes 196640 | tf_op jit(solution)/shard_map/ppermute | solution.py:21
  253.2 0.6 fusion.53
  253.8 6.3 %collective-permute-done.9 = bf16[256,384]{1,0:T(8,128)(2,1)S(1)} collective-permute-done((bf16[256,384]{1,0:T(8,128)(2,1)S(1)}, bf16[256,384]{1,0:T(8,128)(2,1)S(1)}, u32[]{:S(2)}, u32[]{:S(2)}) %collective-permute-start.9) | collective-permute-done | bytes 196640 | tf_op jit(solution)/shard_map/ppermute | solution.py:21
  260.1 1.8 add_convert_fusion
  (9 shorter events, 0.2 us)
Async XLA Ops:
  6.5 12.8 %copy-start.5 = (f32[3,3,256]{2,1,0:T(4,128)S(1)}, f32[3,3,256]{2,1,0:T(4,128)}, u32[]{:S(2)}) copy-start(f32[3,3,256]{2,1,0:T(4,128)} %param.9) | copy-start | bytes 27652
  6.5 12.9 %copy-start.4 = (f32[16,256]{1,0:T(8,128)S(1)}, f32[16,256]{1,0:T(8,128)}, u32[]{:S(2)}) copy-start(f32[16,256]{1,0:T(8,128)} %param.10) | copy-start | bytes 49156
  6.5 12.9 %copy-start.3 = (f32[16,256]{1,0:T(8,128)S(1)}, f32[16,256]{1,0:T(8,128)}, u32[]{:S(2)}) copy-start(f32[16,256]{1,0:T(8,128)} %param.11) | copy-start | bytes 49156
  6.5 81.8 %all-gather.2.cloned.1.call-start = ((), (), s32[]{:S(2)}) async-start(), calls=%async_computation.1 | async-start | bytes 12976128 | tf_op jit(solution)/shard_map/all_gather | solution.py:54
  7.3 211.9 %reduce-scatter.2.cloned.1.call-start = ((), (), s32[]{:S(2)}) async-start(), calls=%async_computation.2 | async-start | bytes 540672 | tf_op jit(solution)/shard_map/reduce_scatter | solution.py:94
  8.8 49.8 %collective-permute-start.1 = (bf16[384,1024]{1,0:T(8,128)(2,1)S(1)}, bf16[384,1024]{1,0:T(8,128)(2,1)}, u32[]{:S(2)}, u32[]{:S(2)}) collective-permute-start(bf16[384,1024]{1,0:T(8,128)(2,1)S(1)} %get-tuple-element.6), channel_id=1, source_target_pairs={{0,6},{2,0},{4,2},{6,4},{1,7},{3,1},{5,3},{7,5},{8,14},{10,8},{12,... | collective-permute-start | bytes 2359304 | tf_op jit(solution)/shard_map/ppermute | solution.py:21
  15.7 48.9 %collective-permute-start = (bf16[384,1024]{1,0:T(8,128)(2,1)S(1)}, bf16[384,1024]{1,0:T(8,128)(2,1)S(1)}, u32[]{:S(2)}, u32[]{:S(2)}) collective-permute-start(bf16[384,1024]{1,0:T(8,128)(2,1)S(1)} %get-tuple-element.5), channel_id=1, source_target_pairs={{0,2},{2,4},{4,6},{6,0},{1,3},{3,5},{5,7},{7,1},{8,10},{10,12},{12... | collective-permute-start | bytes 2359304 | tf_op jit(solution)/shard_map/ppermute | solution.py:21
  15.7 75.3 %collective-permute-start.2 = (bf16[384,1024]{1,0:T(8,128)(2,1)S(1)}, bf16[384,1024]{1,0:T(8,128)(2,1)}, u32[]{:S(2)}, u32[]{:S(2)}) collective-permute-start(bf16[384,1024]{1,0:T(8,128)(2,1)S(1)} %get-tuple-element.6), channel_id=1, source_target_pairs={{0,2},{2,4},{4,6},{6,0},{1,3},{3,5},{5,7},{7,1},{8,10},{10,12},{12... | collective-permute-start | bytes 2359304 | tf_op jit(solution)/shard_map/ppermute | solution.py:21
  17.0 80.5 %collective-permute-start.3 = (bf16[384,1024]{1,0:T(8,128)(2,1)S(1)}, bf16[384,1024]{1,0:T(8,128)(2,1)}, u32[]{:S(2)}, u32[]{:S(2)}) collective-permute-start(bf16[384,1024]{1,0:T(8,128)(2,1)S(1)} %get-tuple-element.5), channel_id=1, source_target_pairs={{0,6},{2,0},{4,2},{6,4},{1,7},{3,1},{5,3},{7,5},{8,14},{10,8},{12,... | collective-permute-start | bytes 2359304 | tf_op jit(solution)/shard_map/ppermute | solution.py:21
  58.6 55.7 %collective-permute-start.5 = (bf16[384,1024]{1,0:T(8,128)(2,1)}, bf16[384,1024]{1,0:T(8,128)(2,1)}, u32[]{:S(2)}, u32[]{:S(2)}) collective-permute-start(bf16[384,1024]{1,0:T(8,128)(2,1)} %collective-permute-done.1), channel_id=1, source_target_pairs={{0,6},{2,0},{4,2},{6,4},{1,7},{3,1},{5,3},{7,5},{8,14},{10,8},{12,... | collective-permute-start | bytes 2359304 | tf_op jit(solution)/shard_map/ppermute | solution.py:21
  64.6 56.5 %collective-permute-start.4 = (bf16[384,1024]{1,0:T(8,128)(2,1)S(1)}, bf16[384,1024]{1,0:T(8,128)(2,1)S(1)}, u32[]{:S(2)}, u32[]{:S(2)}) collective-permute-start(bf16[384,1024]{1,0:T(8,128)(2,1)S(1)} %collective-permute-done), channel_id=1, source_target_pairs={{0,2},{2,4},{4,6},{6,0},{1,3},{3,5},{5,7},{7,1},{8,10},{10,12},{12... | collective-permute-start | bytes 2359304 | tf_op jit(solution)/shard_map/ppermute | solution.py:21
  88.3 28.7 %copy-start.2 = (bf16[256,3,8192]{2,0,1:T(8,128)(2,1)S(1)}, bf16[256,3,8192]{2,0,1:T(8,128)(2,1)}, u32[]{:S(2)}) copy-start(bf16[256,3,8192]{2,0,1:T(8,128)(2,1)} %all-gather.2.cloned.1.call-done) | copy-start | bytes 37748740
  94.3 22.7 %copy-start.1 = (bf16[384,2048]{1,0:T(8,128)(2,1)S(1)}, bf16[384,2048]{1,0:T(8,128)(2,1)}, u32[]{:S(2)}) copy-start(bf16[384,2048]{1,0:T(8,128)(2,1)} %param.7) | copy-start | bytes 4718596
  122.2 8.0 %collective-permute-start.6 = (bf16[256,3,2]{2,0,1:T(8,128)(2,1)S(1)}, bf16[256,3,2]{2,0,1:T(8,128)(2,1)S(1)}, u32[]{:S(2)}, u32[]{:S(2)}) collective-permute-start(bf16[256,3,2]{2,0,1:T(8,128)(2,1)S(1)} %slice.51), channel_id=1, source_target_pairs={{0,8},{8,16},{16,24},{24,32},{32,40},{40,48},{48,56},{56,64},{64,7... | collective-permute-start | bytes 9224 | tf_op jit(solution)/shard_map/ppermute | solution.py:10
  227.6 7.6 %copy-start.6 = (f32[256]{0:T(256)S(1)}, f32[256]{0:T(256)}, u32[]{:S(2)}) copy-start(f32[256]{0:T(256)} %param.12) | copy-start | bytes 3076
  227.6 16.9 %copy-start = (bf16[1024,2048]{1,0:T(8,128)(2,1)S(1)}, bf16[1024,2048]{1,0:T(8,128)(2,1)}, u32[]{:S(2)}) copy-start(bf16[1024,2048]{1,0:T(8,128)(2,1)} %param.13) | copy-start | bytes 12582916
  235.4 9.7 %collective-permute-start.7 = (bf16[256,384]{1,0:T(8,128)(2,1)S(1)}, bf16[256,384]{1,0:T(8,128)(2,1)S(1)}, u32[]{:S(2)}, u32[]{:S(2)}) collective-permute-start(bf16[256,384]{1,0:T(8,128)(2,1)S(1)} %fusion.69), channel_id=1, source_target_pairs={{0,2},{2,4},{4,6},{6,0},{1,3},{3,5},{5,7},{7,1},{8,10},{10,12},{12... | collective-permute-start | bytes 589832 | tf_op jit(solution)/shard_map/ppermute | solution.py:21
  237.7 15.5 %collective-permute-start.8 = (bf16[256,384]{1,0:T(8,128)(2,1)S(1)}, bf16[256,384]{1,0:T(8,128)(2,1)S(1)}, u32[]{:S(2)}, u32[]{:S(2)}) collective-permute-start(bf16[256,384]{1,0:T(8,128)(2,1)S(1)} %fusion.69), channel_id=1, source_target_pairs={{0,4},{2,6},{4,0},{6,2},{1,5},{3,7},{5,1},{7,3},{8,12},{10,14},{12... | collective-permute-start | bytes 589832 | tf_op jit(solution)/shard_map/ppermute | solution.py:21
  241.4 18.8 %collective-permute-start.9 = (bf16[256,384]{1,0:T(8,128)(2,1)S(1)}, bf16[256,384]{1,0:T(8,128)(2,1)S(1)}, u32[]{:S(2)}, u32[]{:S(2)}) collective-permute-start(bf16[256,384]{1,0:T(8,128)(2,1)S(1)} %fusion.69), channel_id=1, source_target_pairs={{0,6},{2,0},{4,2},{6,4},{1,7},{3,1},{5,3},{7,5},{8,14},{10,8},{12,... | collective-permute-start | bytes 589832 | tf_op jit(solution)/shard_map/ppermute | solution.py:21
Sparse Core Ops, SparseCore 0:
  9.8 78.4 all-gather.1
  135.0 84.1 reduce-scatter.1

commit v3 on v2

--- a/solution.py
+++ b/solution.py
@@ -84,14 +84,21 @@
     upper = (tau[:, None] <= tau[None, :]).astype(jnp.float32)
     tail = jnp.exp(-decay[:, :, None] * (tok_rows - 1.0 - tau))
     ending = jnp.sum(tail * z_f[None], axis=2)
+    states = lax.all_to_all(
+        jnp.broadcast_to(ending[None], (seq_count,) + ending.shape),
+        "seq",
+        split_axis=0,
+        concat_axis=0,
+        tiled=True,
+    )
     blocks = jnp.arange(seq_count)
-    lag = jnp.maximum(blocks - 1 - seq_rank, 0).astype(jnp.float32)
+    lag = jnp.maximum(seq_rank - 1 - blocks, 0).astype(jnp.float32)
     carry = jnp.where(
-        (blocks > seq_rank)[:, None, None],
+        (blocks < seq_rank)[:, None, None],
         jnp.exp(-decay[None] * (tok_rows * lag)[:, None, None]),
         0.0,
     )
-    incoming = lax.psum_scatter(carry * ending[None], "seq", scatter_dimension=0, tiled=True)[0]
+    incoming = jnp.sum(carry * states, axis=0)
     prefix = hidot("mcs,st->mct", grow * z_f[None], upper)
     intra = fall * prefix
     inter = jnp.exp(-decay[:, :, None] * (tau + 1.0)) * incoming[:, :, None]

time: 269 us -> 204 us (0.76)
  waiting for transfers between devices: 183 us -> 111 us
  starting transfers between devices: 31.2 us -> 38.1 us
    reduce_scatter x1 -> x0, waiting for transfers between devices: 84.1 us -> none  [on_device(): lax.psum_scatter(carry * ending[None], 'seq', scatter_dimension=0, tiled=...]
    all_to_all x0 -> x1, waiting for transfers between devices: none -> 11.4 us  [on_device(): lax.all_to_all(jnp.broadcast_to(ending[None], (seq_count,) + ending.shape...]
    all_to_all x0 -> x1, starting transfers between devices: none -> 8.39 us  [on_device(): lax.all_to_all(jnp.broadcast_to(ending[None], (seq_count,) + ending.shape...]
  transfers between devices with their start and end apart: 12 -> 12, of which waited for: 9 -> 9; matrix products, arithmetic and copies ran while one was open for 7% -> 9% of each run, Pallas kernels for 0% -> 0%
where the time goes in v3:
time: 204 us
  waiting for transfers between devices  111 us (54%)
  starting transfers between devices  38.1 us (19%)
  matrix products  33.9 us (17%)
  between operations  13.7 us (7%)
  other arithmetic  3.97 us (2%)
  local copies, waits for them, and re-layouts  2.6 us (1%)
    ppermute x9, waiting for transfers between devices, ring_shift(): lax.ppermute(value, axis, [(source, (source + steps) % count) for source...  73.2 us
    ppermute x9, starting transfers between devices, ring_shift(): lax.ppermute(value, axis, [(source, (source + steps) % count) for source...  24.1 us
    all_gather x1, waiting for transfers between devices, on_device(): w_full = lax.all_gather(w_in, 'seq', axis=2, tiled=True)  23.7 us
    dot_general x6, matrix products, on_device(): jnp.einsum('cgd,td->cgt', block_of(step, lo, hi), piece, preferred_elemen...  13.3 us
    all_to_all x1, waiting for transfers between devices, on_device(): lax.all_to_all(jnp.broadcast_to(ending[None], (seq_count,) + ending.shape...  11.4 us
    all_to_all x1, starting transfers between devices, on_device(): lax.all_to_all(jnp.broadcast_to(ending[None], (seq_count,) + ending.shape...  8.39 us
    dot_general x1, matrix products, hidot(): jnp.einsum(form, left, right, precision=lax.Precision.HIGHEST, preferred_...  7.69 us
    dot_general x1, matrix products, on_device(): jnp.einsum('mc,mct->ct', gains, intra + inter, precision=lax.Precision.HI...  7.56 us
  transfers between devices with their start and end apart: 12, of which 9 were waited for; matrix products, arithmetic and copies ran while one was open for 9% of the time, Pallas kernels for 0%

profile of v3, /device:TPU:1, one launch (start us, length us, event | category | flops | bytes accessed | tf_op | source)
XLA Modules:
  0.0 203.7 jit_solution(2657957993000396943)
XLA Ops:
  6.5 0.0 copy-start.5
  6.5 0.0 copy-start.4
  6.5 0.0 copy-start.3
  6.5 0.0 all-gather.2.cloned.1.call-start
  6.5 0.7 all-gather.2.cloned.1.call-update
  7.3 1.5 fusion.83
  8.8 6.9 %collective-permute-start.1 = (bf16[384,1024]{1,0:T(8,128)(2,1)S(1)}, bf16[384,1024]{1,0:T(8,128)(2,1)}, u32[]{:S(2)}, u32[]{:S(2)}) collective-permute-start(bf16[384,1024]{1,0:T(8,128)(2,1)S(1)} %get-tuple-element.6), channel_id=1, source_target_pairs={{0,6},{2,0},{4,2},{6,4},{1,7},{3,1},{5,3},{7,5},{8,14},{10,8},{12,... | collective-permute-start | bytes 2359304 | tf_op jit(solution)/shard_map/ppermute | solution.py:21
  15.7 0.0 collective-permute-start
  15.7 1.3 collective-permute-start.2
  16.9 2.3 %collective-permute-start.3 = (bf16[384,1024]{1,0:T(8,128)(2,1)S(1)}, bf16[384,1024]{1,0:T(8,128)(2,1)}, u32[]{:S(2)}, u32[]{:S(2)}) collective-permute-start(bf16[384,1024]{1,0:T(8,128)(2,1)S(1)} %get-tuple-element.5), channel_id=1, source_target_pairs={{0,6},{2,0},{4,2},{6,4},{1,7},{3,1},{5,3},{7,5},{8,14},{10,8},{12,... | collective-permute-start | bytes 2359304 | tf_op jit(solution)/shard_map/ppermute | solution.py:21
  19.3 0.0 copy-done.5
  19.3 0.0 copy-done.4
  19.3 0.0 copy-done.3
  19.3 39.3 %collective-permute-done.1 = bf16[384,1024]{1,0:T(8,128)(2,1)} collective-permute-done((bf16[384,1024]{1,0:T(8,128)(2,1)S(1)}, bf16[384,1024]{1,0:T(8,128)(2,1)}, u32[]{:S(2)}, u32[]{:S(2)}) %collective-permute-start.1) | collective-permute-done | bytes 786464 | tf_op jit(solution)/shard_map/ppermute | solution.py:21
  58.6 6.0 %collective-permute-start.5 = (bf16[384,1024]{1,0:T(8,128)(2,1)}, bf16[384,1024]{1,0:T(8,128)(2,1)}, u32[]{:S(2)}, u32[]{:S(2)}) collective-permute-start(bf16[384,1024]{1,0:T(8,128)(2,1)} %collective-permute-done.1), channel_id=1, source_target_pairs={{0,6},{2,0},{4,2},{6,4},{1,7},{3,1},{5,3},{7,5},{8,14},{10,8},{12,... | collective-permute-start | bytes 2359304 | tf_op jit(solution)/shard_map/ppermute | solution.py:21
  64.6 0.0 collective-permute-done
  64.6 0.0 collective-permute-start.4
  64.6 23.7 %all-gather.2.cloned.1.call-done = bf16[256,3,8192]{2,0,1:T(8,128)(2,1)} async-done(((bf16[256,3,256]{2,0,1:T(8,128)(2,1)}), bf16[256,3,8192]{2,0,1:T(8,128)(2,1)}) %all-gather.2.cloned.1.call-update) | async-done | bytes 12582928 | tf_op jit(solution)/shard_map/all_gather | solution.py:54
  88.3 0.0 copy-start.2
  88.3 2.8 %fusion.22 = f32[256,3,384]{2,0,1:T(8,128)S(1)} fusion(bf16[256,3,8192]{2,0,1:T(8,128)(2,1)} %all-gather.2.cloned.1.call-done, s32[]{:T(128)S(6)} %select_n.75, bf16[384,1024]{1,0:T(8,128)(2,1)} %collective-permute-done.1), kind=kOutput, calls=%fused_computation.23 | convolution fusion | flops 603979776 | bytes 3538948 | tf_op jit(solution)/shard_map/cgd,td->cgt/dot_general | solution.py:62
  91.1 0.0 collective-permute-done.2
  91.1 3.2 %fusion.20 = f32[256,3,384]{2,0,1:T(8,128)S(1)} fusion(bf16[256,3,8192]{2,0,1:T(8,128)(2,1)} %all-gather.2.cloned.1.call-done, s32[]{:T(128)S(6)} %select_n.76, bf16[384,1024]{1,0:T(8,128)(2,1)} %collective-permute-done.2), kind=kOutput, calls=%fused_computation.21 | convolution fusion | flops 603979776 | bytes 3538948 | tf_op jit(solution)/shard_map/cgd,td->cgt/dot_general | solution.py:62
  94.3 0.0 copy-start.1
  94.3 3.1 %collective-permute-done.3 = bf16[384,1024]{1,0:T(8,128)(2,1)} collective-permute-done((bf16[384,1024]{1,0:T(8,128)(2,1)S(1)}, bf16[384,1024]{1,0:T(8,128)(2,1)}, u32[]{:S(2)}, u32[]{:S(2)}) %collective-permute-start.3) | collective-permute-done | bytes 786464 | tf_op jit(solution)/shard_map/ppermute | solution.py:21
  97.4 2.6 %fusion.18 = f32[256,3,384]{2,0,1:T(8,128)S(1)} fusion(bf16[256,3,8192]{2,0,1:T(8,128)(2,1)} %all-gather.2.cloned.1.call-done, s32[]{:T(128)S(6)} %select_n.77, bf16[384,1024]{1,0:T(8,128)(2,1)} %collective-permute-done.3), kind=kOutput, calls=%fused_computation.19 | convolution fusion | flops 603979776 | bytes 3538948 | tf_op jit(solution)/shard_map/cgd,td->cgt/dot_general | solution.py:62
  100.0 14.3 %collective-permute-done.5 = bf16[384,1024]{1,0:T(8,128)(2,1)} collective-permute-done((bf16[384,1024]{1,0:T(8,128)(2,1)}, bf16[384,1024]{1,0:T(8,128)(2,1)}, u32[]{:S(2)}, u32[]{:S(2)}) %collective-permute-start.5) | collective-permute-done | bytes 786464 | tf_op jit(solution)/shard_map/ppermute | solution.py:21
  114.3 2.6 %fusion.14 = f32[256,3,384]{2,0,1:T(8,128)S(1)} fusion(bf16[256,3,8192]{2,0,1:T(8,128)(2,1)} %all-gather.2.cloned.1.call-done, s32[]{:T(128)S(6)} %select_n.80, bf16[384,1024]{1,0:T(8,128)(2,1)} %collective-permute-done.5), kind=kOutput, calls=%fused_computation.15 | convolution fusion | flops 603979776 | bytes 3538948 | tf_op jit(solution)/shard_map/cgd,td->cgt/dot_general | solution.py:62
  116.9 0.0 copy-done.2
  116.9 0.0 copy-done.1
  116.9 1.8 fusion.9
  118.8 1.0 fusion.41
  119.8 1.2 collective-permute-done.4
  121.0 1.0 fusion.44
  122.1 0.1 slice.51
  122.2 5.6 %collective-permute-start.6 = (bf16[256,3,2]{2,0,1:T(8,128)(2,1)S(1)}, bf16[256,3,2]{2,0,1:T(8,128)(2,1)S(1)}, u32[]{:S(2)}, u32[]{:S(2)}) collective-permute-start(bf16[256,3,2]{2,0,1:T(8,128)(2,1)S(1)} %slice.51), channel_id=1, source_target_pairs={{0,8},{8,16},{16,24},{24,32},{32,40},{40,48},{48,56},{56,64},{64,7... | collective-permute-start | bytes 9224 | tf_op jit(solution)/shard_map/ppermute | solution.py:10
  127.8 2.4 %collective-permute-done.6 = bf16[256,3,2]{2,0,1:T(8,128)(2,1)S(1)} collective-permute-done((bf16[256,3,2]{2,0,1:T(8,128)(2,1)S(1)}, bf16[256,3,2]{2,0,1:T(8,128)(2,1)S(1)}, u32[]{:S(2)}, u32[]{:S(2)}) %collective-permute-start.6) | collective-permute-done | bytes 3104 | tf_op jit(solution)/shard_map/ppermute | solution.py:10
  130.2 0.4 pad_maximum_fusion
  130.6 0.2 convert_element_type.36
  130.8 1.1 fusion.47
  131.9 1.9 multiply_reduce_fusion
  133.8 0.9 broadcast_in_dim.12
  134.7 8.4 %all-to-all-start = ((f32[32,16,256]{2,1,0:T(8,128)}), f32[32,16,256]{2,1,0:T(8,128)S(1)}, u32[]{:S(2)}, u32[]{:S(2)}) async-start(f32[32,16,256]{2,1,0:T(8,128)} %broadcast_in_dim.12), calls=%async_computation | async-start | bytes 1048576 | tf_op jit(solution)/shard_map/all_to_all | solution.py:87
  143.1 0.1 copy.8
  143.3 11.4 %all-to-all-done = f32[32,16,256]{2,1,0:T(8,128)S(1)} async-done(((f32[32,16,256]{2,1,0:T(8,128)}), f32[32,16,256]{2,1,0:T(8,128)S(1)}, u32[]{:S(2)}, u32[]{:S(2)}) %all-to-all-start) | async-done | bytes 524320 | tf_op jit(solution)/shard_map/all_to_all | solution.py:87
  154.7 0.2 multiply_reduce_fusion.1
  154.8 7.7 %multiply_add_fusion = f32[16,256,384]{2,1,0:T(8,128)S(1)} fusion(f32[16,256]{1,0:T(8,128)S(1)} %multiply_reduce_fusion.1, f32[384]{0:T(512)S(1)} %iota_add_fusion, f32[16,256]{1,0:T(8,128)S(1)} %get-tuple-element.7, f32[256,384]{1,0:T(8,128)S(1)} %convert_element_type.39, f32[16,256]{1,0:T(8,128)S(1)} %copy-done.4), kind=kOutput, calls=%fused_computation.2 | convolution fusion | flops 7258914816 | bytes 6735360 | tf_op jit(solution)/shard_map/mcs,st->mct/dot_general | solution.py:14
  162.5 0.0 copy-start.6
  162.5 0.0 copy-start
  162.6 7.6 %fusion = f32[256,1,384]{2,1,0:T(1,128)S(1)} fusion(f32[16,256,1]{0,2,1:T(1,128)S(1)} %copy.8, f32[16,256,384]{2,1,0:T(8,128)S(1)} %multiply_add_fusion), kind=kOutput, calls=%fused_computation | convolution fusion | flops 18874368 | bytes 6701056 | tf_op jit(solution)/shard_map/mc,mct->ct/dot_general | solution.py:105
  170.1 0.0 copy-done.6
  170.1 0.1 fusion.70
  170.3 2.0 collective-permute-start.7
  172.3 4.5 %collective-permute-start.8 = (bf16[256,384]{1,0:T(8,128)(2,1)S(1)}, bf16[256,384]{1,0:T(8,128)(2,1)S(1)}, u32[]{:S(2)}, u32[]{:S(2)}) collective-permute-start(bf16[256,384]{1,0:T(8,128)(2,1)S(1)} %fusion.69), channel_id=1, source_target_pairs={{0,4},{2,6},{4,0},{6,2},{1,5},{3,7},{5,1},{7,3},{8,12},{10,14},{12... | collective-permute-start | bytes 589832 | tf_op jit(solution)/shard_map/ppermute | solution.py:21
  176.7 1.2 collective-permute-start.9
  177.9 0.0 copy-done
  177.9 0.6 fusion.57
  178.5 4.3 %collective-permute-done.7 = bf16[256,384]{1,0:T(8,128)(2,1)S(1)} collective-permute-done((bf16[256,384]{1,0:T(8,128)(2,1)S(1)}, bf16[256,384]{1,0:T(8,128)(2,1)S(1)}, u32[]{:S(2)}, u32[]{:S(2)}) %collective-permute-start.7) | collective-permute-done | bytes 196640 | tf_op jit(solution)/shard_map/ppermute | solution.py:21
  182.8 0.6 fusion.55
  183.4 11.0 %collective-permute-done.8 = bf16[256,384]{1,0:T(8,128)(2,1)S(1)} collective-permute-done((bf16[256,384]{1,0:T(8,128)(2,1)S(1)}, bf16[256,384]{1,0:T(8,128)(2,1)S(1)}, u32[]{:S(2)}, u32[]{:S(2)}) %collective-permute-start.8) | collective-permute-done | bytes 196640 | tf_op jit(solution)/shard_map/ppermute | solution.py:21
  194.5 0.6 fusion.53
  195.0 0.0 collective-permute-done.9
  195.1 1.8 add_convert_fusion
  (9 shorter events, 0.2 us)
Async XLA Ops:
  6.5 12.7 %copy-start.5 = (f32[3,3,256]{2,1,0:T(4,128)S(1)}, f32[3,3,256]{2,1,0:T(4,128)}, u32[]{:S(2)}) copy-start(f32[3,3,256]{2,1,0:T(4,128)} %param.9) | copy-start | bytes 27652
  6.5 12.7 %copy-start.4 = (f32[16,256]{1,0:T(8,128)S(1)}, f32[16,256]{1,0:T(8,128)}, u32[]{:S(2)}) copy-start(f32[16,256]{1,0:T(8,128)} %param.10) | copy-start | bytes 49156
  6.5 12.7 %copy-start.3 = (f32[16,256]{1,0:T(8,128)S(1)}, f32[16,256]{1,0:T(8,128)}, u32[]{:S(2)}) copy-start(f32[16,256]{1,0:T(8,128)} %param.11) | copy-start | bytes 49156
  6.5 81.8 %all-gather.2.cloned.1.call-start = ((), (), s32[]{:S(2)}) async-start(), calls=%async_computation.1 | async-start | bytes 12976128 | tf_op jit(solution)/shard_map/all_gather | solution.py:54
  8.8 49.8 %collective-permute-start.1 = (bf16[384,1024]{1,0:T(8,128)(2,1)S(1)}, bf16[384,1024]{1,0:T(8,128)(2,1)}, u32[]{:S(2)}, u32[]{:S(2)}) collective-permute-start(bf16[384,1024]{1,0:T(8,128)(2,1)S(1)} %get-tuple-element.6), channel_id=1, source_target_pairs={{0,6},{2,0},{4,2},{6,4},{1,7},{3,1},{5,3},{7,5},{8,14},{10,8},{12,... | collective-permute-start | bytes 2359304 | tf_op jit(solution)/shard_map/ppermute | solution.py:21
  15.7 48.9 %collective-permute-start = (bf16[384,1024]{1,0:T(8,128)(2,1)S(1)}, bf16[384,1024]{1,0:T(8,128)(2,1)S(1)}, u32[]{:S(2)}, u32[]{:S(2)}) collective-permute-start(bf16[384,1024]{1,0:T(8,128)(2,1)S(1)} %get-tuple-element.5), channel_id=1, source_target_pairs={{0,2},{2,4},{4,6},{6,0},{1,3},{3,5},{5,7},{7,1},{8,10},{10,12},{12... | collective-permute-start | bytes 2359304 | tf_op jit(solution)/shard_map/ppermute | solution.py:21
  15.7 75.4 %collective-permute-start.2 = (bf16[384,1024]{1,0:T(8,128)(2,1)S(1)}, bf16[384,1024]{1,0:T(8,128)(2,1)}, u32[]{:S(2)}, u32[]{:S(2)}) collective-permute-start(bf16[384,1024]{1,0:T(8,128)(2,1)S(1)} %get-tuple-element.6), channel_id=1, source_target_pairs={{0,2},{2,4},{4,6},{6,0},{1,3},{3,5},{5,7},{7,1},{8,10},{10,12},{12... | collective-permute-start | bytes 2359304 | tf_op jit(solution)/shard_map/ppermute | solution.py:21
  16.9 80.5 %collective-permute-start.3 = (bf16[384,1024]{1,0:T(8,128)(2,1)S(1)}, bf16[384,1024]{1,0:T(8,128)(2,1)}, u32[]{:S(2)}, u32[]{:S(2)}) collective-permute-start(bf16[384,1024]{1,0:T(8,128)(2,1)S(1)} %get-tuple-element.5), channel_id=1, source_target_pairs={{0,6},{2,0},{4,2},{6,4},{1,7},{3,1},{5,3},{7,5},{8,14},{10,8},{12,... | collective-permute-start | bytes 2359304 | tf_op jit(solution)/shard_map/ppermute | solution.py:21
  58.6 55.7 %collective-permute-start.5 = (bf16[384,1024]{1,0:T(8,128)(2,1)}, bf16[384,1024]{1,0:T(8,128)(2,1)}, u32[]{:S(2)}, u32[]{:S(2)}) collective-permute-start(bf16[384,1024]{1,0:T(8,128)(2,1)} %collective-permute-done.1), channel_id=1, source_target_pairs={{0,6},{2,0},{4,2},{6,4},{1,7},{3,1},{5,3},{7,5},{8,14},{10,8},{12,... | collective-permute-start | bytes 2359304 | tf_op jit(solution)/shard_map/ppermute | solution.py:21
  64.6 56.5 %collective-permute-start.4 = (bf16[384,1024]{1,0:T(8,128)(2,1)S(1)}, bf16[384,1024]{1,0:T(8,128)(2,1)S(1)}, u32[]{:S(2)}, u32[]{:S(2)}) collective-permute-start(bf16[384,1024]{1,0:T(8,128)(2,1)S(1)} %collective-permute-done), channel_id=1, source_target_pairs={{0,2},{2,4},{4,6},{6,0},{1,3},{3,5},{5,7},{7,1},{8,10},{10,12},{12... | collective-permute-start | bytes 2359304 | tf_op jit(solution)/shard_map/ppermute | solution.py:21
  88.3 28.6 %copy-start.2 = (bf16[256,3,8192]{2,0,1:T(8,128)(2,1)S(1)}, bf16[256,3,8192]{2,0,1:T(8,128)(2,1)}, u32[]{:S(2)}) copy-start(bf16[256,3,8192]{2,0,1:T(8,128)(2,1)} %all-gather.2.cloned.1.call-done) | copy-start | bytes 37748740
  94.3 22.6 %copy-start.1 = (bf16[384,2048]{1,0:T(8,128)(2,1)S(1)}, bf16[384,2048]{1,0:T(8,128)(2,1)}, u32[]{:S(2)}) copy-start(bf16[384,2048]{1,0:T(8,128)(2,1)} %param.7) | copy-start | bytes 4718596
  122.2 8.0 %collective-permute-start.6 = (bf16[256,3,2]{2,0,1:T(8,128)(2,1)S(1)}, bf16[256,3,2]{2,0,1:T(8,128)(2,1)S(1)}, u32[]{:S(2)}, u32[]{:S(2)}) collective-permute-start(bf16[256,3,2]{2,0,1:T(8,128)(2,1)S(1)} %slice.51), channel_id=1, source_target_pairs={{0,8},{8,16},{16,24},{24,32},{32,40},{40,48},{48,56},{56,64},{64,7... | collective-permute-start | bytes 9224 | tf_op jit(solution)/shard_map/ppermute | solution.py:10
  134.7 20.0 %all-to-all-start = ((f32[32,16,256]{2,1,0:T(8,128)}), f32[32,16,256]{2,1,0:T(8,128)S(1)}, u32[]{:S(2)}, u32[]{:S(2)}) async-start(f32[32,16,256]{2,1,0:T(8,128)} %broadcast_in_dim.12), calls=%async_computation | async-start | bytes 1048576 | tf_op jit(solution)/shard_map/all_to_all | solution.py:87
  162.5 7.6 %copy-start.6 = (f32[256]{0:T(256)S(1)}, f32[256]{0:T(256)}, u32[]{:S(2)}) copy-start(f32[256]{0:T(256)} %param.12) | copy-start | bytes 3076
  162.5 15.4 %copy-start = (bf16[1024,2048]{1,0:T(8,128)(2,1)S(1)}, bf16[1024,2048]{1,0:T(8,128)(2,1)}, u32[]{:S(2)}) copy-start(bf16[1024,2048]{1,0:T(8,128)(2,1)} %param.13) | copy-start | bytes 12582916
  170.3 12.5 %collective-permute-start.7 = (bf16[256,384]{1,0:T(8,128)(2,1)S(1)}, bf16[256,384]{1,0:T(8,128)(2,1)S(1)}, u32[]{:S(2)}, u32[]{:S(2)}) collective-permute-start(bf16[256,384]{1,0:T(8,128)(2,1)S(1)} %fusion.69), channel_id=1, source_target_pairs={{0,2},{2,4},{4,6},{6,0},{1,3},{3,5},{5,7},{7,1},{8,10},{10,12},{12... | collective-permute-start | bytes 589832 | tf_op jit(solution)/shard_map/ppermute | solution.py:21
  172.3 22.2 %collective-permute-start.8 = (bf16[256,384]{1,0:T(8,128)(2,1)S(1)}, bf16[256,384]{1,0:T(8,128)(2,1)S(1)}, u32[]{:S(2)}, u32[]{:S(2)}) collective-permute-start(bf16[256,384]{1,0:T(8,128)(2,1)S(1)} %fusion.69), channel_id=1, source_target_pairs={{0,4},{2,6},{4,0},{6,2},{1,5},{3,7},{5,1},{7,3},{8,12},{10,14},{12... | collective-permute-start | bytes 589832 | tf_op jit(solution)/shard_map/ppermute | solution.py:21
  176.7 18.3 %collective-permute-start.9 = (bf16[256,384]{1,0:T(8,128)(2,1)S(1)}, bf16[256,384]{1,0:T(8,128)(2,1)S(1)}, u32[]{:S(2)}, u32[]{:S(2)}) collective-permute-start(bf16[256,384]{1,0:T(8,128)(2,1)S(1)} %fusion.69), channel_id=1, source_target_pairs={{0,6},{2,0},{4,2},{6,4},{1,7},{3,1},{5,3},{7,5},{8,14},{10,8},{12,... | collective-permute-start | bytes 589832 | tf_op jit(solution)/shard_map/ppermute | solution.py:21
Sparse Core Ops, SparseCore 0:
  9.8 78.4 all-gather.1

commit v4 on v3

--- a/solution.py
+++ b/solution.py
@@ -101,8 +101,9 @@
     incoming = jnp.sum(carry * states, axis=0)
     prefix = hidot("mcs,st->mct", grow * z_f[None], upper)
     intra = fall * prefix
-    inter = jnp.exp(-decay[:, :, None] * (tau + 1.0)) * incoming[:, :, None]
-    conv = jnp.einsum("mc,mct->ct", gains, intra + inter, precision=lax.Precision.HIGHEST)
+    near = jnp.sum(gains[:, :, None] * intra, axis=0)
+    onward = lax.optimization_barrier(jnp.exp(-decay[:, :, None] * (tau + 1.0)))
+    conv = near + jnp.sum((gains * incoming)[:, :, None] * onward, axis=0)
     longc = (conv + skip[:, None] * z_f).astype(jnp.bfloat16)
     long_f = lax.optimization_barrier(longc).astype(jnp.float32)
     gated = (query * long_f).astype(jnp.bfloat16)

time: 204 us -> 200 us (0.980)
  matrix products: 33.9 us -> 26.5 us
  other arithmetic: 3.97 us -> 6.86 us
    dot_general x1 -> x0, matrix products: 7.56 us -> none  [on_device(): jnp.einsum('mc,mct->ct', gains, intra + inter, precision=lax.Precision.HI...]
    exp x0 -> x1, other arithmetic: none -> 3.99 us  [on_device(): onward = lax.optimization_barrier(jnp.exp(-decay[:, :, None] * (tau + 1.0)))]
where the time goes in v4:
time: 200 us; the launch traced here: 199 us
  waiting for transfers between devices  112 us (56%)
  starting transfers between devices  38.1 us (19%)
  matrix products  26.5 us (13%)
  between operations  13.7 us (7%)
  other arithmetic  6.86 us (3%)
  local copies, waits for them, and re-layouts  2.51 us (1%)
    ppermute x9, waiting for transfers between devices, ring_shift(): lax.ppermute(value, axis, [(source, (source + steps) % count) for source...  73.3 us
    ppermute x9, starting transfers between devices, ring_shift(): lax.ppermute(value, axis, [(source, (source + steps) % count) for source...  24.1 us
    all_gather x1, waiting for transfers between devices, on_device(): w_full = lax.all_gather(w_in, 'seq', axis=2, tiled=True)  23.7 us
    dot_general x6, matrix products, on_device(): jnp.einsum('cgd,td->cgt', block_of(step, lo, hi), piece, preferred_elemen...  13.3 us
    all_to_all x1, waiting for transfers between devices, on_device(): lax.all_to_all(jnp.broadcast_to(ending[None], (seq_count,) + ending.shape...  11.5 us
    all_to_all x1, starting transfers between devices, on_device(): lax.all_to_all(jnp.broadcast_to(ending[None], (seq_count,) + ending.shape...  8.38 us
    dot_general x1, matrix products, hidot(): jnp.einsum(form, left, right, precision=lax.Precision.HIGHEST, preferred_...  7.86 us
    ppermute x1, starting transfers between devices, from_behind(): lax.ppermute(value, axis, [(source, source + steps) for source in range(l...  5.57 us
  transfers between devices with their start and end apart: 12, of which 9 were waited for; matrix products, arithmetic and copies ran while one was open for 9% of the time, Pallas kernels for 0%

profile of v4, /device:TPU:1, one launch (start us, length us, event | category | flops | bytes accessed | tf_op | source)
XLA Modules:
  0.0 199.3 jit_solution(2944860797909662154)
XLA Ops:
  6.5 0.0 copy-start.5
  6.5 0.0 all-gather.2.cloned.1.call-start
  6.5 0.7 all-gather.2.cloned.1.call-update
  7.3 1.5 fusion.81
  8.8 6.9 %collective-permute-start.1 = (bf16[384,1024]{1,0:T(8,128)(2,1)S(1)}, bf16[384,1024]{1,0:T(8,128)(2,1)}, u32[]{:S(2)}, u32[]{:S(2)}) collective-permute-start(bf16[384,1024]{1,0:T(8,128)(2,1)S(1)} %get-tuple-element.8), channel_id=1, source_target_pairs={{0,6},{2,0},{4,2},{6,4},{1,7},{3,1},{5,3},{7,5},{8,14},{10,8},{12,... | collective-permute-start | bytes 2359304 | tf_op jit(solution)/shard_map/ppermute | solution.py:21
  15.7 0.0 collective-permute-start
  15.7 1.3 collective-permute-start.2
  16.9 2.3 %collective-permute-start.3 = (bf16[384,1024]{1,0:T(8,128)(2,1)S(1)}, bf16[384,1024]{1,0:T(8,128)(2,1)}, u32[]{:S(2)}, u32[]{:S(2)}) collective-permute-start(bf16[384,1024]{1,0:T(8,128)(2,1)S(1)} %get-tuple-element.7), channel_id=1, source_target_pairs={{0,6},{2,0},{4,2},{6,4},{1,7},{3,1},{5,3},{7,5},{8,14},{10,8},{12,... | collective-permute-start | bytes 2359304 | tf_op jit(solution)/shard_map/ppermute | solution.py:21
  19.3 0.0 copy-done.5
  19.3 39.3 %collective-permute-done.1 = bf16[384,1024]{1,0:T(8,128)(2,1)} collective-permute-done((bf16[384,1024]{1,0:T(8,128)(2,1)S(1)}, bf16[384,1024]{1,0:T(8,128)(2,1)}, u32[]{:S(2)}, u32[]{:S(2)}) %collective-permute-start.1) | collective-permute-done | bytes 786464 | tf_op jit(solution)/shard_map/ppermute | solution.py:21
  58.6 6.0 %collective-permute-start.5 = (bf16[384,1024]{1,0:T(8,128)(2,1)}, bf16[384,1024]{1,0:T(8,128)(2,1)}, u32[]{:S(2)}, u32[]{:S(2)}) collective-permute-start(bf16[384,1024]{1,0:T(8,128)(2,1)} %collective-permute-done.1), channel_id=1, source_target_pairs={{0,6},{2,0},{4,2},{6,4},{1,7},{3,1},{5,3},{7,5},{8,14},{10,8},{12,... | collective-permute-start | bytes 2359304 | tf_op jit(solution)/shard_map/ppermute | solution.py:21
  64.6 0.0 collective-permute-done
  64.6 0.0 collective-permute-start.4
  64.6 23.7 %all-gather.2.cloned.1.call-done = bf16[256,3,8192]{2,0,1:T(8,128)(2,1)} async-done(((bf16[256,3,256]{2,0,1:T(8,128)(2,1)}), bf16[256,3,8192]{2,0,1:T(8,128)(2,1)}) %all-gather.2.cloned.1.call-update) | async-done | bytes 12582928 | tf_op jit(solution)/shard_map/all_gather | solution.py:54
  88.3 2.8 %fusion.20 = f32[256,3,384]{2,0,1:T(8,128)S(1)} fusion(bf16[256,3,8192]{2,0,1:T(8,128)(2,1)} %all-gather.2.cloned.1.call-done, s32[]{:T(128)S(6)} %select_n.75, bf16[384,1024]{1,0:T(8,128)(2,1)} %collective-permute-done.1), kind=kOutput, calls=%fused_computation.23 | convolution fusion | flops 603979776 | bytes 3538948 | tf_op jit(solution)/shard_map/cgd,td->cgt/dot_general | solution.py:62
  91.1 0.0 collective-permute-done.2
  91.1 3.2 %fusion.18 = f32[256,3,384]{2,0,1:T(8,128)S(1)} fusion(bf16[256,3,8192]{2,0,1:T(8,128)(2,1)} %all-gather.2.cloned.1.call-done, s32[]{:T(128)S(6)} %select_n.76, bf16[384,1024]{1,0:T(8,128)(2,1)} %collective-permute-done.2), kind=kOutput, calls=%fused_computation.21 | convolution fusion | flops 603979776 | bytes 3538948 | tf_op jit(solution)/shard_map/cgd,td->cgt/dot_general | solution.py:62
  94.3 0.0 copy-start.1
  94.3 3.1 %collective-permute-done.3 = bf16[384,1024]{1,0:T(8,128)(2,1)} collective-permute-done((bf16[384,1024]{1,0:T(8,128)(2,1)S(1)}, bf16[384,1024]{1,0:T(8,128)(2,1)}, u32[]{:S(2)}, u32[]{:S(2)}) %collective-permute-start.3) | collective-permute-done | bytes 786464 | tf_op jit(solution)/shard_map/ppermute | solution.py:21
  97.4 2.6 %fusion.16 = f32[256,3,384]{2,0,1:T(8,128)S(1)} fusion(bf16[256,3,8192]{2,0,1:T(8,128)(2,1)} %all-gather.2.cloned.1.call-done, s32[]{:T(128)S(6)} %select_n.77, bf16[384,1024]{1,0:T(8,128)(2,1)} %collective-permute-done.3), kind=kOutput, calls=%fused_computation.19 | convolution fusion | flops 603979776 | bytes 3538948 | tf_op jit(solution)/shard_map/cgd,td->cgt/dot_general | solution.py:62
  100.0 14.3 %collective-permute-done.5 = bf16[384,1024]{1,0:T(8,128)(2,1)} collective-permute-done((bf16[384,1024]{1,0:T(8,128)(2,1)}, bf16[384,1024]{1,0:T(8,128)(2,1)}, u32[]{:S(2)}, u32[]{:S(2)}) %collective-permute-start.5) | collective-permute-done | bytes 786464 | tf_op jit(solution)/shard_map/ppermute | solution.py:21
  114.3 2.6 %fusion.12 = f32[256,3,384]{2,0,1:T(8,128)S(1)} fusion(bf16[256,3,8192]{2,0,1:T(8,128)(2,1)} %all-gather.2.cloned.1.call-done, s32[]{:T(128)S(6)} %select_n.80, bf16[384,1024]{1,0:T(8,128)(2,1)} %collective-permute-done.5), kind=kOutput, calls=%fused_computation.15 | convolution fusion | flops 603979776 | bytes 3538948 | tf_op jit(solution)/shard_map/cgd,td->cgt/dot_general | solution.py:62
  116.9 0.0 copy-done.2
  116.9 0.0 copy-done.1
  116.9 1.8 fusion.7
  118.7 1.0 fusion.39
  119.8 0.0 copy-start.3
  119.8 1.2 collective-permute-done.4
  121.0 1.0 fusion.42
  122.1 0.1 slice.51
  122.2 5.6 %collective-permute-start.6 = (bf16[256,3,2]{2,0,1:T(8,128)(2,1)S(1)}, bf16[256,3,2]{2,0,1:T(8,128)(2,1)S(1)}, u32[]{:S(2)}, u32[]{:S(2)}) collective-permute-start(bf16[256,3,2]{2,0,1:T(8,128)(2,1)S(1)} %slice.51), channel_id=1, source_target_pairs={{0,8},{8,16},{16,24},{24,32},{32,40},{40,48},{48,56},{56,64},{64,7... | collective-permute-start | bytes 9224 | tf_op jit(solution)/shard_map/ppermute | solution.py:10
  127.8 0.0 copy-done.3
  127.8 2.4 %collective-permute-done.6 = bf16[256,3,2]{2,0,1:T(8,128)(2,1)S(1)} collective-permute-done((bf16[256,3,2]{2,0,1:T(8,128)(2,1)S(1)}, bf16[256,3,2]{2,0,1:T(8,128)(2,1)S(1)}, u32[]{:S(2)}, u32[]{:S(2)}) %collective-permute-start.6) | collective-permute-done | bytes 3104 | tf_op jit(solution)/shard_map/ppermute | solution.py:10
  130.2 0.4 pad_maximum_fusion
  130.6 0.2 convert_element_type.36
  130.8 1.1 fusion.45
  132.0 0.0 copy-start.4
  132.0 4.0 %multiply_exponential_fusion = (f32[16,256,384]{2,1,0:T(8,128)}, f32[16,256]{1,0:T(8,128)S(1)}) fusion(f32[384]{0:T(512)S(1)} %get-tuple-element.14, f32[16,256]{1,0:T(8,128)S(1)} %neg.8, f32[256,384]{1,0:T(8,128)S(1)} %convert_element_type.39, f32[384]{0:T(512)S(1)} %get-tuple-element.15), kind=kLoop, calls=%fused_computation.1 | loop fusion | flops 6287360 | bytes 6720512 | tf_op jit(solution)/shard_map/exp | solution.py:105
  136.0 0.9 broadcast_in_dim.12
  136.8 8.4 %all-to-all-start = ((f32[32,16,256]{2,1,0:T(8,128)}), f32[32,16,256]{2,1,0:T(8,128)S(1)}, u32[]{:S(2)}, u32[]{:S(2)}) async-start(f32[32,16,256]{2,1,0:T(8,128)} %broadcast_in_dim.12), calls=%async_computation | async-start | bytes 1048576 | tf_op jit(solution)/shard_map/all_to_all | solution.py:87
  145.3 11.5 %all-to-all-done = f32[32,16,256]{2,1,0:T(8,128)S(1)} async-done(((f32[32,16,256]{2,1,0:T(8,128)}), f32[32,16,256]{2,1,0:T(8,128)S(1)}, u32[]{:S(2)}, u32[]{:S(2)}) %all-to-all-start) | async-done | bytes 524320 | tf_op jit(solution)/shard_map/all_to_all | solution.py:87
  156.8 0.2 multiply_reduce_fusion.3
  157.0 0.0 copy-done.4
  157.0 0.0 slice-start.1
  157.0 7.9 %multiply_reduce_fusion.2 = f32[256,384]{1,0:T(8,128)S(1)} fusion(f32[16,256]{1,0:T(8,128)S(1)} %neg.8, f32[16,256]{1,0:T(8,128)S(1)} %get-tuple-element.6, f32[256,384]{1,0:T(8,128)S(1)} %convert_element_type.39, f32[16,256]{1,0:T(8,128)S(1)} %copy-done.3), kind=kOutput, calls=%fused_computation.3 | convolution fusion | flops 7257243648 | bytes 835584 | tf_op jit(solution)/shard_map/mcs,st->mct/dot_general | solution.py:14
  164.9 0.0 slice-done
  164.9 0.0 slice-done.1
  164.9 0.0 copy-start.6
  164.9 0.0 copy-start
  164.9 0.7 multiply_reduce_fusion
  165.7 0.0 copy-done.6
  165.7 0.1 add_convert_fusion.1
  165.8 0.1 fusion.67
  165.9 2.0 collective-permute-start.7
  167.8 4.5 %collective-permute-start.8 = (bf16[256,384]{1,0:T(8,128)(2,1)S(1)}, bf16[256,384]{1,0:T(8,128)(2,1)S(1)}, u32[]{:S(2)}, u32[]{:S(2)}) collective-permute-start(bf16[256,384]{1,0:T(8,128)(2,1)S(1)} %fusion.67), channel_id=1, source_target_pairs={{0,4},{2,6},{4,0},{6,2},{1,5},{3,7},{5,1},{7,3},{8,12},{10,14},{12... | collective-permute-start | bytes 589832 | tf_op jit(solution)/shard_map/ppermute | solution.py:21
  172.3 1.2 collective-permute-start.9
  173.5 0.0 copy-done
  173.5 0.6 fusion.55
  174.1 4.3 %collective-permute-done.7 = bf16[256,384]{1,0:T(8,128)(2,1)S(1)} collective-permute-done((bf16[256,384]{1,0:T(8,128)(2,1)S(1)}, bf16[256,384]{1,0:T(8,128)(2,1)S(1)}, u32[]{:S(2)}, u32[]{:S(2)}) %collective-permute-start.7) | collective-permute-done | bytes 196640 | tf_op jit(solution)/shard_map/ppermute | solution.py:21
  178.4 0.6 fusion.53
  179.0 11.0 %collective-permute-done.8 = bf16[256,384]{1,0:T(8,128)(2,1)S(1)} collective-permute-done((bf16[256,384]{1,0:T(8,128)(2,1)S(1)}, bf16[256,384]{1,0:T(8,128)(2,1)S(1)}, u32[]{:S(2)}, u32[]{:S(2)}) %collective-permute-start.8) | collective-permute-done | bytes 196640 | tf_op jit(solution)/shard_map/ppermute | solution.py:21
  190.0 0.6 fusion.51
  190.6 0.0 collective-permute-done.9
  190.6 1.8 add_convert_fusion
  (11 shorter events, 0.1 us)
Async XLA Ops:
  6.5 12.7 %copy-start.5 = (f32[3,3,256]{2,1,0:T(4,128)S(1)}, f32[3,3,256]{2,1,0:T(4,128)}, u32[]{:S(2)}) copy-start(f32[3,3,256]{2,1,0:T(4,128)} %param.9) | copy-start | bytes 27652
  6.5 81.8 %all-gather.2.cloned.1.call-start = ((), (), s32[]{:S(2)}) async-start(), calls=%async_computation.1 | async-start | bytes 12976128 | tf_op jit(solution)/shard_map/all_gather | solution.py:54
  8.8 49.8 %collective-permute-start.1 = (bf16[384,1024]{1,0:T(8,128)(2,1)S(1)}, bf16[384,1024]{1,0:T(8,128)(2,1)}, u32[]{:S(2)}, u32[]{:S(2)}) collective-permute-start(bf16[384,1024]{1,0:T(8,128)(2,1)S(1)} %get-tuple-element.8), channel_id=1, source_target_pairs={{0,6},{2,0},{4,2},{6,4},{1,7},{3,1},{5,3},{7,5},{8,14},{10,8},{12,... | collective-permute-start | bytes 2359304 | tf_op jit(solution)/shard_map/ppermute | solution.py:21
  15.7 48.9 %collective-permute-start = (bf16[384,1024]{1,0:T(8,128)(2,1)S(1)}, bf16[384,1024]{1,0:T(8,128)(2,1)S(1)}, u32[]{:S(2)}, u32[]{:S(2)}) collective-permute-start(bf16[384,1024]{1,0:T(8,128)(2,1)S(1)} %get-tuple-element.7), channel_id=1, source_target_pairs={{0,2},{2,4},{4,6},{6,0},{1,3},{3,5},{5,7},{7,1},{8,10},{10,12},{12... | collective-permute-start | bytes 2359304 | tf_op jit(solution)/shard_map/ppermute | solution.py:21
  15.7 75.4 %collective-permute-start.2 = (bf16[384,1024]{1,0:T(8,128)(2,1)S(1)}, bf16[384,1024]{1,0:T(8,128)(2,1)}, u32[]{:S(2)}, u32[]{:S(2)}) collective-permute-start(bf16[384,1024]{1,0:T(8,128)(2,1)S(1)} %get-tuple-element.8), channel_id=1, source_target_pairs={{0,2},{2,4},{4,6},{6,0},{1,3},{3,5},{5,7},{7,1},{8,10},{10,12},{12... | collective-permute-start | bytes 2359304 | tf_op jit(solution)/shard_map/ppermute | solution.py:21
  16.9 80.5 %collective-permute-start.3 = (bf16[384,1024]{1,0:T(8,128)(2,1)S(1)}, bf16[384,1024]{1,0:T(8,128)(2,1)}, u32[]{:S(2)}, u32[]{:S(2)}) collective-permute-start(bf16[384,1024]{1,0:T(8,128)(2,1)S(1)} %get-tuple-element.7), channel_id=1, source_target_pairs={{0,6},{2,0},{4,2},{6,4},{1,7},{3,1},{5,3},{7,5},{8,14},{10,8},{12,... | collective-permute-start | bytes 2359304 | tf_op jit(solution)/shard_map/ppermute | solution.py:21
  58.6 55.7 %collective-permute-start.5 = (bf16[384,1024]{1,0:T(8,128)(2,1)}, bf16[384,1024]{1,0:T(8,128)(2,1)}, u32[]{:S(2)}, u32[]{:S(2)}) collective-permute-start(bf16[384,1024]{1,0:T(8,128)(2,1)} %collective-permute-done.1), channel_id=1, source_target_pairs={{0,6},{2,0},{4,2},{6,4},{1,7},{3,1},{5,3},{7,5},{8,14},{10,8},{12,... | collective-permute-start | bytes 2359304 | tf_op jit(solution)/shard_map/ppermute | solution.py:21
  64.6 56.5 %collective-permute-start.4 = (bf16[384,1024]{1,0:T(8,128)(2,1)S(1)}, bf16[384,1024]{1,0:T(8,128)(2,1)S(1)}, u32[]{:S(2)}, u32[]{:S(2)}) collective-permute-start(bf16[384,1024]{1,0:T(8,128)(2,1)S(1)} %collective-permute-done), channel_id=1, source_target_pairs={{0,2},{2,4},{4,6},{6,0},{1,3},{3,5},{5,7},{7,1},{8,10},{10,12},{12... | collective-permute-start | bytes 2359304 | tf_op jit(solution)/shard_map/ppermute | solution.py:21
  88.3 28.6 %copy-start.2 = (bf16[256,3,8192]{2,0,1:T(8,128)(2,1)S(1)}, bf16[256,3,8192]{2,0,1:T(8,128)(2,1)}, u32[]{:S(2)}) copy-start(bf16[256,3,8192]{2,0,1:T(8,128)(2,1)} %all-gather.2.cloned.1.call-done) | copy-start | bytes 37748740
  94.3 22.6 %copy-start.1 = (bf16[384,2048]{1,0:T(8,128)(2,1)S(1)}, bf16[384,2048]{1,0:T(8,128)(2,1)}, u32[]{:S(2)}) copy-start(bf16[384,2048]{1,0:T(8,128)(2,1)} %param.7) | copy-start | bytes 4718596
  119.8 8.0 %copy-start.3 = (f32[16,256]{1,0:T(8,128)S(1)}, f32[16,256]{1,0:T(8,128)}, u32[]{:S(2)}) copy-start(f32[16,256]{1,0:T(8,128)} %param.10) | copy-start | bytes 49156
  122.2 8.0 %collective-permute-start.6 = (bf16[256,3,2]{2,0,1:T(8,128)(2,1)S(1)}, bf16[256,3,2]{2,0,1:T(8,128)(2,1)S(1)}, u32[]{:S(2)}, u32[]{:S(2)}) collective-permute-start(bf16[256,3,2]{2,0,1:T(8,128)(2,1)S(1)} %slice.51), channel_id=1, source_target_pairs={{0,8},{8,16},{16,24},{24,32},{32,40},{40,48},{48,56},{56,64},{64,7... | collective-permute-start | bytes 9224 | tf_op jit(solution)/shard_map/ppermute | solution.py:10
  132.0 25.0 %copy-start.4 = (f32[16,256]{1,0:T(8,128)S(1)}, f32[16,256]{1,0:T(8,128)}, u32[]{:S(2)}) copy-start(f32[16,256]{1,0:T(8,128)} %param.11) | copy-start | bytes 49156
  136.8 20.0 %all-to-all-start = ((f32[32,16,256]{2,1,0:T(8,128)}), f32[32,16,256]{2,1,0:T(8,128)S(1)}, u32[]{:S(2)}, u32[]{:S(2)}) async-start(f32[32,16,256]{2,1,0:T(8,128)} %broadcast_in_dim.12), calls=%async_computation | async-start | bytes 1048576 | tf_op jit(solution)/shard_map/all_to_all | solution.py:87
  156.8 8.1 %slice-start = ((s8[6291456]{0:T(1024)(128)(4,1)}), s8[4194304]{0:T(1024)(128)(4,1)S(1)}, s32[]{:S(2)}) async-start(s8[6291456]{0:T(1024)(128)(4,1)} %bitcast.43), calls=%async_computation.2 | async-start | bytes 8388608
  157.0 7.9 %slice-start.1 = ((s8[6291456]{0:T(1024)(128)(4,1)}), s8[2097152]{0:T(1024)(128)(4,1)S(1)}, s32[]{:S(2)}) async-start(s8[6291456]{0:T(1024)(128)(4,1)} %bitcast.43), calls=%async_computation.3 | async-start | bytes 4194304
  164.9 0.8 copy-start.6
  164.9 8.6 %copy-start = (bf16[1024,2048]{1,0:T(8,128)(2,1)S(1)}, bf16[1024,2048]{1,0:T(8,128)(2,1)}, u32[]{:S(2)}) copy-start(bf16[1024,2048]{1,0:T(8,128)(2,1)} %param.13) | copy-start | bytes 12582916
  165.9 12.5 %collective-permute-start.7 = (bf16[256,384]{1,0:T(8,128)(2,1)S(1)}, bf16[256,384]{1,0:T(8,128)(2,1)S(1)}, u32[]{:S(2)}, u32[]{:S(2)}) collective-permute-start(bf16[256,384]{1,0:T(8,128)(2,1)S(1)} %fusion.67), channel_id=1, source_target_pairs={{0,2},{2,4},{4,6},{6,0},{1,3},{3,5},{5,7},{7,1},{8,10},{10,12},{12... | collective-permute-start | bytes 589832 | tf_op jit(solution)/shard_map/ppermute | solution.py:21
  167.8 22.2 %collective-permute-start.8 = (bf16[256,384]{1,0:T(8,128)(2,1)S(1)}, bf16[256,384]{1,0:T(8,128)(2,1)S(1)}, u32[]{:S(2)}, u32[]{:S(2)}) collective-permute-start(bf16[256,384]{1,0:T(8,128)(2,1)S(1)} %fusion.67), channel_id=1, source_target_pairs={{0,4},{2,6},{4,0},{6,2},{1,5},{3,7},{5,1},{7,3},{8,12},{10,14},{12... | collective-permute-start | bytes 589832 | tf_op jit(solution)/shard_map/ppermute | solution.py:21
  172.3 18.3 %collective-permute-start.9 = (bf16[256,384]{1,0:T(8,128)(2,1)S(1)}, bf16[256,384]{1,0:T(8,128)(2,1)S(1)}, u32[]{:S(2)}, u32[]{:S(2)}) collective-permute-start(bf16[256,384]{1,0:T(8,128)(2,1)S(1)} %fusion.67), channel_id=1, source_target_pairs={{0,6},{2,0},{4,2},{6,4},{1,7},{3,1},{5,3},{7,5},{8,14},{10,8},{12,... | collective-permute-start | bytes 589832 | tf_op jit(solution)/shard_map/ppermute | solution.py:21
Sparse Core Ops, SparseCore 0:
  9.8 78.4 all-gather.1

commit v5 on v2

--- a/solution.py
+++ b/solution.py
@@ -84,18 +84,16 @@
     upper = (tau[:, None] <= tau[None, :]).astype(jnp.float32)
     tail = jnp.exp(-decay[:, :, None] * (tok_rows - 1.0 - tau))
     ending = jnp.sum(tail * z_f[None], axis=2)
-    blocks = jnp.arange(seq_count)
-    lag = jnp.maximum(blocks - 1 - seq_rank, 0).astype(jnp.float32)
-    carry = jnp.where(
-        (blocks > seq_rank)[:, None, None],
-        jnp.exp(-decay[None] * (tok_rows * lag)[:, None, None]),
-        0.0,
-    )
-    incoming = lax.psum_scatter(carry * ending[None], "seq", scatter_dimension=0, tiled=True)[0]
+    incoming = from_behind(ending, "seq", 1)
+    span = 1
+    while span < seq_count:
+        incoming = incoming + jnp.exp(-decay * float(tok_rows * span)) * from_behind(incoming, "seq", span)
+        span *= 2
     prefix = hidot("mcs,st->mct", grow * z_f[None], upper)
     intra = fall * prefix
-    inter = jnp.exp(-decay[:, :, None] * (tau + 1.0)) * incoming[:, :, None]
-    conv = jnp.einsum("mc,mct->ct", gains, intra + inter, precision=lax.Precision.HIGHEST)
+    near = jnp.sum(gains[:, :, None] * intra, axis=0)
+    onward = lax.optimization_barrier(jnp.exp(-decay[:, :, None] * (tau + 1.0)))
+    conv = near + jnp.sum((gains * incoming)[:, :, None] * onward, axis=0)
     longc = (conv + skip[:, None] * z_f).astype(jnp.bfloat16)
     long_f = lax.optimization_barrier(longc).astype(jnp.float32)
     gated = (query * long_f).astype(jnp.bfloat16)

time: 269 us -> 217 us (0.81)
  the two profiles are of different devices: /device:TPU:1 before, /device:TPU:6 now
where the time goes in v5:
time: 217 us; the launch traced here: 216 us
  waiting for transfers between devices  131 us (60%)
  starting transfers between devices  36.3 us (17%)
  matrix products  27.1 us (12%)
  between operations  13.7 us (6%)
  other arithmetic  6.77 us (3%)
    ppermute x9, waiting for transfers between devices, ring_shift(): lax.ppermute(value, axis, [(source, (source + steps) % count) for source...  71.1 us
    ppermute x7, waiting for transfers between devices, from_behind(): lax.ppermute(value, axis, [(source, source + steps) for source in range(l...  39.5 us
    ppermute x9, starting transfers between devices, ring_shift(): lax.ppermute(value, axis, [(source, (source + steps) % count) for source...  23.8 us
    all_gather x1, waiting for transfers between devices, on_device(): w_full = lax.all_gather(w_in, 'seq', axis=2, tiled=True)  19.3 us
    dot_general x6, matrix products, on_device(): jnp.einsum('cgd,td->cgt', block_of(step, lo, hi), piece, preferred_elemen...  12.8 us
    ppermute x7, starting transfers between devices, from_behind(): lax.ppermute(value, axis, [(source, source + steps) for source in range(l...  12.5 us
    dot_general x1, matrix products, hidot(): jnp.einsum(form, left, right, precision=lax.Precision.HIGHEST, preferred_...  8.96 us
  transfers between devices with their start and end apart: 17, of which 14 were waited for; matrix products, arithmetic and copies ran while one was open for 8% of the time, Pallas kernels for 0%

profile of v5, /device:TPU:6, one launch (start us, length us, event | category | flops | bytes accessed | tf_op | source)
XLA Modules:
  0.0 216.2 jit_solution(10139603360391695513)
XLA Ops:
  6.5 0.7 all-gather.2.cloned.1.call-update
  7.3 1.5 fusion.80
  8.8 6.4 %collective-permute-start.1 = (bf16[384,1024]{1,0:T(8,128)(2,1)S(1)}, bf16[384,1024]{1,0:T(8,128)(2,1)}, u32[]{:S(2)}, u32[]{:S(2)}) collective-permute-start(bf16[384,1024]{1,0:T(8,128)(2,1)S(1)} %get-tuple-element.8), channel_id=1, source_target_pairs={{0,6},{2,0},{4,2},{6,4},{1,7},{3,1},{5,3},{7,5},{8,14},{10,8},{12,... | collective-permute-start | bytes 2359304 | tf_op jit(solution)/shard_map/ppermute | solution.py:21
  15.1 0.0 collective-permute-start
  15.1 1.5 collective-permute-start.2
  16.7 2.6 %collective-permute-start.3 = (bf16[384,1024]{1,0:T(8,128)(2,1)S(1)}, bf16[384,1024]{1,0:T(8,128)(2,1)}, u32[]{:S(2)}, u32[]{:S(2)}) collective-permute-start(bf16[384,1024]{1,0:T(8,128)(2,1)S(1)} %get-tuple-element.7), channel_id=1, source_target_pairs={{0,6},{2,0},{4,2},{6,4},{1,7},{3,1},{5,3},{7,5},{8,14},{10,8},{12,... | collective-permute-start | bytes 2359304 | tf_op jit(solution)/shard_map/ppermute | solution.py:21
  19.3 42.7 %collective-permute-done.1 = bf16[384,1024]{1,0:T(8,128)(2,1)} collective-permute-done((bf16[384,1024]{1,0:T(8,128)(2,1)S(1)}, bf16[384,1024]{1,0:T(8,128)(2,1)}, u32[]{:S(2)}, u32[]{:S(2)}) %collective-permute-start.1) | collective-permute-done | bytes 786464 | tf_op jit(solution)/shard_map/ppermute | solution.py:21
  62.0 4.8 %collective-permute-start.5 = (bf16[384,1024]{1,0:T(8,128)(2,1)}, bf16[384,1024]{1,0:T(8,128)(2,1)}, u32[]{:S(2)}, u32[]{:S(2)}) collective-permute-start(bf16[384,1024]{1,0:T(8,128)(2,1)} %collective-permute-done.1), channel_id=1, source_target_pairs={{0,6},{2,0},{4,2},{6,4},{1,7},{3,1},{5,3},{7,5},{8,14},{10,8},{12,... | collective-permute-start | bytes 2359304 | tf_op jit(solution)/shard_map/ppermute | solution.py:21
  66.8 0.0 collective-permute-done
  66.8 0.0 collective-permute-start.4
  66.8 19.3 %all-gather.2.cloned.1.call-done = bf16[256,3,8192]{2,0,1:T(8,128)(2,1)} async-done(((bf16[256,3,256]{2,0,1:T(8,128)(2,1)}), bf16[256,3,8192]{2,0,1:T(8,128)(2,1)}) %all-gather.2.cloned.1.call-update) | async-done | bytes 12582928 | tf_op jit(solution)/shard_map/all_gather | solution.py:54
  86.2 2.8 %fusion.20 = f32[256,3,384]{2,0,1:T(8,128)S(1)} fusion(bf16[256,3,8192]{2,0,1:T(8,128)(2,1)} %all-gather.2.cloned.1.call-done, s32[]{:T(128)S(6)} %select_n.71, bf16[384,1024]{1,0:T(8,128)(2,1)} %collective-permute-done.1), kind=kOutput, calls=%fused_computation.23 | convolution fusion | flops 603979776 | bytes 3538948 | tf_op jit(solution)/shard_map/cgd,td->cgt/dot_general | solution.py:62
  88.9 14.5 %collective-permute-done.2 = bf16[384,1024]{1,0:T(8,128)(2,1)} collective-permute-done((bf16[384,1024]{1,0:T(8,128)(2,1)S(1)}, bf16[384,1024]{1,0:T(8,128)(2,1)}, u32[]{:S(2)}, u32[]{:S(2)}) %collective-permute-start.2) | collective-permute-done | bytes 786464 | tf_op jit(solution)/shard_map/ppermute | solution.py:21
  103.4 2.6 %fusion.18 = f32[256,3,384]{2,0,1:T(8,128)S(1)} fusion(bf16[256,3,8192]{2,0,1:T(8,128)(2,1)} %all-gather.2.cloned.1.call-done, s32[]{:T(128)S(6)} %select_n.72, bf16[384,1024]{1,0:T(8,128)(2,1)} %collective-permute-done.2), kind=kOutput, calls=%fused_computation.21 | convolution fusion | flops 603979776 | bytes 3538948 | tf_op jit(solution)/shard_map/cgd,td->cgt/dot_general | solution.py:62
  106.0 0.0 copy-start.1
  106.0 0.0 collective-permute-done.3
  106.0 2.7 %fusion.16 = f32[256,3,384]{2,0,1:T(8,128)S(1)} fusion(bf16[256,3,8192]{2,0,1:T(8,128)(2,1)} %all-gather.2.cloned.1.call-done, s32[]{:T(128)S(6)} %select_n.73, bf16[384,1024]{1,0:T(8,128)(2,1)} %collective-permute-done.3), kind=kOutput, calls=%fused_computation.19 | convolution fusion | flops 603979776 | bytes 3538948 | tf_op jit(solution)/shard_map/cgd,td->cgt/dot_general | solution.py:62
  108.7 7.6 %collective-permute-done.5 = bf16[384,1024]{1,0:T(8,128)(2,1)} collective-permute-done((bf16[384,1024]{1,0:T(8,128)(2,1)}, bf16[384,1024]{1,0:T(8,128)(2,1)}, u32[]{:S(2)}, u32[]{:S(2)}) %collective-permute-start.5) | collective-permute-done | bytes 786464 | tf_op jit(solution)/shard_map/ppermute | solution.py:21
  116.3 2.6 %fusion.12 = f32[256,3,384]{2,0,1:T(8,128)S(1)} fusion(bf16[256,3,8192]{2,0,1:T(8,128)(2,1)} %all-gather.2.cloned.1.call-done, s32[]{:T(128)S(6)} %select_n.76, bf16[384,1024]{1,0:T(8,128)(2,1)} %collective-permute-done.5), kind=kOutput, calls=%fused_computation.15 | convolution fusion | flops 603979776 | bytes 3538948 | tf_op jit(solution)/shard_map/cgd,td->cgt/dot_general | solution.py:62
  119.0 1.8 fusion.7
  120.8 1.0 fusion.39
  121.8 0.0 copy-start.4
  121.8 0.0 collective-permute-done.4
  121.8 1.0 fusion.42
  122.9 0.1 slice.51
  123.0 2.1 collective-permute-start.6
  125.1 7.0 %collective-permute-done.6 = bf16[256,3,2]{2,0,1:T(8,128)(2,1)S(1)} collective-permute-done((bf16[256,3,2]{2,0,1:T(8,128)(2,1)S(1)}, bf16[256,3,2]{2,0,1:T(8,128)(2,1)S(1)}, u32[]{:S(2)}, u32[]{:S(2)}) %collective-permute-start.6) | collective-permute-done | bytes 3104 | tf_op jit(solution)/shard_map/ppermute | solution.py:10
  132.1 0.4 pad_maximum_fusion
  132.5 0.2 convert_element_type.29
  132.7 1.1 fusion.45
  133.9 0.0 copy-start.2
  133.9 0.0 copy-start.5
  133.9 4.0 %multiply_exponential_fusion = (f32[16,256,384]{2,1,0:T(8,128)}, f32[16,256]{1,0:T(8,128)S(1)}) fusion(f32[384]{0:T(512)S(1)} %get-tuple-element.14, f32[16,256]{1,0:T(8,128)S(1)} %neg.3, f32[256,384]{1,0:T(8,128)S(1)} %convert_element_type.32, f32[384]{0:T(512)S(1)} %get-tuple-element.15), kind=kLoop, calls=%fused_computation.1 | loop fusion | flops 6287360 | bytes 6720512 | tf_op jit(solution)/shard_map/exp | solution.py:95
  137.9 1.9 collective-permute-start.7
  139.8 5.2 %collective-permute-done.7 = f32[16,256]{1,0:T(8,128)S(1)} collective-permute-done((f32[16,256]{1,0:T(8,128)S(1)}, f32[16,256]{1,0:T(8,128)S(1)}, u32[]{:S(2)}, u32[]{:S(2)}) %collective-permute-start.7) | collective-permute-done | bytes 16416 | tf_op jit(solution)/shard_map/ppermute | solution.py:10
  145.1 1.9 collective-permute-start.8
  147.0 5.2 %collective-permute-done.8 = f32[16,256]{1,0:T(8,128)S(1)} collective-permute-done((f32[16,256]{1,0:T(8,128)S(1)}, f32[16,256]{1,0:T(8,128)S(1)}, u32[]{:S(2)}, u32[]{:S(2)}) %collective-permute-start.8) | collective-permute-done | bytes 16416 | tf_op jit(solution)/shard_map/ppermute | solution.py:10
  152.3 1.9 collective-permute-start.9
  154.2 5.8 %collective-permute-done.9 = f32[16,256]{1,0:T(8,128)S(1)} collective-permute-done((f32[16,256]{1,0:T(8,128)S(1)}, f32[16,256]{1,0:T(8,128)S(1)}, u32[]{:S(2)}, u32[]{:S(2)}) %collective-permute-start.9) | collective-permute-done | bytes 16416 | tf_op jit(solution)/shard_map/ppermute | solution.py:10
  160.0 1.9 collective-permute-start.10
  161.9 0.0 copy-done.2
  161.9 6.1 %collective-permute-done.10 = f32[16,256]{1,0:T(8,128)S(1)} collective-permute-done((f32[16,256]{1,0:T(8,128)S(1)}, f32[16,256]{1,0:T(8,128)S(1)}, u32[]{:S(2)}, u32[]{:S(2)}) %collective-permute-start.10) | collective-permute-done | bytes 16416 | tf_op jit(solution)/shard_map/ppermute | solution.py:10
  168.1 1.4 collective-permute-start.11
  169.5 4.3 %collective-permute-done.11 = f32[16,256]{1,0:T(8,128)S(1)} collective-permute-done((f32[16,256]{1,0:T(8,128)S(1)}, f32[16,256]{1,0:T(8,128)S(1)}, u32[]{:S(2)}, u32[]{:S(2)}) %collective-permute-start.11) | collective-permute-done | bytes 16416 | tf_op jit(solution)/shard_map/ppermute | solution.py:10
  173.8 1.3 collective-permute-start.12
  175.2 5.8 %collective-permute-done.12 = f32[16,256]{1,0:T(8,128)S(1)} collective-permute-done((f32[16,256]{1,0:T(8,128)S(1)}, f32[16,256]{1,0:T(8,128)S(1)}, u32[]{:S(2)}, u32[]{:S(2)}) %collective-permute-start.12) | collective-permute-done | bytes 16416 | tf_op jit(solution)/shard_map/ppermute | solution.py:10
  181.0 0.0 slice-start.1
  181.0 9.0 %multiply_reduce_fusion.2 = f32[256,384]{1,0:T(8,128)S(1)} fusion(f32[16,256]{1,0:T(8,128)S(1)} %neg.3, f32[16,256]{1,0:T(8,128)S(1)} %get-tuple-element.6, f32[256,384]{1,0:T(8,128)} %copy-done.2, f32[16,256]{1,0:T(8,128)S(1)} %copy-done.4), kind=kOutput, calls=%fused_computation.3 | convolution fusion | flops 7257243648 | bytes 835584 | tf_op jit(solution)/shard_map/mcs,st->mct/dot_general | solution.py:14
  190.0 0.0 copy-start.7
  190.0 0.0 copy-start
  190.0 0.8 multiply_reduce_fusion
  190.8 0.1 add_convert_fusion.1
  190.9 0.1 fusion.67
  191.0 2.2 %collective-permute-start.13 = (bf16[256,384]{1,0:T(8,128)(2,1)S(1)}, bf16[256,384]{1,0:T(8,128)(2,1)S(1)}, u32[]{:S(2)}, u32[]{:S(2)}) collective-permute-start(bf16[256,384]{1,0:T(8,128)(2,1)S(1)} %fusion.67), channel_id=1, source_target_pairs={{0,2},{2,4},{4,6},{6,0},{1,3},{3,5},{5,7},{7,1},{8,10},{10,12},{12... | collective-permute-start | bytes 589832 | tf_op jit(solution)/shard_map/ppermute | solution.py:21
  193.2 4.8 %collective-permute-start.14 = (bf16[256,384]{1,0:T(8,128)(2,1)S(1)}, bf16[256,384]{1,0:T(8,128)(2,1)S(1)}, u32[]{:S(2)}, u32[]{:S(2)}) collective-permute-start(bf16[256,384]{1,0:T(8,128)(2,1)S(1)} %fusion.67), channel_id=1, source_target_pairs={{0,4},{2,6},{4,0},{6,2},{1,5},{3,7},{5,1},{7,3},{8,12},{10,14},{12... | collective-permute-start | bytes 589832 | tf_op jit(solution)/shard_map/ppermute | solution.py:21
  198.0 1.5 collective-permute-start.15
  199.4 0.0 copy-done
  199.4 0.6 fusion.55
  200.0 1.8 collective-permute-done.13
  201.8 0.6 fusion.53
  202.4 4.1 %collective-permute-done.14 = bf16[256,384]{1,0:T(8,128)(2,1)S(1)} collective-permute-done((bf16[256,384]{1,0:T(8,128)(2,1)S(1)}, bf16[256,384]{1,0:T(8,128)(2,1)S(1)}, u32[]{:S(2)}, u32[]{:S(2)}) %collective-permute-start.14) | collective-permute-done | bytes 196640 | tf_op jit(solution)/shard_map/ppermute | solution.py:21
  206.5 0.6 fusion.51
  207.1 0.5 collective-permute-done.15
  207.6 1.8 add_convert_fusion
  (23 shorter events, 0.2 us)
Async XLA Ops:
  6.5 12.8 %copy-start.6 = (f32[3,3,256]{2,1,0:T(4,128)S(1)}, f32[3,3,256]{2,1,0:T(4,128)}, u32[]{:S(2)}) copy-start(f32[3,3,256]{2,1,0:T(4,128)} %param.9) | copy-start | bytes 27652
  6.5 79.6 %all-gather.2.cloned.1.call-start = ((), (), s32[]{:S(2)}) async-start(), calls=%async_computation | async-start | bytes 12976128 | tf_op jit(solution)/shard_map/all_gather | solution.py:54
  8.8 53.2 %collective-permute-start.1 = (bf16[384,1024]{1,0:T(8,128)(2,1)S(1)}, bf16[384,1024]{1,0:T(8,128)(2,1)}, u32[]{:S(2)}, u32[]{:S(2)}) collective-permute-start(bf16[384,1024]{1,0:T(8,128)(2,1)S(1)} %get-tuple-element.8), channel_id=1, source_target_pairs={{0,6},{2,0},{4,2},{6,4},{1,7},{3,1},{5,3},{7,5},{8,14},{10,8},{12,... | collective-permute-start | bytes 2359304 | tf_op jit(solution)/shard_map/ppermute | solution.py:21
  15.1 51.7 %collective-permute-start = (bf16[384,1024]{1,0:T(8,128)(2,1)S(1)}, bf16[384,1024]{1,0:T(8,128)(2,1)S(1)}, u32[]{:S(2)}, u32[]{:S(2)}) collective-permute-start(bf16[384,1024]{1,0:T(8,128)(2,1)S(1)} %get-tuple-element.7), channel_id=1, source_target_pairs={{0,2},{2,4},{4,6},{6,0},{1,3},{3,5},{5,7},{7,1},{8,10},{10,12},{12... | collective-permute-start | bytes 2359304 | tf_op jit(solution)/shard_map/ppermute | solution.py:21
  15.1 88.2 %collective-permute-start.2 = (bf16[384,1024]{1,0:T(8,128)(2,1)S(1)}, bf16[384,1024]{1,0:T(8,128)(2,1)}, u32[]{:S(2)}, u32[]{:S(2)}) collective-permute-start(bf16[384,1024]{1,0:T(8,128)(2,1)S(1)} %get-tuple-element.8), channel_id=1, source_target_pairs={{0,2},{2,4},{4,6},{6,0},{1,3},{3,5},{5,7},{7,1},{8,10},{10,12},{12... | collective-permute-start | bytes 2359304 | tf_op jit(solution)/shard_map/ppermute | solution.py:21
  16.7 89.3 %collective-permute-start.3 = (bf16[384,1024]{1,0:T(8,128)(2,1)S(1)}, bf16[384,1024]{1,0:T(8,128)(2,1)}, u32[]{:S(2)}, u32[]{:S(2)}) collective-permute-start(bf16[384,1024]{1,0:T(8,128)(2,1)S(1)} %get-tuple-element.7), channel_id=1, source_target_pairs={{0,6},{2,0},{4,2},{6,4},{1,7},{3,1},{5,3},{7,5},{8,14},{10,8},{12,... | collective-permute-start | bytes 2359304 | tf_op jit(solution)/shard_map/ppermute | solution.py:21
  62.0 54.4 %collective-permute-start.5 = (bf16[384,1024]{1,0:T(8,128)(2,1)}, bf16[384,1024]{1,0:T(8,128)(2,1)}, u32[]{:S(2)}, u32[]{:S(2)}) collective-permute-start(bf16[384,1024]{1,0:T(8,128)(2,1)} %collective-permute-done.1), channel_id=1, source_target_pairs={{0,6},{2,0},{4,2},{6,4},{1,7},{3,1},{5,3},{7,5},{8,14},{10,8},{12,... | collective-permute-start | bytes 2359304 | tf_op jit(solution)/shard_map/ppermute | solution.py:21
  66.8 55.0 %collective-permute-start.4 = (bf16[384,1024]{1,0:T(8,128)(2,1)S(1)}, bf16[384,1024]{1,0:T(8,128)(2,1)S(1)}, u32[]{:S(2)}, u32[]{:S(2)}) collective-permute-start(bf16[384,1024]{1,0:T(8,128)(2,1)S(1)} %collective-permute-done), channel_id=1, source_target_pairs={{0,2},{2,4},{4,6},{6,0},{1,3},{3,5},{5,7},{7,1},{8,10},{10,12},{12... | collective-permute-start | bytes 2359304 | tf_op jit(solution)/shard_map/ppermute | solution.py:21
  86.1 32.8 %copy-start.3 = (bf16[256,3,8192]{2,0,1:T(8,128)(2,1)S(1)}, bf16[256,3,8192]{2,0,1:T(8,128)(2,1)}, u32[]{:S(2)}) copy-start(bf16[256,3,8192]{2,0,1:T(8,128)(2,1)} %all-gather.2.cloned.1.call-done) | copy-start | bytes 37748740
  106.0 13.0 %copy-start.1 = (bf16[384,2048]{1,0:T(8,128)(2,1)S(1)}, bf16[384,2048]{1,0:T(8,128)(2,1)}, u32[]{:S(2)}) copy-start(bf16[384,2048]{1,0:T(8,128)(2,1)} %param.7) | copy-start | bytes 4718596
  121.8 3.3 %copy-start.4 = (f32[16,256]{1,0:T(8,128)S(1)}, f32[16,256]{1,0:T(8,128)}, u32[]{:S(2)}) copy-start(f32[16,256]{1,0:T(8,128)} %param.10) | copy-start | bytes 49156
  123.0 9.1 %collective-permute-start.6 = (bf16[256,3,2]{2,0,1:T(8,128)(2,1)S(1)}, bf16[256,3,2]{2,0,1:T(8,128)(2,1)S(1)}, u32[]{:S(2)}, u32[]{:S(2)}) collective-permute-start(bf16[256,3,2]{2,0,1:T(8,128)(2,1)S(1)} %slice.51), channel_id=1, source_target_pairs={{0,8},{8,16},{16,24},{24,32},{32,40},{40,48},{48,56},{56,64},{64,7... | collective-permute-start | bytes 9224 | tf_op jit(solution)/shard_map/ppermute | solution.py:10
  133.9 28.1 %copy-start.2 = (f32[256,384]{1,0:T(8,128)}, f32[256,384]{1,0:T(8,128)S(1)}, u32[]{:S(2)}) copy-start(f32[256,384]{1,0:T(8,128)S(1)} %convert_element_type.32) | copy-start | bytes 1179652
  133.9 47.1 %copy-start.5 = (f32[16,256]{1,0:T(8,128)S(1)}, f32[16,256]{1,0:T(8,128)}, u32[]{:S(2)}) copy-start(f32[16,256]{1,0:T(8,128)} %param.11) | copy-start | bytes 49156
  137.9 7.2 %collective-permute-start.7 = (f32[16,256]{1,0:T(8,128)S(1)}, f32[16,256]{1,0:T(8,128)S(1)}, u32[]{:S(2)}, u32[]{:S(2)}) collective-permute-start(f32[16,256]{1,0:T(8,128)S(1)} %get-tuple-element.10), channel_id=1, source_target_pairs={{0,8},{8,16},{16,24},{24,32},{32,40},{40,48},{48,56},{56,64},{64,7... | collective-permute-start | bytes 49160 | tf_op jit(solution)/shard_map/ppermute | solution.py:10
  145.1 7.2 %collective-permute-start.8 = (f32[16,256]{1,0:T(8,128)S(1)}, f32[16,256]{1,0:T(8,128)S(1)}, u32[]{:S(2)}, u32[]{:S(2)}) collective-permute-start(f32[16,256]{1,0:T(8,128)S(1)} %collective-permute-done.7), channel_id=1, source_target_pairs={{0,8},{8,16},{16,24},{24,32},{32,40},{40,48},{48,56},{56,64},{64,7... | collective-permute-start | bytes 49160 | tf_op jit(solution)/shard_map/ppermute | solution.py:10
  152.3 7.7 %collective-permute-start.9 = (f32[16,256]{1,0:T(8,128)S(1)}, f32[16,256]{1,0:T(8,128)S(1)}, u32[]{:S(2)}, u32[]{:S(2)}) collective-permute-start(f32[16,256]{1,0:T(8,128)S(1)} %multiply_add_fusion.3), channel_id=1, source_target_pairs={{0,16},{8,24},{16,32},{24,40},{32,48},{40,56},{48,64},{56,72},{64,... | collective-permute-start | bytes 49160 | tf_op jit(solution)/shard_map/ppermute | solution.py:10
  160.0 8.0 %collective-permute-start.10 = (f32[16,256]{1,0:T(8,128)S(1)}, f32[16,256]{1,0:T(8,128)S(1)}, u32[]{:S(2)}, u32[]{:S(2)}) collective-permute-start(f32[16,256]{1,0:T(8,128)S(1)} %multiply_add_fusion.2), channel_id=1, source_target_pairs={{0,32},{8,40},{16,48},{24,56},{32,64},{40,72},{48,80},{56,88},{64,... | collective-permute-start | bytes 49160 | tf_op jit(solution)/shard_map/ppermute | solution.py:10
  168.0 21.9 %slice-start = ((s8[6291456]{0:T(1024)(128)(4,1)}), s8[2097152]{0:T(1024)(128)(4,1)S(1)}, s32[]{:S(2)}) async-start(s8[6291456]{0:T(1024)(128)(4,1)} %bitcast.43), calls=%async_computation.1 | async-start | bytes 4194304
  168.1 5.8 %collective-permute-start.11 = (f32[16,256]{1,0:T(8,128)S(1)}, f32[16,256]{1,0:T(8,128)S(1)}, u32[]{:S(2)}, u32[]{:S(2)}) collective-permute-start(f32[16,256]{1,0:T(8,128)S(1)} %multiply_add_fusion.1), channel_id=1, source_target_pairs={{0,64},{8,72},{16,80},{24,88},{32,96},{40,104},{48,112},{56,120},{... | collective-permute-start | bytes 49160 | tf_op jit(solution)/shard_map/ppermute | solution.py:10
  173.8 7.1 %collective-permute-start.12 = (f32[16,256]{1,0:T(8,128)S(1)}, f32[16,256]{1,0:T(8,128)S(1)}, u32[]{:S(2)}, u32[]{:S(2)}) collective-permute-start(f32[16,256]{1,0:T(8,128)S(1)} %multiply_add_fusion), channel_id=1, source_target_pairs={{0,128},{8,136},{16,144},{24,152},{32,160},{40,168},{48,176},{56,1... | collective-permute-start | bytes 49160 | tf_op jit(solution)/shard_map/ppermute | solution.py:10
  181.0 9.0 %slice-start.1 = ((s8[6291456]{0:T(1024)(128)(4,1)}), s8[4194304]{0:T(1024)(128)(4,1)S(1)}, s32[]{:S(2)}) async-start(s8[6291456]{0:T(1024)(128)(4,1)} %bitcast.43), calls=%async_computation.2 | async-start | bytes 8388608
  190.0 0.8 copy-start.7
  190.0 9.4 %copy-start = (bf16[1024,2048]{1,0:T(8,128)(2,1)S(1)}, bf16[1024,2048]{1,0:T(8,128)(2,1)}, u32[]{:S(2)}) copy-start(bf16[1024,2048]{1,0:T(8,128)(2,1)} %param.13) | copy-start | bytes 12582916
  191.0 10.9 %collective-permute-start.13 = (bf16[256,384]{1,0:T(8,128)(2,1)S(1)}, bf16[256,384]{1,0:T(8,128)(2,1)S(1)}, u32[]{:S(2)}, u32[]{:S(2)}) collective-permute-start(bf16[256,384]{1,0:T(8,128)(2,1)S(1)} %fusion.67), channel_id=1, source_target_pairs={{0,2},{2,4},{4,6},{6,0},{1,3},{3,5},{5,7},{7,1},{8,10},{10,12},{12... | collective-permute-start | bytes 589832 | tf_op jit(solution)/shard_map/ppermute | solution.py:21
  193.2 13.3 %collective-permute-start.14 = (bf16[256,384]{1,0:T(8,128)(2,1)S(1)}, bf16[256,384]{1,0:T(8,128)(2,1)S(1)}, u32[]{:S(2)}, u32[]{:S(2)}) collective-permute-start(bf16[256,384]{1,0:T(8,128)(2,1)S(1)} %fusion.67), channel_id=1, source_target_pairs={{0,4},{2,6},{4,0},{6,2},{1,5},{3,7},{5,1},{7,3},{8,12},{10,14},{12... | collective-permute-start | bytes 589832 | tf_op jit(solution)/shard_map/ppermute | solution.py:21
  198.0 9.6 %collective-permute-start.15 = (bf16[256,384]{1,0:T(8,128)(2,1)S(1)}, bf16[256,384]{1,0:T(8,128)(2,1)S(1)}, u32[]{:S(2)}, u32[]{:S(2)}) collective-permute-start(bf16[256,384]{1,0:T(8,128)(2,1)S(1)} %fusion.67), channel_id=1, source_target_pairs={{0,6},{2,0},{4,2},{6,4},{1,7},{3,1},{5,3},{7,5},{8,14},{10,8},{12,... | collective-permute-start | bytes 589832 | tf_op jit(solution)/shard_map/ppermute | solution.py:21
Sparse Core Ops, SparseCore 0:
  9.8 76.2 all-gather.1

commit v6 on v4

--- a/solution.py
+++ b/solution.py
@@ -79,10 +79,15 @@
     z_f = lax.optimization_barrier(zprod).astype(jnp.float32)
     gains = residue * jnp.sqrt(decay)
     tau = jnp.arange(tok_rows, dtype=jnp.float32)
-    grow = jnp.exp(decay[:, :, None] * tau)
-    fall = jnp.exp(-decay[:, :, None] * tau)
-    upper = (tau[:, None] <= tau[None, :]).astype(jnp.float32)
-    tail = jnp.exp(-decay[:, :, None] * (tok_rows - 1.0 - tau))
+    grow, fall, tail, onward = lax.optimization_barrier(
+        (
+            jnp.exp(decay[:, :, None] * tau),
+            jnp.exp(-decay[:, :, None] * tau),
+            jnp.exp(-decay[:, :, None] * (tok_rows - 1.0 - tau)),
+            jnp.exp(-decay[:, :, None] * (tau + 1.0)),
+        )
+    )
+    upper = (tau[:, None] <= tau[None, :]).astype(jnp.bfloat16)
     ending = jnp.sum(tail * z_f[None], axis=2)
     states = lax.all_to_all(
         jnp.broadcast_to(ending[None], (seq_count,) + ending.shape),
@@ -99,10 +104,14 @@
         0.0,
     )
     incoming = jnp.sum(carry * states, axis=0)
-    prefix = hidot("mcs,st->mct", grow * z_f[None], upper)
+    lifted = grow * z_f[None]
+    prefix = jnp.zeros_like(lifted)
+    for _ in range(3):
+        part = lifted.astype(jnp.bfloat16)
+        prefix = prefix + jnp.einsum("mcs,st->mct", part, upper, preferred_element_type=jnp.float32)
+        lifted = lifted - part.astype(jnp.float32)
     intra = fall * prefix
     near = jnp.sum(gains[:, :, None] * intra, axis=0)
-    onward = lax.optimization_barrier(jnp.exp(-decay[:, :, None] * (tau + 1.0)))
     conv = near + jnp.sum((gains * incoming)[:, :, None] * onward, axis=0)
     longc = (conv + skip[:, None] * z_f).astype(jnp.bfloat16)
     long_f = lax.optimization_barrier(longc).astype(jnp.float32)
@@ -111,7 +120,10 @@
         index = (chan_rank - step) % chan_count
         return lax.dynamic_slice_in_dim(w_out, index * ch_dev, ch_dev, axis=0)
 
-    shifts = [step if step <= chan_count // 2 else step - chan_count for step in range(1, chan_count)]
+    shifts = sorted(
+        [step if step <= chan_count // 2 else step - chan_count for step in range(1, chan_count)],
+        key=lambda step: -abs(step),
+    )
     arrived = [(step, ring_shift(gated, "chan", step)) for step in shifts]
     mixed = jnp.einsum("ct,ce->te", gated, rows_of(0), preferred_element_type=jnp.float32)
     for step, piece in arrived:

time: 200 us -> 208 us (1.040)
  waiting for transfers between devices: 112 us -> 92.1 us
  matrix products: 26.5 us -> 39.8 us
  other arithmetic: 6.86 us -> 18.1 us
  local copies, waits for them, and re-layouts: 2.51 us -> 4.76 us
    all_gather x1, waiting for transfers between devices: 23.7 us -> 1.01 us  [on_device(): w_full = lax.all_gather(w_in, 'seq', axis=2, tiled=True)]
    ppermute x9, waiting for transfers between devices: 73.3 us -> 87.9 us  [ring_shift(): lax.ppermute(value, axis, [(source, (source + steps) % count) for source...]
    dot_general x1 -> x3, matrix products: 7.86 us -> 20.9 us  [on_device(): jnp.einsum('mcs,st->mct', part, upper, preferred_element_type=jnp.float32)]
    all_to_all x1, waiting for transfers between devices: 11.5 us -> 0.01 us  [on_device(): lax.all_to_all(jnp.broadcast_to(ending[None], (seq_count,) + ending.shape...]
    exp x1 -> x2, other arithmetic: 3.99 us -> 11 us  [the longest x1 7.87 us: on_device(): jnp.exp(-decay[:, :, None] * (tau + 1.0))]
    reduce_sum x1, other arithmetic: 0.74 us -> 3.38 us  [on_device(): conv = near + jnp.sum((gains * incoming)[:, :, None] * onward, axis=0)]
    unnamed x18 -> x26, local copies, waits for them, and re-layouts: 0.05 us -> 2.3 us
  transfers between devices with their start and end apart: 12 -> 12, of which waited for: 9 -> 6; matrix products, arithmetic and copies ran while one was open for 9% -> 20% of each run, Pallas kernels for 0% -> 0%
where the time goes in v6:
time: 208 us; the launch traced here: 206 us
  waiting for transfers between devices  92.1 us (44%)
  matrix products  39.8 us (19%)
  starting transfers between devices  37.6 us (18%)
  other arithmetic  18.1 us (9%)
  between operations  13.7 us (7%)
  local copies, waits for them, and re-layouts  4.76 us (2%)
    ppermute x9, waiting for transfers between devices, ring_shift(): lax.ppermute(value, axis, [(source, (source + steps) % count) for source...  87.9 us
    ppermute x9, starting transfers between devices, ring_shift(): lax.ppermute(value, axis, [(source, (source + steps) % count) for source...  23.9 us
    dot_general x3, matrix products, on_device(): jnp.einsum('mcs,st->mct', part, upper, preferred_element_type=jnp.float32)  20.9 us
    dot_general x6, matrix products, on_device(): jnp.einsum('cgd,td->cgt', block_of(step, lo, hi), piece, preferred_elemen...  13.4 us
    all_to_all x1, starting transfers between devices, on_device(): lax.all_to_all(jnp.broadcast_to(ending[None], (seq_count,) + ending.shape...  8.53 us
    exp x1, other arithmetic, on_device(): jnp.exp(-decay[:, :, None] * (tau + 1.0))  7.87 us
    ppermute x1, starting transfers between devices, from_behind(): lax.ppermute(value, axis, [(source, source + steps) for source in range(l...  5.2 us
  transfers between devices with their start and end apart: 12, of which 6 were waited for; matrix products, arithmetic and copies ran while one was open for 20% of the time, Pallas kernels for 0%

profile of v6, /device:TPU:1, one launch (start us, length us, event | category | flops | bytes accessed | tf_op | source)
XLA Modules:
  0.0 206.1 jit_solution(11256895527227681830)
XLA Ops:
  6.5 0.0 all-gather.2.cloned.1.call-start
  6.5 0.7 all-gather.2.cloned.1.call-update
  7.3 1.5 fusion.84
  8.8 6.9 %collective-permute-start.3 = (bf16[384,1024]{1,0:T(8,128)(2,1)S(1)}, bf16[384,1024]{1,0:T(8,128)(2,1)}, u32[]{:S(2)}, u32[]{:S(2)}) collective-permute-start(bf16[384,1024]{1,0:T(8,128)(2,1)S(1)} %get-tuple-element.15), channel_id=1, source_target_pairs={{0,6},{2,0},{4,2},{6,4},{1,7},{3,1},{5,3},{7,5},{8,14},{10,8},{12,... | collective-permute-start | bytes 2359304 | tf_op jit(solution)/shard_map/ppermute | solution.py:21
  15.7 0.0 collective-permute-start
  15.7 1.3 collective-permute-start.2
  16.9 2.3 %collective-permute-start.1 = (bf16[384,1024]{1,0:T(8,128)(2,1)S(1)}, bf16[384,1024]{1,0:T(8,128)(2,1)}, u32[]{:S(2)}, u32[]{:S(2)}) collective-permute-start(bf16[384,1024]{1,0:T(8,128)(2,1)S(1)} %get-tuple-element.16), channel_id=1, source_target_pairs={{0,6},{2,0},{4,2},{6,4},{1,7},{3,1},{5,3},{7,5},{8,14},{10,8},{12,... | collective-permute-start | bytes 2359304 | tf_op jit(solution)/shard_map/ppermute | solution.py:21
  19.3 0.0 copy-done.5
  19.3 7.9 %multiply_exponential_fusion = (f32[16,256,384]{2,1,0:T(8,128)}, f32[16,256,384]{2,1,0:T(8,128)}, f32[16,256,384]{2,1,0:T(8,128)}) fusion(f32[384]{0:T(512)S(1)} %get-tuple-element.23, f32[16,256]{1,0:T(8,128)S(1)} %neg.8, f32[384]{0:T(512)S(1)} %get-tuple-element.24), kind=kLoop, calls=%fused_computation.5 | loop fusion | flops 4718592 | bytes 18893824 | tf_op jit(solution)/shard_map/exp | solution.py:87
  27.1 3.1 %multiply_exponential_fusion.3 = f32[16,256,384]{2,1,0:T(8,128)} fusion(f32[16,256]{1,0:T(8,128)S(1)} %copy-done.5), kind=kLoop, calls=%fused_computation.8 | loop fusion | flops 1572864 | bytes 6307840 | tf_op jit(solution)/shard_map/exp | solution.py:84
  30.3 0.0 copy-done.7
  30.3 10.7 %collective-permute-done = bf16[384,1024]{1,0:T(8,128)(2,1)S(1)} collective-permute-done((bf16[384,1024]{1,0:T(8,128)(2,1)S(1)}, bf16[384,1024]{1,0:T(8,128)(2,1)S(1)}, u32[]{:S(2)}, u32[]{:S(2)}) %collective-permute-start) | collective-permute-done | bytes 786464 | tf_op jit(solution)/shard_map/ppermute | solution.py:21
  41.0 0.0 collective-permute-start.4
  41.0 39.5 %collective-permute-done.1 = bf16[384,1024]{1,0:T(8,128)(2,1)} collective-permute-done((bf16[384,1024]{1,0:T(8,128)(2,1)S(1)}, bf16[384,1024]{1,0:T(8,128)(2,1)}, u32[]{:S(2)}, u32[]{:S(2)}) %collective-permute-start.1) | collective-permute-done | bytes 786464 | tf_op jit(solution)/shard_map/ppermute | solution.py:21
  80.5 6.8 %collective-permute-start.5 = (bf16[384,1024]{1,0:T(8,128)(2,1)}, bf16[384,1024]{1,0:T(8,128)(2,1)}, u32[]{:S(2)}, u32[]{:S(2)}) collective-permute-start(bf16[384,1024]{1,0:T(8,128)(2,1)} %collective-permute-done.1), channel_id=1, source_target_pairs={{0,6},{2,0},{4,2},{6,4},{1,7},{3,1},{5,3},{7,5},{8,14},{10,8},{12,... | collective-permute-start | bytes 2359304 | tf_op jit(solution)/shard_map/ppermute | solution.py:21
  87.3 1.0 all-gather.2.cloned.1.call-done
  88.3 2.8 %fusion.21 = f32[256,3,384]{2,0,1:T(8,128)S(1)} fusion(bf16[256,3,8192]{2,0,1:T(8,128)(2,1)} %all-gather.2.cloned.1.call-done, s32[]{:T(128)S(6)} %select_n.75, bf16[384,1024]{1,0:T(8,128)(2,1)} %collective-permute-done.1), kind=kOutput, calls=%fused_computation.29 | convolution fusion | flops 603979776 | bytes 3538948 | tf_op jit(solution)/shard_map/cgd,td->cgt/dot_general | solution.py:62
  91.1 0.0 collective-permute-done.3
  91.1 3.2 %fusion.17 = f32[256,3,384]{2,0,1:T(8,128)S(1)} fusion(bf16[256,3,8192]{2,0,1:T(8,128)(2,1)} %all-gather.2.cloned.1.call-done, s32[]{:T(128)S(6)} %select_n.77, bf16[384,1024]{1,0:T(8,128)(2,1)} %collective-permute-done.3), kind=kOutput, calls=%fused_computation.25 | convolution fusion | flops 603979776 | bytes 3538948 | tf_op jit(solution)/shard_map/cgd,td->cgt/dot_general | solution.py:62
  94.3 0.0 copy-start.3
  94.3 0.0 collective-permute-done.2
  94.3 2.7 %fusion.19 = f32[256,3,384]{2,0,1:T(8,128)S(1)} fusion(bf16[256,3,8192]{2,0,1:T(8,128)(2,1)} %all-gather.2.cloned.1.call-done, s32[]{:T(128)S(6)} %select_n.76, bf16[384,1024]{1,0:T(8,128)(2,1)} %collective-permute-done.2), kind=kOutput, calls=%fused_computation.27 | convolution fusion | flops 603979776 | bytes 3538948 | tf_op jit(solution)/shard_map/cgd,td->cgt/dot_general | solution.py:62
  97.1 23.1 %collective-permute-done.5 = bf16[384,1024]{1,0:T(8,128)(2,1)} collective-permute-done((bf16[384,1024]{1,0:T(8,128)(2,1)}, bf16[384,1024]{1,0:T(8,128)(2,1)}, u32[]{:S(2)}, u32[]{:S(2)}) %collective-permute-start.5) | collective-permute-done | bytes 786464 | tf_op jit(solution)/shard_map/ppermute | solution.py:21
  120.1 2.6 %fusion.13 = f32[256,3,384]{2,0,1:T(8,128)S(1)} fusion(bf16[256,3,8192]{2,0,1:T(8,128)(2,1)} %all-gather.2.cloned.1.call-done, s32[]{:T(128)S(6)} %select_n.80, bf16[384,1024]{1,0:T(8,128)(2,1)} %collective-permute-done.5), kind=kOutput, calls=%fused_computation.21 | convolution fusion | flops 603979776 | bytes 3538948 | tf_op jit(solution)/shard_map/cgd,td->cgt/dot_general | solution.py:62
  122.8 1.8 fusion.8
  124.6 1.0 fusion.40
  125.6 0.0 collective-permute-done.4
  125.6 0.0 slice-start.2
  125.6 1.0 fusion.43
  126.7 0.1 slice.51
  126.8 5.2 %collective-permute-start.6 = (bf16[256,3,2]{2,0,1:T(8,128)(2,1)S(1)}, bf16[256,3,2]{2,0,1:T(8,128)(2,1)S(1)}, u32[]{:S(2)}, u32[]{:S(2)}) collective-permute-start(bf16[256,3,2]{2,0,1:T(8,128)(2,1)S(1)} %slice.51), channel_id=1, source_target_pairs={{0,8},{8,16},{16,24},{24,32},{32,40},{40,48},{48,56},{56,64},{64,7... | collective-permute-start | bytes 9224 | tf_op jit(solution)/shard_map/ppermute | solution.py:10
  132.1 2.5 %collective-permute-done.6 = bf16[256,3,2]{2,0,1:T(8,128)(2,1)S(1)} collective-permute-done((bf16[256,3,2]{2,0,1:T(8,128)(2,1)S(1)}, bf16[256,3,2]{2,0,1:T(8,128)(2,1)S(1)}, u32[]{:S(2)}, u32[]{:S(2)}) %collective-permute-start.6) | collective-permute-done | bytes 3104 | tf_op jit(solution)/shard_map/ppermute | solution.py:10
  134.6 0.4 pad_maximum_fusion
  135.0 0.0 slice-start.3
  135.0 0.2 convert_element_type.51
  135.2 1.1 fusion.46
  136.3 0.0 copy-start.1
  136.3 1.0 copy-done.1
  137.4 0.0 slice-done.2
  137.4 0.0 slice-done.3
  137.4 0.6 multiply_reduce_fusion.1
  138.0 0.8 broadcast_in_dim.12
  138.9 8.5 %all-to-all-start = ((f32[32,16,256]{2,1,0:T(8,128)}), f32[32,16,256]{2,1,0:T(8,128)S(1)}, u32[]{:S(2)}, u32[]{:S(2)}) async-start(f32[32,16,256]{2,1,0:T(8,128)} %broadcast_in_dim.12), calls=%async_computation | async-start | bytes 1048576 | tf_op jit(solution)/shard_map/all_to_all | solution.py:92
  147.4 0.0 slice-start.1
  147.4 7.7 %fusion.4 = f32[16,256,384]{2,1,0:T(8,128)} fusion(f32[16,256,384]{2,1,0:T(8,128)} %multiply_exponential_fusion.3, f32[256,384]{1,0:T(8,128)S(1)} %convert_element_type.54), kind=kOutput, calls=%fused_computation.13 | convolution fusion | flops 1220689920 | bytes 12976128 | tf_op jit(solution)/shard_map/mcs,st->mct/dot_general | solution.py:111
  155.1 0.0 slice-done.1
  155.2 4.8 %fusion = f32[16,256,384]{2,1,0:T(8,128)} fusion(f32[16,256,384]{2,1,0:T(8,128)S(1)} %bitcast.46, f32[256,384]{1,0:T(8,128)S(1)} %convert_element_type.54), kind=kOutput, calls=%fused_computation.10 | convolution fusion | flops 1211252736 | bytes 12976128 | tf_op jit(solution)/shard_map/mcs,st->mct/dot_general | solution.py:111
  160.0 0.0 all-to-all-done
  160.0 0.2 multiply_reduce_fusion.3
  160.2 3.4 %multiply_reduce_fusion = f32[256,384]{1,0:T(8,128)S(1)} fusion(f32[16,256,384]{2,1,0:T(8,128)} %get-tuple-element.12, f32[16,256]{1,0:T(8,128)S(1)} %get-tuple-element.13), kind=kLoop, calls=%fused_computation | loop fusion | flops 3047424 | bytes 6701056 | tf_op jit(solution)/shard_map/reduce_sum | solution.py:115
  163.6 1.2 copy-done
  164.8 8.4 %multiply_reduce_fusion.2 = f32[256,384]{1,0:T(8,128)S(1)} fusion(f32[16,256,384]{2,1,0:T(8,128)} %get-tuple-element.9, f32[16,256,384]{2,1,0:T(8,128)S(1)} %copy-done, f32[16,256,384]{2,1,0:T(8,128)} %fusion, f32[16,256]{1,0:T(8,128)S(1)} %get-tuple-element.14, f32[16,256,384]{2,1,0:T(8,128)} %multiply_exponential_fusion.3, ...), kind=kOutput, calls=%fused_computation.2 | convolution fusion | flops 1223737344 | bytes 25968640 | tf_op jit(solution)/shard_map/mcs,st->mct/dot_general | solution.py:111
  173.3 0.1 add_convert_fusion.1
  173.4 1.0 fusion.70
  174.5 4.4 %collective-permute-start.9 = (bf16[256,384]{1,0:T(8,128)(2,1)S(1)}, bf16[256,384]{1,0:T(8,128)(2,1)S(1)}, u32[]{:S(2)}, u32[]{:S(2)}) collective-permute-start(bf16[256,384]{1,0:T(8,128)(2,1)S(1)} %fusion.70), channel_id=1, source_target_pairs={{0,6},{2,0},{4,2},{6,4},{1,7},{3,1},{5,3},{7,5},{8,14},{10,8},{12,... | collective-permute-start | bytes 589832 | tf_op jit(solution)/shard_map/ppermute | solution.py:21
  178.8 0.0 collective-permute-start.8
  178.8 2.2 %collective-permute-start.7 = (bf16[256,384]{1,0:T(8,128)(2,1)S(1)}, bf16[256,384]{1,0:T(8,128)(2,1)S(1)}, u32[]{:S(2)}, u32[]{:S(2)}) collective-permute-start(bf16[256,384]{1,0:T(8,128)(2,1)S(1)} %fusion.70), channel_id=1, source_target_pairs={{0,4},{2,6},{4,0},{6,2},{1,5},{3,7},{5,1},{7,3},{8,12},{10,14},{12... | collective-permute-start | bytes 589832 | tf_op jit(solution)/shard_map/ppermute | solution.py:21
  181.0 0.6 fusion.56
  181.6 14.6 %collective-permute-done.7 = bf16[256,384]{1,0:T(8,128)(2,1)S(1)} collective-permute-done((bf16[256,384]{1,0:T(8,128)(2,1)S(1)}, bf16[256,384]{1,0:T(8,128)(2,1)S(1)}, u32[]{:S(2)}, u32[]{:S(2)}) %collective-permute-start.7) | collective-permute-done | bytes 196640 | tf_op jit(solution)/shard_map/ppermute | solution.py:21
  196.2 0.6 fusion.54
  196.8 0.0 collective-permute-done.8
  196.8 0.6 fusion.52
  197.4 0.0 collective-permute-done.9
  197.4 1.9 add_convert_fusion
  (24 shorter events, 0.1 us)
Async XLA Ops:
  6.5 12.7 %copy-start.5 = (f32[16,256]{1,0:T(8,128)S(1)}, f32[16,256]{1,0:T(8,128)}, u32[]{:S(2)}) copy-start(f32[16,256]{1,0:T(8,128)} %param.10) | copy-start | bytes 49156
  6.5 81.8 %all-gather.2.cloned.1.call-start = ((), (), s32[]{:S(2)}) async-start(), calls=%async_computation.1 | async-start | bytes 12976128 | tf_op jit(solution)/shard_map/all_gather | solution.py:54
  8.8 82.3 %collective-permute-start.3 = (bf16[384,1024]{1,0:T(8,128)(2,1)S(1)}, bf16[384,1024]{1,0:T(8,128)(2,1)}, u32[]{:S(2)}, u32[]{:S(2)}) collective-permute-start(bf16[384,1024]{1,0:T(8,128)(2,1)S(1)} %get-tuple-element.15), channel_id=1, source_target_pairs={{0,6},{2,0},{4,2},{6,4},{1,7},{3,1},{5,3},{7,5},{8,14},{10,8},{12,... | collective-permute-start | bytes 2359304 | tf_op jit(solution)/shard_map/ppermute | solution.py:21
  15.7 25.4 %collective-permute-start = (bf16[384,1024]{1,0:T(8,128)(2,1)S(1)}, bf16[384,1024]{1,0:T(8,128)(2,1)S(1)}, u32[]{:S(2)}, u32[]{:S(2)}) collective-permute-start(bf16[384,1024]{1,0:T(8,128)(2,1)S(1)} %get-tuple-element.15), channel_id=1, source_target_pairs={{0,2},{2,4},{4,6},{6,0},{1,3},{3,5},{5,7},{7,1},{8,10},{10,12},{12... | collective-permute-start | bytes 2359304 | tf_op jit(solution)/shard_map/ppermute | solution.py:21
  15.7 78.7 %collective-permute-start.2 = (bf16[384,1024]{1,0:T(8,128)(2,1)S(1)}, bf16[384,1024]{1,0:T(8,128)(2,1)}, u32[]{:S(2)}, u32[]{:S(2)}) collective-permute-start(bf16[384,1024]{1,0:T(8,128)(2,1)S(1)} %get-tuple-element.16), channel_id=1, source_target_pairs={{0,2},{2,4},{4,6},{6,0},{1,3},{3,5},{5,7},{7,1},{8,10},{10,12},{12... | collective-permute-start | bytes 2359304 | tf_op jit(solution)/shard_map/ppermute | solution.py:21
  16.9 63.6 %collective-permute-start.1 = (bf16[384,1024]{1,0:T(8,128)(2,1)S(1)}, bf16[384,1024]{1,0:T(8,128)(2,1)}, u32[]{:S(2)}, u32[]{:S(2)}) collective-permute-start(bf16[384,1024]{1,0:T(8,128)(2,1)S(1)} %get-tuple-element.16), channel_id=1, source_target_pairs={{0,6},{2,0},{4,2},{6,4},{1,7},{3,1},{5,3},{7,5},{8,14},{10,8},{12,... | collective-permute-start | bytes 2359304 | tf_op jit(solution)/shard_map/ppermute | solution.py:21
  27.1 3.1 %copy-start.7 = (f32[3,3,256]{2,1,0:T(4,128)S(1)}, f32[3,3,256]{2,1,0:T(4,128)}, u32[]{:S(2)}) copy-start(f32[3,3,256]{2,1,0:T(4,128)} %param.9) | copy-start | bytes 27652
  41.0 84.6 %collective-permute-start.4 = (bf16[384,1024]{1,0:T(8,128)(2,1)S(1)}, bf16[384,1024]{1,0:T(8,128)(2,1)S(1)}, u32[]{:S(2)}, u32[]{:S(2)}) collective-permute-start(bf16[384,1024]{1,0:T(8,128)(2,1)S(1)} %collective-permute-done), channel_id=1, source_target_pairs={{0,2},{2,4},{4,6},{6,0},{1,3},{3,5},{5,7},{7,1},{8,10},{10,12},{12... | collective-permute-start | bytes 2359304 | tf_op jit(solution)/shard_map/ppermute | solution.py:21
  80.5 39.6 %collective-permute-start.5 = (bf16[384,1024]{1,0:T(8,128)(2,1)}, bf16[384,1024]{1,0:T(8,128)(2,1)}, u32[]{:S(2)}, u32[]{:S(2)}) collective-permute-start(bf16[384,1024]{1,0:T(8,128)(2,1)} %collective-permute-done.1), channel_id=1, source_target_pairs={{0,6},{2,0},{4,2},{6,4},{1,7},{3,1},{5,3},{7,5},{8,14},{10,8},{12,... | collective-permute-start | bytes 2359304 | tf_op jit(solution)/shard_map/ppermute | solution.py:21
  88.3 34.5 %copy-start.4 = (bf16[256,3,8192]{2,0,1:T(8,128)(2,1)S(1)}, bf16[256,3,8192]{2,0,1:T(8,128)(2,1)}, u32[]{:S(2)}) copy-start(bf16[256,3,8192]{2,0,1:T(8,128)(2,1)} %all-gather.2.cloned.1.call-done) | copy-start | bytes 37748740
  94.3 28.5 %copy-start.3 = (bf16[384,2048]{1,0:T(8,128)(2,1)S(1)}, bf16[384,2048]{1,0:T(8,128)(2,1)}, u32[]{:S(2)}) copy-start(bf16[384,2048]{1,0:T(8,128)(2,1)} %param.7) | copy-start | bytes 4718596
  125.6 11.8 %slice-start.2 = ((s8[6291456]{0:T(1024)(128)(4,1)}), s8[2097152]{0:T(1024)(128)(4,1)S(1)}, s32[]{:S(2)}) async-start(s8[6291456]{0:T(1024)(128)(4,1)} %bitcast.47), calls=%async_computation.4 | async-start | bytes 4194304
  126.8 7.8 %collective-permute-start.6 = (bf16[256,3,2]{2,0,1:T(8,128)(2,1)S(1)}, bf16[256,3,2]{2,0,1:T(8,128)(2,1)S(1)}, u32[]{:S(2)}, u32[]{:S(2)}) collective-permute-start(bf16[256,3,2]{2,0,1:T(8,128)(2,1)S(1)} %slice.51), channel_id=1, source_target_pairs={{0,8},{8,16},{16,24},{24,32},{32,40},{40,48},{48,56},{56,64},{64,7... | collective-permute-start | bytes 9224 | tf_op jit(solution)/shard_map/ppermute | solution.py:10
  135.0 2.4 %slice-start.3 = ((s8[6291456]{0:T(1024)(128)(4,1)}), s8[4194304]{0:T(1024)(128)(4,1)S(1)}, s32[]{:S(2)}) async-start(s8[6291456]{0:T(1024)(128)(4,1)} %bitcast.47), calls=%async_computation.5 | async-start | bytes 8388608
  136.3 1.0 copy-start.1
  138.9 16.3 %slice-start = ((s8[6291456]{0:T(1024)(128)(4,1)}), s8[2097152]{0:T(1024)(128)(4,1)S(1)}, s32[]{:S(2)}) async-start(s8[6291456]{0:T(1024)(128)(4,1)} %bitcast.45), calls=%async_computation.2 | async-start | bytes 4194304
  138.9 21.1 %all-to-all-start = ((f32[32,16,256]{2,1,0:T(8,128)}), f32[32,16,256]{2,1,0:T(8,128)S(1)}, u32[]{:S(2)}, u32[]{:S(2)}) async-start(f32[32,16,256]{2,1,0:T(8,128)} %broadcast_in_dim.12), calls=%async_computation | async-start | bytes 1048576 | tf_op jit(solution)/shard_map/all_to_all | solution.py:92
  147.4 7.7 %slice-start.1 = ((s8[6291456]{0:T(1024)(128)(4,1)}), s8[4194304]{0:T(1024)(128)(4,1)S(1)}, s32[]{:S(2)}) async-start(s8[6291456]{0:T(1024)(128)(4,1)} %bitcast.45), calls=%async_computation.3 | async-start | bytes 8388608
  155.2 5.0 %copy-start.6 = (f32[16,256]{1,0:T(8,128)S(1)}, f32[16,256]{1,0:T(8,128)}, u32[]{:S(2)}) copy-start(f32[16,256]{1,0:T(8,128)} %param.11) | copy-start | bytes 49156
  160.2 4.6 %copy-start = (f32[16,256,384]{2,1,0:T(8,128)S(1)}, f32[16,256,384]{2,1,0:T(8,128)}, u32[]{:S(2)}) copy-start(f32[16,256,384]{2,1,0:T(8,128)} %fusion.4) | copy-start | bytes 18874372
  164.8 8.4 %copy-start.8 = (f32[256]{0:T(256)S(1)}, f32[256]{0:T(256)}, u32[]{:S(2)}) copy-start(f32[256]{0:T(256)} %param.12) | copy-start | bytes 3076
  164.8 16.2 %copy-start.2 = (bf16[1024,2048]{1,0:T(8,128)(2,1)S(1)}, bf16[1024,2048]{1,0:T(8,128)(2,1)}, u32[]{:S(2)}) copy-start(bf16[1024,2048]{1,0:T(8,128)(2,1)} %param.13) | copy-start | bytes 12582916
  174.5 22.9 %collective-permute-start.9 = (bf16[256,384]{1,0:T(8,128)(2,1)S(1)}, bf16[256,384]{1,0:T(8,128)(2,1)S(1)}, u32[]{:S(2)}, u32[]{:S(2)}) collective-permute-start(bf16[256,384]{1,0:T(8,128)(2,1)S(1)} %fusion.70), channel_id=1, source_target_pairs={{0,6},{2,0},{4,2},{6,4},{1,7},{3,1},{5,3},{7,5},{8,14},{10,8},{12,... | collective-permute-start | bytes 589832 | tf_op jit(solution)/shard_map/ppermute | solution.py:21
  178.8 17.9 %collective-permute-start.8 = (bf16[256,384]{1,0:T(8,128)(2,1)S(1)}, bf16[256,384]{1,0:T(8,128)(2,1)S(1)}, u32[]{:S(2)}, u32[]{:S(2)}) collective-permute-start(bf16[256,384]{1,0:T(8,128)(2,1)S(1)} %fusion.70), channel_id=1, source_target_pairs={{0,2},{2,4},{4,6},{6,0},{1,3},{3,5},{5,7},{7,1},{8,10},{10,12},{12... | collective-permute-start | bytes 589832 | tf_op jit(solution)/shard_map/ppermute | solution.py:21
  178.8 17.3 %collective-permute-start.7 = (bf16[256,384]{1,0:T(8,128)(2,1)S(1)}, bf16[256,384]{1,0:T(8,128)(2,1)S(1)}, u32[]{:S(2)}, u32[]{:S(2)}) collective-permute-start(bf16[256,384]{1,0:T(8,128)(2,1)S(1)} %fusion.70), channel_id=1, source_target_pairs={{0,4},{2,6},{4,0},{6,2},{1,5},{3,7},{5,1},{7,3},{8,12},{10,14},{12... | collective-permute-start | bytes 589832 | tf_op jit(solution)/shard_map/ppermute | solution.py:21
Sparse Core Ops, SparseCore 0:
  9.8 78.4 all-gather.1

commit v7 on v4

--- a/solution.py
+++ b/solution.py
@@ -8,12 +8,6 @@
     count = lax.axis_size(axis)
     leading, last = (max(0, -steps), min(count, count - steps))
     return lax.ppermute(value, axis, [(source, source + steps) for source in range(leading, last)])
-
-
-def hidot(form, left, right):
-    return jnp.einsum(
-        form, left, right, precision=lax.Precision.HIGHEST, preferred_element_type=jnp.float32
-    )
 
 
 def ring_shift(value, axis, steps):
@@ -99,7 +93,13 @@
         0.0,
     )
     incoming = jnp.sum(carry * states, axis=0)
-    prefix = hidot("mcs,st->mct", grow * z_f[None], upper)
+    prefix = jnp.einsum(
+        "mcs,st->mct",
+        grow * z_f[None],
+        upper,
+        precision=lax.Precision.HIGH,
+        preferred_element_type=jnp.float32,
+    )
     intra = fall * prefix
     near = jnp.sum(gains[:, :, None] * intra, axis=0)
     onward = lax.optimization_barrier(jnp.exp(-decay[:, :, None] * (tau + 1.0)))
@@ -111,7 +111,10 @@
         index = (chan_rank - step) % chan_count
         return lax.dynamic_slice_in_dim(w_out, index * ch_dev, ch_dev, axis=0)
 
-    shifts = [step if step <= chan_count // 2 else step - chan_count for step in range(1, chan_count)]
+    shifts = sorted(
+        [step if step <= chan_count // 2 else step - chan_count for step in range(1, chan_count)],
+        key=lambda step: -abs(step),
+    )
     arrived = [(step, ring_shift(gated, "chan", step)) for step in shifts]
     mixed = jnp.einsum("ct,ce->te", gated, rows_of(0), preferred_element_type=jnp.float32)
     for step, piece in arrived:

time: 200 us -> 196 us (0.980)
  matrix products: 26.5 us -> 24.3 us
  waiting for transfers between devices: 112 us -> 110 us
    dot_general x1, matrix products: 7.86 us -> 5.61 us  [on_device(): jnp.einsum('mcs,st->mct', grow * z_f[None], upper, precision=lax.Precisio...]
where the time goes in v7:
time: 196 us
  waiting for transfers between devices  110 us (56%)
  starting transfers between devices  38.1 us (19%)
  matrix products  24.3 us (12%)
  between operations  13.7 us (7%)
  other arithmetic  6.86 us (4%)
  local copies, waits for them, and re-layouts  2.51 us (1%)
    ppermute x9, waiting for transfers between devices, ring_shift(): lax.ppermute(value, axis, [(source, (source + steps) % count) for source...  72 us
    ppermute x9, starting transfers between devices, ring_shift(): lax.ppermute(value, axis, [(source, (source + steps) % count) for source...  24.1 us
    all_gather x1, waiting for transfers between devices, on_device(): w_full = lax.all_gather(w_in, 'seq', axis=2, tiled=True)  23.7 us
    dot_general x6, matrix products, on_device(): jnp.einsum('cgd,td->cgt', block_of(step, lo, hi), piece, preferred_elemen...  13.3 us
    all_to_all x1, waiting for transfers between devices, on_device(): lax.all_to_all(jnp.broadcast_to(ending[None], (seq_count,) + ending.shape...  11.5 us
    all_to_all x1, starting transfers between devices, on_device(): lax.all_to_all(jnp.broadcast_to(ending[None], (seq_count,) + ending.shape...  8.38 us
    dot_general x1, matrix products, on_device(): jnp.einsum('mcs,st->mct', grow * z_f[None], upper, precision=lax.Precisio...  5.61 us
    ppermute x1, starting transfers between devices, from_behind(): lax.ppermute(value, axis, [(source, source + steps) for source in range(l...  5.57 us
  transfers between devices with their start and end apart: 12, of which 9 were waited for; matrix products, arithmetic and copies ran while one was open for 9% of the time, Pallas kernels for 0%

profile of v7, /device:TPU:1, one launch (start us, length us, event | category | flops | bytes accessed | tf_op | source)
XLA Modules:
  0.0 195.7 jit_solution(13616717643876165242)
XLA Ops:
  6.5 0.0 copy-start.5
  6.5 0.0 all-gather.2.cloned.1.call-start
  6.5 0.7 all-gather.2.cloned.1.call-update
  7.3 1.5 fusion.81
  8.8 6.9 %collective-permute-start.1 = (bf16[384,1024]{1,0:T(8,128)(2,1)S(1)}, bf16[384,1024]{1,0:T(8,128)(2,1)}, u32[]{:S(2)}, u32[]{:S(2)}) collective-permute-start(bf16[384,1024]{1,0:T(8,128)(2,1)S(1)} %get-tuple-element.8), channel_id=1, source_target_pairs={{0,6},{2,0},{4,2},{6,4},{1,7},{3,1},{5,3},{7,5},{8,14},{10,8},{12,... | collective-permute-start | bytes 2359304 | tf_op jit(solution)/shard_map/ppermute | solution.py:15
  15.7 0.0 collective-permute-start
  15.7 1.3 collective-permute-start.2
  16.9 2.3 %collective-permute-start.3 = (bf16[384,1024]{1,0:T(8,128)(2,1)S(1)}, bf16[384,1024]{1,0:T(8,128)(2,1)}, u32[]{:S(2)}, u32[]{:S(2)}) collective-permute-start(bf16[384,1024]{1,0:T(8,128)(2,1)S(1)} %get-tuple-element.7), channel_id=1, source_target_pairs={{0,6},{2,0},{4,2},{6,4},{1,7},{3,1},{5,3},{7,5},{8,14},{10,8},{12,... | collective-permute-start | bytes 2359304 | tf_op jit(solution)/shard_map/ppermute | solution.py:15
  19.3 0.0 copy-done.5
  19.3 39.3 %collective-permute-done.1 = bf16[384,1024]{1,0:T(8,128)(2,1)} collective-permute-done((bf16[384,1024]{1,0:T(8,128)(2,1)S(1)}, bf16[384,1024]{1,0:T(8,128)(2,1)}, u32[]{:S(2)}, u32[]{:S(2)}) %collective-permute-start.1) | collective-permute-done | bytes 786464 | tf_op jit(solution)/shard_map/ppermute | solution.py:15
  58.6 6.0 %collective-permute-start.5 = (bf16[384,1024]{1,0:T(8,128)(2,1)}, bf16[384,1024]{1,0:T(8,128)(2,1)}, u32[]{:S(2)}, u32[]{:S(2)}) collective-permute-start(bf16[384,1024]{1,0:T(8,128)(2,1)} %collective-permute-done.1), channel_id=1, source_target_pairs={{0,6},{2,0},{4,2},{6,4},{1,7},{3,1},{5,3},{7,5},{8,14},{10,8},{12,... | collective-permute-start | bytes 2359304 | tf_op jit(solution)/shard_map/ppermute | solution.py:15
  64.6 0.0 collective-permute-done
  64.6 0.0 collective-permute-start.4
  64.6 23.7 %all-gather.2.cloned.1.call-done = bf16[256,3,8192]{2,0,1:T(8,128)(2,1)} async-done(((bf16[256,3,256]{2,0,1:T(8,128)(2,1)}), bf16[256,3,8192]{2,0,1:T(8,128)(2,1)}) %all-gather.2.cloned.1.call-update) | async-done | bytes 12582928 | tf_op jit(solution)/shard_map/all_gather | solution.py:48
  88.3 2.8 %fusion.20 = f32[256,3,384]{2,0,1:T(8,128)S(1)} fusion(bf16[256,3,8192]{2,0,1:T(8,128)(2,1)} %all-gather.2.cloned.1.call-done, s32[]{:T(128)S(6)} %select_n.75, bf16[384,1024]{1,0:T(8,128)(2,1)} %collective-permute-done.1), kind=kOutput, calls=%fused_computation.23 | convolution fusion | flops 603979776 | bytes 3538948 | tf_op jit(solution)/shard_map/cgd,td->cgt/dot_general | solution.py:56
  91.1 0.0 collective-permute-done.2
  91.1 3.2 %fusion.18 = f32[256,3,384]{2,0,1:T(8,128)S(1)} fusion(bf16[256,3,8192]{2,0,1:T(8,128)(2,1)} %all-gather.2.cloned.1.call-done, s32[]{:T(128)S(6)} %select_n.76, bf16[384,1024]{1,0:T(8,128)(2,1)} %collective-permute-done.2), kind=kOutput, calls=%fused_computation.21 | convolution fusion | flops 603979776 | bytes 3538948 | tf_op jit(solution)/shard_map/cgd,td->cgt/dot_general | solution.py:56
  94.3 0.0 copy-start.1
  94.3 3.1 %collective-permute-done.3 = bf16[384,1024]{1,0:T(8,128)(2,1)} collective-permute-done((bf16[384,1024]{1,0:T(8,128)(2,1)S(1)}, bf16[384,1024]{1,0:T(8,128)(2,1)}, u32[]{:S(2)}, u32[]{:S(2)}) %collective-permute-start.3) | collective-permute-done | bytes 786464 | tf_op jit(solution)/shard_map/ppermute | solution.py:15
  97.4 2.6 %fusion.16 = f32[256,3,384]{2,0,1:T(8,128)S(1)} fusion(bf16[256,3,8192]{2,0,1:T(8,128)(2,1)} %all-gather.2.cloned.1.call-done, s32[]{:T(128)S(6)} %select_n.77, bf16[384,1024]{1,0:T(8,128)(2,1)} %collective-permute-done.3), kind=kOutput, calls=%fused_computation.19 | convolution fusion | flops 603979776 | bytes 3538948 | tf_op jit(solution)/shard_map/cgd,td->cgt/dot_general | solution.py:56
  100.0 14.3 %collective-permute-done.5 = bf16[384,1024]{1,0:T(8,128)(2,1)} collective-permute-done((bf16[384,1024]{1,0:T(8,128)(2,1)}, bf16[384,1024]{1,0:T(8,128)(2,1)}, u32[]{:S(2)}, u32[]{:S(2)}) %collective-permute-start.5) | collective-permute-done | bytes 786464 | tf_op jit(solution)/shard_map/ppermute | solution.py:15
  114.3 2.6 %fusion.12 = f32[256,3,384]{2,0,1:T(8,128)S(1)} fusion(bf16[256,3,8192]{2,0,1:T(8,128)(2,1)} %all-gather.2.cloned.1.call-done, s32[]{:T(128)S(6)} %select_n.80, bf16[384,1024]{1,0:T(8,128)(2,1)} %collective-permute-done.5), kind=kOutput, calls=%fused_computation.15 | convolution fusion | flops 603979776 | bytes 3538948 | tf_op jit(solution)/shard_map/cgd,td->cgt/dot_general | solution.py:56
  116.9 0.0 copy-done.2
  116.9 0.0 copy-done.1
  116.9 1.8 fusion.7
  118.7 1.0 fusion.39
  119.8 0.0 copy-start.3
  119.8 1.2 collective-permute-done.4
  121.0 1.0 fusion.42
  122.1 0.1 slice.51
  122.2 5.6 %collective-permute-start.6 = (bf16[256,3,2]{2,0,1:T(8,128)(2,1)S(1)}, bf16[256,3,2]{2,0,1:T(8,128)(2,1)S(1)}, u32[]{:S(2)}, u32[]{:S(2)}) collective-permute-start(bf16[256,3,2]{2,0,1:T(8,128)(2,1)S(1)} %slice.51), channel_id=1, source_target_pairs={{0,8},{8,16},{16,24},{24,32},{32,40},{40,48},{48,56},{56,64},{64,7... | collective-permute-start | bytes 9224 | tf_op jit(solution)/shard_map/ppermute | solution.py:10
  127.8 0.0 copy-done.3
  127.8 2.4 %collective-permute-done.6 = bf16[256,3,2]{2,0,1:T(8,128)(2,1)S(1)} collective-permute-done((bf16[256,3,2]{2,0,1:T(8,128)(2,1)S(1)}, bf16[256,3,2]{2,0,1:T(8,128)(2,1)S(1)}, u32[]{:S(2)}, u32[]{:S(2)}) %collective-permute-start.6) | collective-permute-done | bytes 3104 | tf_op jit(solution)/shard_map/ppermute | solution.py:10
  130.2 0.4 pad_maximum_fusion
  130.6 0.2 convert_element_type.36
  130.8 1.1 fusion.45
  132.0 0.0 copy-start.4
  132.0 4.0 %multiply_exponential_fusion = (f32[16,256,384]{2,1,0:T(8,128)}, f32[16,256]{1,0:T(8,128)S(1)}) fusion(f32[384]{0:T(512)S(1)} %get-tuple-element.14, f32[16,256]{1,0:T(8,128)S(1)} %neg.8, f32[256,384]{1,0:T(8,128)S(1)} %convert_element_type.39, f32[384]{0:T(512)S(1)} %get-tuple-element.15), kind=kLoop, calls=%fused_computation.1 | loop fusion | flops 6287360 | bytes 6720512 | tf_op jit(solution)/shard_map/exp | solution.py:105
  136.0 0.9 broadcast_in_dim.12
  136.8 8.4 %all-to-all-start = ((f32[32,16,256]{2,1,0:T(8,128)}), f32[32,16,256]{2,1,0:T(8,128)S(1)}, u32[]{:S(2)}, u32[]{:S(2)}) async-start(f32[32,16,256]{2,1,0:T(8,128)} %broadcast_in_dim.12), calls=%async_computation | async-start | bytes 1048576 | tf_op jit(solution)/shard_map/all_to_all | solution.py:81
  145.3 11.5 %all-to-all-done = f32[32,16,256]{2,1,0:T(8,128)S(1)} async-done(((f32[32,16,256]{2,1,0:T(8,128)}), f32[32,16,256]{2,1,0:T(8,128)S(1)}, u32[]{:S(2)}, u32[]{:S(2)}) %all-to-all-start) | async-done | bytes 524320 | tf_op jit(solution)/shard_map/all_to_all | solution.py:81
  156.8 0.2 multiply_reduce_fusion.3
  157.0 0.0 copy-done.4
  157.0 0.0 slice-start.1
  157.0 5.6 %multiply_reduce_fusion.2 = f32[256,384]{1,0:T(8,128)S(1)} fusion(f32[16,256]{1,0:T(8,128)S(1)} %neg.8, f32[16,256]{1,0:T(8,128)S(1)} %get-tuple-element.6, f32[256,384]{1,0:T(8,128)S(1)} %convert_element_type.39, f32[16,256]{1,0:T(8,128)S(1)} %copy-done.3), kind=kOutput, calls=%fused_computation.3 | convolution fusion | flops 3633364992 | bytes 835584 | tf_op jit(solution)/shard_map/mcs,st->mct/dot_general | solution.py:96
  162.6 0.0 slice-done
  162.6 0.0 slice-done.1
  162.7 0.0 copy-start.6
  162.7 0.0 copy-start
  162.7 0.7 multiply_reduce_fusion
  163.4 0.0 copy-done.6
  163.4 0.1 add_convert_fusion.1
  163.6 0.1 fusion.67
  163.6 4.0 %collective-permute-start.7 = (bf16[256,384]{1,0:T(8,128)(2,1)S(1)}, bf16[256,384]{1,0:T(8,128)(2,1)S(1)}, u32[]{:S(2)}, u32[]{:S(2)}) collective-permute-start(bf16[256,384]{1,0:T(8,128)(2,1)S(1)} %fusion.67), channel_id=1, source_target_pairs={{0,4},{2,6},{4,0},{6,2},{1,5},{3,7},{5,1},{7,3},{8,12},{10,14},{12... | collective-permute-start | bytes 589832 | tf_op jit(solution)/shard_map/ppermute | solution.py:15
  167.7 2.4 %collective-permute-start.8 = (bf16[256,384]{1,0:T(8,128)(2,1)S(1)}, bf16[256,384]{1,0:T(8,128)(2,1)S(1)}, u32[]{:S(2)}, u32[]{:S(2)}) collective-permute-start(bf16[256,384]{1,0:T(8,128)(2,1)S(1)} %fusion.67), channel_id=1, source_target_pairs={{0,2},{2,4},{4,6},{6,0},{1,3},{3,5},{5,7},{7,1},{8,10},{10,12},{12... | collective-permute-start | bytes 589832 | tf_op jit(solution)/shard_map/ppermute | solution.py:15
  170.1 1.2 collective-permute-start.9
  171.2 0.0 copy-done
  171.2 0.6 fusion.55
  171.8 4.2 %collective-permute-done.7 = bf16[256,384]{1,0:T(8,128)(2,1)S(1)} collective-permute-done((bf16[256,384]{1,0:T(8,128)(2,1)S(1)}, bf16[256,384]{1,0:T(8,128)(2,1)S(1)}, u32[]{:S(2)}, u32[]{:S(2)}) %collective-permute-start.7) | collective-permute-done | bytes 196640 | tf_op jit(solution)/shard_map/ppermute | solution.py:15
  176.1 0.6 fusion.53
  176.7 9.8 %collective-permute-done.8 = bf16[256,384]{1,0:T(8,128)(2,1)S(1)} collective-permute-done((bf16[256,384]{1,0:T(8,128)(2,1)S(1)}, bf16[256,384]{1,0:T(8,128)(2,1)S(1)}, u32[]{:S(2)}, u32[]{:S(2)}) %collective-permute-start.8) | collective-permute-done | bytes 196640 | tf_op jit(solution)/shard_map/ppermute | solution.py:15
  186.5 0.6 fusion.51
  187.1 0.0 collective-permute-done.9
  187.1 1.8 add_convert_fusion
  (11 shorter events, 0.1 us)
Async XLA Ops:
  6.5 12.7 %copy-start.5 = (f32[3,3,256]{2,1,0:T(4,128)S(1)}, f32[3,3,256]{2,1,0:T(4,128)}, u32[]{:S(2)}) copy-start(f32[3,3,256]{2,1,0:T(4,128)} %param.9) | copy-start | bytes 27652
  6.5 81.8 %all-gather.2.cloned.1.call-start = ((), (), s32[]{:S(2)}) async-start(), calls=%async_computation.1 | async-start | bytes 12976128 | tf_op jit(solution)/shard_map/all_gather | solution.py:48
  8.8 49.8 %collective-permute-start.1 = (bf16[384,1024]{1,0:T(8,128)(2,1)S(1)}, bf16[384,1024]{1,0:T(8,128)(2,1)}, u32[]{:S(2)}, u32[]{:S(2)}) collective-permute-start(bf16[384,1024]{1,0:T(8,128)(2,1)S(1)} %get-tuple-element.8), channel_id=1, source_target_pairs={{0,6},{2,0},{4,2},{6,4},{1,7},{3,1},{5,3},{7,5},{8,14},{10,8},{12,... | collective-permute-start | bytes 2359304 | tf_op jit(solution)/shard_map/ppermute | solution.py:15
  15.7 48.9 %collective-permute-start = (bf16[384,1024]{1,0:T(8,128)(2,1)S(1)}, bf16[384,1024]{1,0:T(8,128)(2,1)S(1)}, u32[]{:S(2)}, u32[]{:S(2)}) collective-permute-start(bf16[384,1024]{1,0:T(8,128)(2,1)S(1)} %get-tuple-element.7), channel_id=1, source_target_pairs={{0,2},{2,4},{4,6},{6,0},{1,3},{3,5},{5,7},{7,1},{8,10},{10,12},{12... | collective-permute-start | bytes 2359304 | tf_op jit(solution)/shard_map/ppermute | solution.py:15
  15.7 75.4 %collective-permute-start.2 = (bf16[384,1024]{1,0:T(8,128)(2,1)S(1)}, bf16[384,1024]{1,0:T(8,128)(2,1)}, u32[]{:S(2)}, u32[]{:S(2)}) collective-permute-start(bf16[384,1024]{1,0:T(8,128)(2,1)S(1)} %get-tuple-element.8), channel_id=1, source_target_pairs={{0,2},{2,4},{4,6},{6,0},{1,3},{3,5},{5,7},{7,1},{8,10},{10,12},{12... | collective-permute-start | bytes 2359304 | tf_op jit(solution)/shard_map/ppermute | solution.py:15
  16.9 80.5 %collective-permute-start.3 = (bf16[384,1024]{1,0:T(8,128)(2,1)S(1)}, bf16[384,1024]{1,0:T(8,128)(2,1)}, u32[]{:S(2)}, u32[]{:S(2)}) collective-permute-start(bf16[384,1024]{1,0:T(8,128)(2,1)S(1)} %get-tuple-element.7), channel_id=1, source_target_pairs={{0,6},{2,0},{4,2},{6,4},{1,7},{3,1},{5,3},{7,5},{8,14},{10,8},{12,... | collective-permute-start | bytes 2359304 | tf_op jit(solution)/shard_map/ppermute | solution.py:15
  58.6 55.7 %collective-permute-start.5 = (bf16[384,1024]{1,0:T(8,128)(2,1)}, bf16[384,1024]{1,0:T(8,128)(2,1)}, u32[]{:S(2)}, u32[]{:S(2)}) collective-permute-start(bf16[384,1024]{1,0:T(8,128)(2,1)} %collective-permute-done.1), channel_id=1, source_target_pairs={{0,6},{2,0},{4,2},{6,4},{1,7},{3,1},{5,3},{7,5},{8,14},{10,8},{12,... | collective-permute-start | bytes 2359304 | tf_op jit(solution)/shard_map/ppermute | solution.py:15
  64.6 56.5 %collective-permute-start.4 = (bf16[384,1024]{1,0:T(8,128)(2,1)S(1)}, bf16[384,1024]{1,0:T(8,128)(2,1)S(1)}, u32[]{:S(2)}, u32[]{:S(2)}) collective-permute-start(bf16[384,1024]{1,0:T(8,128)(2,1)S(1)} %collective-permute-done), channel_id=1, source_target_pairs={{0,2},{2,4},{4,6},{6,0},{1,3},{3,5},{5,7},{7,1},{8,10},{10,12},{12... | collective-permute-start | bytes 2359304 | tf_op jit(solution)/shard_map/ppermute | solution.py:15
  88.3 28.6 %copy-start.2 = (bf16[256,3,8192]{2,0,1:T(8,128)(2,1)S(1)}, bf16[256,3,8192]{2,0,1:T(8,128)(2,1)}, u32[]{:S(2)}) copy-start(bf16[256,3,8192]{2,0,1:T(8,128)(2,1)} %all-gather.2.cloned.1.call-done) | copy-start | bytes 37748740
  94.3 22.6 %copy-start.1 = (bf16[384,2048]{1,0:T(8,128)(2,1)S(1)}, bf16[384,2048]{1,0:T(8,128)(2,1)}, u32[]{:S(2)}) copy-start(bf16[384,2048]{1,0:T(8,128)(2,1)} %param.7) | copy-start | bytes 4718596
  119.8 8.0 %copy-start.3 = (f32[16,256]{1,0:T(8,128)S(1)}, f32[16,256]{1,0:T(8,128)}, u32[]{:S(2)}) copy-start(f32[16,256]{1,0:T(8,128)} %param.10) | copy-start | bytes 49156
  122.2 8.0 %collective-permute-start.6 = (bf16[256,3,2]{2,0,1:T(8,128)(2,1)S(1)}, bf16[256,3,2]{2,0,1:T(8,128)(2,1)S(1)}, u32[]{:S(2)}, u32[]{:S(2)}) collective-permute-start(bf16[256,3,2]{2,0,1:T(8,128)(2,1)S(1)} %slice.51), channel_id=1, source_target_pairs={{0,8},{8,16},{16,24},{24,32},{32,40},{40,48},{48,56},{56,64},{64,7... | collective-permute-start | bytes 9224 | tf_op jit(solution)/shard_map/ppermute | solution.py:10
  132.0 25.0 %copy-start.4 = (f32[16,256]{1,0:T(8,128)S(1)}, f32[16,256]{1,0:T(8,128)}, u32[]{:S(2)}) copy-start(f32[16,256]{1,0:T(8,128)} %param.11) | copy-start | bytes 49156
  136.8 20.0 %all-to-all-start = ((f32[32,16,256]{2,1,0:T(8,128)}), f32[32,16,256]{2,1,0:T(8,128)S(1)}, u32[]{:S(2)}, u32[]{:S(2)}) async-start(f32[32,16,256]{2,1,0:T(8,128)} %broadcast_in_dim.12), calls=%async_computation | async-start | bytes 1048576 | tf_op jit(solution)/shard_map/all_to_all | solution.py:81
  156.8 5.8 %slice-start = ((s8[6291456]{0:T(1024)(128)(4,1)}), s8[4194304]{0:T(1024)(128)(4,1)S(1)}, s32[]{:S(2)}) async-start(s8[6291456]{0:T(1024)(128)(4,1)} %bitcast.43), calls=%async_computation.2 | async-start | bytes 8388608
  157.0 5.6 %slice-start.1 = ((s8[6291456]{0:T(1024)(128)(4,1)}), s8[2097152]{0:T(1024)(128)(4,1)S(1)}, s32[]{:S(2)}) async-start(s8[6291456]{0:T(1024)(128)(4,1)} %bitcast.43), calls=%async_computation.3 | async-start | bytes 4194304
  162.7 0.8 copy-start.6
  162.7 8.6 %copy-start = (bf16[1024,2048]{1,0:T(8,128)(2,1)S(1)}, bf16[1024,2048]{1,0:T(8,128)(2,1)}, u32[]{:S(2)}) copy-start(bf16[1024,2048]{1,0:T(8,128)(2,1)} %param.13) | copy-start | bytes 12582916
  163.6 12.5 %collective-permute-start.7 = (bf16[256,384]{1,0:T(8,128)(2,1)S(1)}, bf16[256,384]{1,0:T(8,128)(2,1)S(1)}, u32[]{:S(2)}, u32[]{:S(2)}) collective-permute-start(bf16[256,384]{1,0:T(8,128)(2,1)S(1)} %fusion.67), channel_id=1, source_target_pairs={{0,4},{2,6},{4,0},{6,2},{1,5},{3,7},{5,1},{7,3},{8,12},{10,14},{12... | collective-permute-start | bytes 589832 | tf_op jit(solution)/shard_map/ppermute | solution.py:15
  167.7 18.8 %collective-permute-start.8 = (bf16[256,384]{1,0:T(8,128)(2,1)S(1)}, bf16[256,384]{1,0:T(8,128)(2,1)S(1)}, u32[]{:S(2)}, u32[]{:S(2)}) collective-permute-start(bf16[256,384]{1,0:T(8,128)(2,1)S(1)} %fusion.67), channel_id=1, source_target_pairs={{0,2},{2,4},{4,6},{6,0},{1,3},{3,5},{5,7},{7,1},{8,10},{10,12},{12... | collective-permute-start | bytes 589832 | tf_op jit(solution)/shard_map/ppermute | solution.py:15
  170.1 17.0 %collective-permute-start.9 = (bf16[256,384]{1,0:T(8,128)(2,1)S(1)}, bf16[256,384]{1,0:T(8,128)(2,1)S(1)}, u32[]{:S(2)}, u32[]{:S(2)}) collective-permute-start(bf16[256,384]{1,0:T(8,128)(2,1)S(1)} %fusion.67), channel_id=1, source_target_pairs={{0,6},{2,0},{4,2},{6,4},{1,7},{3,1},{5,3},{7,5},{8,14},{10,8},{12,... | collective-permute-start | bytes 589832 | tf_op jit(solution)/shard_map/ppermute | solution.py:15
Sparse Core Ops, SparseCore 0:
  9.8 78.4 all-gather.1

commit v8 on v7

--- a/solution.py
+++ b/solution.py
@@ -107,20 +107,19 @@
     longc = (conv + skip[:, None] * z_f).astype(jnp.bfloat16)
     long_f = lax.optimization_barrier(longc).astype(jnp.float32)
     gated = (query * long_f).astype(jnp.bfloat16)
-    def rows_of(step):
-        index = (chan_rank - step) % chan_count
-        return lax.dynamic_slice_in_dim(w_out, index * ch_dev, ch_dev, axis=0)
-
-    shifts = sorted(
-        [step if step <= chan_count // 2 else step - chan_count for step in range(1, chan_count)],
-        key=lambda step: -abs(step),
+    every = lax.all_to_all(
+        jnp.broadcast_to(gated[None], (chan_count,) + gated.shape),
+        "chan",
+        split_axis=0,
+        concat_axis=0,
+        tiled=True,
     )
-    arrived = [(step, ring_shift(gated, "chan", step)) for step in shifts]
-    mixed = jnp.einsum("ct,ce->te", gated, rows_of(0), preferred_element_type=jnp.float32)
-    for step, piece in arrived:
-        mixed = mixed + jnp.einsum(
-            "ct,ce->te", piece, rows_of(step), preferred_element_type=jnp.float32
-        )
+    mixed = jnp.einsum(
+        "ct,ce->te",
+        every.reshape(chan_count * ch_dev, tok_rows),
+        w_out,
+        preferred_element_type=jnp.float32,
+    )
     return mixed.astype(jnp.bfloat16)
 
 

time: 196 us -> 201 us (1.026)
  blocking collectives: 0 us -> 26.7 us
  waiting for transfers between devices: 110 us -> 96.3 us
  starting transfers between devices: 38.1 us -> 30.5 us
    all_to_all x0 -> x1, blocking collectives: none -> 26.7 us  [on_device(): lax.all_to_all(jnp.broadcast_to(gated[None], (chan_count,) + gated.shape)...]
    ppermute x9 -> x6, waiting for transfers between devices: 72 us -> 57.9 us  [ring_shift(): lax.ppermute(value, axis, [(source, (source + steps) % count) for source...]
    ppermute x9 -> x6, starting transfers between devices: 24.1 us -> 16.5 us  [ring_shift(): lax.ppermute(value, axis, [(source, (source + steps) % count) for source...]
  transfers between devices with their start and end apart: 12 -> 9, of which waited for: 9 -> 7; matrix products, arithmetic and copies ran while one was open for 9% -> 8% of each run, Pallas kernels for 0% -> 0%
where the time goes in v8:
time: 201 us; the launch traced here: 200 us
  waiting for transfers between devices  96.3 us (48%)
  starting transfers between devices  30.5 us (15%)
  blocking collectives  26.7 us (13%)
  matrix products  23.7 us (12%)
  between operations  13.7 us (7%)
  other arithmetic  6.9 us (3%)
  local copies, waits for them, and re-layouts  2.58 us (1%)
    ppermute x6, waiting for transfers between devices, ring_shift(): lax.ppermute(value, axis, [(source, (source + steps) % count) for source...  57.9 us
    all_to_all x1, blocking collectives, on_device(): lax.all_to_all(jnp.broadcast_to(gated[None], (chan_count,) + gated.shape)...  26.7 us
    all_gather x1, waiting for transfers between devices, on_device(): w_full = lax.all_gather(w_in, 'seq', axis=2, tiled=True)  23.7 us
    ppermute x6, starting transfers between devices, ring_shift(): lax.ppermute(value, axis, [(source, (source + steps) % count) for source...  16.5 us
    dot_general x6, matrix products, on_device(): jnp.einsum('cgd,td->cgt', block_of(step, lo, hi), piece, preferred_elemen...  13.3 us
    all_to_all x1, waiting for transfers between devices, on_device(): lax.all_to_all(jnp.broadcast_to(ending[None], (seq_count,) + ending.shape...  11.6 us
    all_to_all x1, starting transfers between devices, on_device(): lax.all_to_all(jnp.broadcast_to(ending[None], (seq_count,) + ending.shape...  8.39 us
    dot_general x1, matrix products, on_device(): jnp.einsum('mcs,st->mct', grow * z_f[None], upper, precision=lax.Precisio...  5.61 us
  transfers between devices with their start and end apart: 9, of which 7 were waited for; matrix products, arithmetic and copies ran while one was open for 8% of the time, Pallas kernels for 0%

profile of v8, /device:TPU:1, one launch (start us, length us, event | category | flops | bytes accessed | tf_op | source)
XLA Modules:
  0.0 200.3 jit_solution(8952320293972581200)
XLA Ops:
  6.5 0.0 all-gather.2.cloned.1.call-start
  6.5 0.7 all-gather.2.cloned.1.call-update
  7.3 0.0 copy-start.4
  7.3 1.5 fusion.67
  8.8 6.9 %collective-permute-start.1 = (bf16[384,1024]{1,0:T(8,128)(2,1)S(1)}, bf16[384,1024]{1,0:T(8,128)(2,1)}, u32[]{:S(2)}, u32[]{:S(2)}) collective-permute-start(bf16[384,1024]{1,0:T(8,128)(2,1)S(1)} %get-tuple-element.8), channel_id=1, source_target_pairs={{0,6},{2,0},{4,2},{6,4},{1,7},{3,1},{5,3},{7,5},{8,14},{10,8},{12,... | collective-permute-start | bytes 2359304 | tf_op jit(solution)/shard_map/ppermute | solution.py:15
  15.7 0.0 collective-permute-start
  15.7 1.3 collective-permute-start.2
  16.9 2.3 %collective-permute-start.3 = (bf16[384,1024]{1,0:T(8,128)(2,1)S(1)}, bf16[384,1024]{1,0:T(8,128)(2,1)}, u32[]{:S(2)}, u32[]{:S(2)}) collective-permute-start(bf16[384,1024]{1,0:T(8,128)(2,1)S(1)} %get-tuple-element.7), channel_id=1, source_target_pairs={{0,6},{2,0},{4,2},{6,4},{1,7},{3,1},{5,3},{7,5},{8,14},{10,8},{12,... | collective-permute-start | bytes 2359304 | tf_op jit(solution)/shard_map/ppermute | solution.py:15
  19.3 0.0 copy-done.4
  19.3 39.3 %collective-permute-done.1 = bf16[384,1024]{1,0:T(8,128)(2,1)} collective-permute-done((bf16[384,1024]{1,0:T(8,128)(2,1)S(1)}, bf16[384,1024]{1,0:T(8,128)(2,1)}, u32[]{:S(2)}, u32[]{:S(2)}) %collective-permute-start.1) | collective-permute-done | bytes 786464 | tf_op jit(solution)/shard_map/ppermute | solution.py:15
  58.6 6.0 %collective-permute-start.5 = (bf16[384,1024]{1,0:T(8,128)(2,1)}, bf16[384,1024]{1,0:T(8,128)(2,1)}, u32[]{:S(2)}, u32[]{:S(2)}) collective-permute-start(bf16[384,1024]{1,0:T(8,128)(2,1)} %collective-permute-done.1), channel_id=1, source_target_pairs={{0,6},{2,0},{4,2},{6,4},{1,7},{3,1},{5,3},{7,5},{8,14},{10,8},{12,... | collective-permute-start | bytes 2359304 | tf_op jit(solution)/shard_map/ppermute | solution.py:15
  64.6 0.0 collective-permute-done
  64.6 0.0 collective-permute-start.4
  64.6 23.7 %all-gather.2.cloned.1.call-done = bf16[256,3,8192]{2,0,1:T(8,128)(2,1)} async-done(((bf16[256,3,256]{2,0,1:T(8,128)(2,1)}), bf16[256,3,8192]{2,0,1:T(8,128)(2,1)}) %all-gather.2.cloned.1.call-update) | async-done | bytes 12582928 | tf_op jit(solution)/shard_map/all_gather | solution.py:48
  88.3 0.0 copy-start.1
  88.3 2.8 %fusion.20 = f32[256,3,384]{2,0,1:T(8,128)S(1)} fusion(bf16[256,3,8192]{2,0,1:T(8,128)(2,1)} %all-gather.2.cloned.1.call-done, s32[]{:T(128)S(6)} %select_n.55, bf16[384,1024]{1,0:T(8,128)(2,1)} %collective-permute-done.1), kind=kOutput, calls=%fused_computation.23 | convolution fusion | flops 603979776 | bytes 3538948 | tf_op jit(solution)/shard_map/cgd,td->cgt/dot_general | solution.py:56
  91.1 0.0 collective-permute-done.2
  91.1 3.3 %fusion.18 = f32[256,3,384]{2,0,1:T(8,128)S(1)} fusion(bf16[256,3,8192]{2,0,1:T(8,128)(2,1)} %all-gather.2.cloned.1.call-done, s32[]{:T(128)S(6)} %select_n.56, bf16[384,1024]{1,0:T(8,128)(2,1)} %collective-permute-done.2), kind=kOutput, calls=%fused_computation.21 | convolution fusion | flops 603979776 | bytes 3538948 | tf_op jit(solution)/shard_map/cgd,td->cgt/dot_general | solution.py:56
  94.3 3.1 %collective-permute-done.3 = bf16[384,1024]{1,0:T(8,128)(2,1)} collective-permute-done((bf16[384,1024]{1,0:T(8,128)(2,1)S(1)}, bf16[384,1024]{1,0:T(8,128)(2,1)}, u32[]{:S(2)}, u32[]{:S(2)}) %collective-permute-start.3) | collective-permute-done | bytes 786464 | tf_op jit(solution)/shard_map/ppermute | solution.py:15
  97.4 2.6 %fusion.16 = f32[256,3,384]{2,0,1:T(8,128)S(1)} fusion(bf16[256,3,8192]{2,0,1:T(8,128)(2,1)} %all-gather.2.cloned.1.call-done, s32[]{:T(128)S(6)} %select_n.57, bf16[384,1024]{1,0:T(8,128)(2,1)} %collective-permute-done.3), kind=kOutput, calls=%fused_computation.19 | convolution fusion | flops 603979776 | bytes 3538948 | tf_op jit(solution)/shard_map/cgd,td->cgt/dot_general | solution.py:56
  100.0 0.0 copy-start
  100.1 14.3 %collective-permute-done.5 = bf16[384,1024]{1,0:T(8,128)(2,1)} collective-permute-done((bf16[384,1024]{1,0:T(8,128)(2,1)}, bf16[384,1024]{1,0:T(8,128)(2,1)}, u32[]{:S(2)}, u32[]{:S(2)}) %collective-permute-start.5) | collective-permute-done | bytes 786464 | tf_op jit(solution)/shard_map/ppermute | solution.py:15
  114.3 2.6 %fusion.12 = f32[256,3,384]{2,0,1:T(8,128)S(1)} fusion(bf16[256,3,8192]{2,0,1:T(8,128)(2,1)} %all-gather.2.cloned.1.call-done, s32[]{:T(128)S(6)} %select_n.60, bf16[384,1024]{1,0:T(8,128)(2,1)} %collective-permute-done.5), kind=kOutput, calls=%fused_computation.15 | convolution fusion | flops 603979776 | bytes 3538948 | tf_op jit(solution)/shard_map/cgd,td->cgt/dot_general | solution.py:56
  116.9 0.0 copy-done.1
  116.9 0.0 copy-done
  116.9 1.8 fusion.7
  118.8 1.0 fusion.39
  119.8 0.0 copy-start.2
  119.8 1.2 collective-permute-done.4
  121.0 1.0 fusion.42
  122.1 0.1 slice.51
  122.2 5.6 %collective-permute-start.6 = (bf16[256,3,2]{2,0,1:T(8,128)(2,1)S(1)}, bf16[256,3,2]{2,0,1:T(8,128)(2,1)S(1)}, u32[]{:S(2)}, u32[]{:S(2)}) collective-permute-start(bf16[256,3,2]{2,0,1:T(8,128)(2,1)S(1)} %slice.51), channel_id=1, source_target_pairs={{0,8},{8,16},{16,24},{24,32},{32,40},{40,48},{48,56},{56,64},{64,7... | collective-permute-start | bytes 9224 | tf_op jit(solution)/shard_map/ppermute | solution.py:10
  127.8 0.0 copy-done.2
  127.8 2.4 %collective-permute-done.6 = bf16[256,3,2]{2,0,1:T(8,128)(2,1)S(1)} collective-permute-done((bf16[256,3,2]{2,0,1:T(8,128)(2,1)S(1)}, bf16[256,3,2]{2,0,1:T(8,128)(2,1)S(1)}, u32[]{:S(2)}, u32[]{:S(2)}) %collective-permute-start.6) | collective-permute-done | bytes 3104 | tf_op jit(solution)/shard_map/ppermute | solution.py:10
  130.2 0.4 pad_maximum_fusion
  130.6 0.2 convert_element_type.36
  130.8 1.1 fusion.45
  132.0 4.0 %multiply_exponential_fusion = (f32[16,256,384]{2,1,0:T(8,128)}, f32[16,256]{1,0:T(8,128)S(1)}) fusion(f32[384]{0:T(512)S(1)} %get-tuple-element.14, f32[16,256]{1,0:T(8,128)S(1)} %neg.8, f32[256,384]{1,0:T(8,128)S(1)} %convert_element_type.39, f32[384]{0:T(512)S(1)} %get-tuple-element.15), kind=kLoop, calls=%fused_computation.1 | loop fusion | flops 6287360 | bytes 6720512 | tf_op jit(solution)/shard_map/exp | solution.py:105
  136.0 0.0 copy-start.3
  136.0 0.9 broadcast_in_dim.14
  136.8 8.4 %all-to-all-start = ((f32[32,16,256]{2,1,0:T(8,128)}), f32[32,16,256]{2,1,0:T(8,128)S(1)}, u32[]{:S(2)}, u32[]{:S(2)}) async-start(f32[32,16,256]{2,1,0:T(8,128)} %broadcast_in_dim.14), calls=%async_computation | async-start | bytes 1048576 | tf_op jit(solution)/shard_map/all_to_all | solution.py:81
  145.3 11.6 %all-to-all-done = f32[32,16,256]{2,1,0:T(8,128)S(1)} async-done(((f32[32,16,256]{2,1,0:T(8,128)}), f32[32,16,256]{2,1,0:T(8,128)S(1)}, u32[]{:S(2)}, u32[]{:S(2)}) %all-to-all-start) | async-done | bytes 524320 | tf_op jit(solution)/shard_map/all_to_all | solution.py:81
  156.8 0.0 slice-start
  156.8 0.2 multiply_reduce_fusion.3
  157.0 0.0 copy-done.3
  157.0 0.0 slice-start.1
  157.1 5.6 %multiply_reduce_fusion.2 = f32[256,384]{1,0:T(8,128)S(1)} fusion(f32[16,256]{1,0:T(8,128)S(1)} %neg.8, f32[16,256]{1,0:T(8,128)S(1)} %get-tuple-element.6, f32[256,384]{1,0:T(8,128)S(1)} %convert_element_type.39, f32[16,256]{1,0:T(8,128)S(1)} %copy-done.2), kind=kOutput, calls=%fused_computation.3 | convolution fusion | flops 3633364992 | bytes 835584 | tf_op jit(solution)/shard_map/mcs,st->mct/dot_general | solution.py:96
  162.7 0.0 slice-done
  162.7 0.0 slice-done.1
  162.7 0.0 copy-start.5
  162.7 0.8 multiply_reduce_fusion
  163.5 0.0 copy-done.5
  163.5 0.0 copy-start.6
  163.5 0.1 add_convert_fusion
  163.7 0.1 broadcast_in_dim.15
  163.7 26.7 %all_to_all.10 = bf16[4,256,384]{2,1,0:T(8,128)(2,1)S(1)} all-to-all(bf16[4,256,384]{2,1,0:T(8,128)(2,1)S(1)} %broadcast_in_dim.15), channel_id=1, replica_groups=mesh['seq'=32,'chan'=4,'rep'=2] {'chan'}, dimensions={0} | all-to-all | bytes 1572864 | tf_op jit(solution)/shard_map/all_to_all | solution.py:110
  190.4 0.0 copy-done.6
  190.4 3.0 %convolution_convert_fusion = bf16[384,2048]{1,0:T(8,128)(2,1)} fusion(bf16[1024,384]{1,0:T(8,128)(2,1)S(1)} %bitcast.44, bf16[1024,2048]{1,0:T(8,128)(2,1)S(1)} %copy-done.6), kind=kOutput, calls=%fused_computation.13 | convolution fusion | flops 1611399168 | bytes 6553600 | tf_op jit(solution)/shard_map/ct,ce->te/dot_general | solution.py:117
  (10 shorter events, 0.2 us)
Async XLA Ops:
  6.5 81.8 %all-gather.2.cloned.1.call-start = ((), (), s32[]{:S(2)}) async-start(), calls=%async_computation.2 | async-start | bytes 12976128 | tf_op jit(solution)/shard_map/all_gather | solution.py:48
  7.3 12.0 %copy-start.4 = (f32[3,3,256]{2,1,0:T(4,128)S(1)}, f32[3,3,256]{2,1,0:T(4,128)}, u32[]{:S(2)}) copy-start(f32[3,3,256]{2,1,0:T(4,128)} %param.9) | copy-start | bytes 27652
  8.8 49.8 %collective-permute-start.1 = (bf16[384,1024]{1,0:T(8,128)(2,1)S(1)}, bf16[384,1024]{1,0:T(8,128)(2,1)}, u32[]{:S(2)}, u32[]{:S(2)}) collective-permute-start(bf16[384,1024]{1,0:T(8,128)(2,1)S(1)} %get-tuple-element.8), channel_id=1, source_target_pairs={{0,6},{2,0},{4,2},{6,4},{1,7},{3,1},{5,3},{7,5},{8,14},{10,8},{12,... | collective-permute-start | bytes 2359304 | tf_op jit(solution)/shard_map/ppermute | solution.py:15
  15.7 48.9 %collective-permute-start = (bf16[384,1024]{1,0:T(8,128)(2,1)S(1)}, bf16[384,1024]{1,0:T(8,128)(2,1)S(1)}, u32[]{:S(2)}, u32[]{:S(2)}) collective-permute-start(bf16[384,1024]{1,0:T(8,128)(2,1)S(1)} %get-tuple-element.7), channel_id=1, source_target_pairs={{0,2},{2,4},{4,6},{6,0},{1,3},{3,5},{5,7},{7,1},{8,10},{10,12},{12... | collective-permute-start | bytes 2359304 | tf_op jit(solution)/shard_map/ppermute | solution.py:15
  15.7 75.4 %collective-permute-start.2 = (bf16[384,1024]{1,0:T(8,128)(2,1)S(1)}, bf16[384,1024]{1,0:T(8,128)(2,1)}, u32[]{:S(2)}, u32[]{:S(2)}) collective-permute-start(bf16[384,1024]{1,0:T(8,128)(2,1)S(1)} %get-tuple-element.8), channel_id=1, source_target_pairs={{0,2},{2,4},{4,6},{6,0},{1,3},{3,5},{5,7},{7,1},{8,10},{10,12},{12... | collective-permute-start | bytes 2359304 | tf_op jit(solution)/shard_map/ppermute | solution.py:15
  16.9 80.5 %collective-permute-start.3 = (bf16[384,1024]{1,0:T(8,128)(2,1)S(1)}, bf16[384,1024]{1,0:T(8,128)(2,1)}, u32[]{:S(2)}, u32[]{:S(2)}) collective-permute-start(bf16[384,1024]{1,0:T(8,128)(2,1)S(1)} %get-tuple-element.7), channel_id=1, source_target_pairs={{0,6},{2,0},{4,2},{6,4},{1,7},{3,1},{5,3},{7,5},{8,14},{10,8},{12,... | collective-permute-start | bytes 2359304 | tf_op jit(solution)/shard_map/ppermute | solution.py:15
  58.6 55.7 %collective-permute-start.5 = (bf16[384,1024]{1,0:T(8,128)(2,1)}, bf16[384,1024]{1,0:T(8,128)(2,1)}, u32[]{:S(2)}, u32[]{:S(2)}) collective-permute-start(bf16[384,1024]{1,0:T(8,128)(2,1)} %collective-permute-done.1), channel_id=1, source_target_pairs={{0,6},{2,0},{4,2},{6,4},{1,7},{3,1},{5,3},{7,5},{8,14},{10,8},{12,... | collective-permute-start | bytes 2359304 | tf_op jit(solution)/shard_map/ppermute | solution.py:15
  64.6 56.5 %collective-permute-start.4 = (bf16[384,1024]{1,0:T(8,128)(2,1)S(1)}, bf16[384,1024]{1,0:T(8,128)(2,1)S(1)}, u32[]{:S(2)}, u32[]{:S(2)}) collective-permute-start(bf16[384,1024]{1,0:T(8,128)(2,1)S(1)} %collective-permute-done), channel_id=1, source_target_pairs={{0,2},{2,4},{4,6},{6,0},{1,3},{3,5},{5,7},{7,1},{8,10},{10,12},{12... | collective-permute-start | bytes 2359304 | tf_op jit(solution)/shard_map/ppermute | solution.py:15
  88.3 28.6 %copy-start.1 = (bf16[256,3,8192]{2,0,1:T(8,128)(2,1)S(1)}, bf16[256,3,8192]{2,0,1:T(8,128)(2,1)}, u32[]{:S(2)}) copy-start(bf16[256,3,8192]{2,0,1:T(8,128)(2,1)} %all-gather.2.cloned.1.call-done) | copy-start | bytes 37748740
  100.0 16.9 %copy-start = (bf16[384,2048]{1,0:T(8,128)(2,1)S(1)}, bf16[384,2048]{1,0:T(8,128)(2,1)}, u32[]{:S(2)}) copy-start(bf16[384,2048]{1,0:T(8,128)(2,1)} %param.7) | copy-start | bytes 4718596
  119.8 8.0 %copy-start.2 = (f32[16,256]{1,0:T(8,128)S(1)}, f32[16,256]{1,0:T(8,128)}, u32[]{:S(2)}) copy-start(f32[16,256]{1,0:T(8,128)} %param.10) | copy-start | bytes 49156
  122.2 8.0 %collective-permute-start.6 = (bf16[256,3,2]{2,0,1:T(8,128)(2,1)S(1)}, bf16[256,3,2]{2,0,1:T(8,128)(2,1)S(1)}, u32[]{:S(2)}, u32[]{:S(2)}) collective-permute-start(bf16[256,3,2]{2,0,1:T(8,128)(2,1)S(1)} %slice.51), channel_id=1, source_target_pairs={{0,8},{8,16},{16,24},{24,32},{32,40},{40,48},{48,56},{56,64},{64,7... | collective-permute-start | bytes 9224 | tf_op jit(solution)/shard_map/ppermute | solution.py:10
  136.0 21.0 %copy-start.3 = (f32[16,256]{1,0:T(8,128)S(1)}, f32[16,256]{1,0:T(8,128)}, u32[]{:S(2)}) copy-start(f32[16,256]{1,0:T(8,128)} %param.11) | copy-start | bytes 49156
  136.8 20.0 %all-to-all-start = ((f32[32,16,256]{2,1,0:T(8,128)}), f32[32,16,256]{2,1,0:T(8,128)S(1)}, u32[]{:S(2)}, u32[]{:S(2)}) async-start(f32[32,16,256]{2,1,0:T(8,128)} %broadcast_in_dim.14), calls=%async_computation | async-start | bytes 1048576 | tf_op jit(solution)/shard_map/all_to_all | solution.py:81
  156.8 5.8 %slice-start = ((s8[6291456]{0:T(1024)(128)(4,1)}), s8[4194304]{0:T(1024)(128)(4,1)S(1)}, s32[]{:S(2)}) async-start(s8[6291456]{0:T(1024)(128)(4,1)} %bitcast.42), calls=%async_computation.3 | async-start | bytes 8388608
  157.0 5.6 %slice-start.1 = ((s8[6291456]{0:T(1024)(128)(4,1)}), s8[2097152]{0:T(1024)(128)(4,1)S(1)}, s32[]{:S(2)}) async-start(s8[6291456]{0:T(1024)(128)(4,1)} %bitcast.42), calls=%async_computation.4 | async-start | bytes 4194304
  162.7 0.8 copy-start.5
  163.5 27.0 %copy-start.6 = (bf16[1024,2048]{1,0:T(8,128)(2,1)S(1)}, bf16[1024,2048]{1,0:T(8,128)(2,1)}, u32[]{:S(2)}) copy-start(bf16[1024,2048]{1,0:T(8,128)(2,1)} %param.13) | copy-start | bytes 12582916
Sparse Core Ops, SparseCore 0:
  9.8 78.4 all-gather.1

commit v9 on v7

--- a/solution.py
+++ b/solution.py
@@ -76,8 +76,8 @@
     grow = jnp.exp(decay[:, :, None] * tau)
     fall = jnp.exp(-decay[:, :, None] * tau)
     upper = (tau[:, None] <= tau[None, :]).astype(jnp.float32)
-    tail = jnp.exp(-decay[:, :, None] * (tok_rows - 1.0 - tau))
-    ending = jnp.sum(tail * z_f[None], axis=2)
+    lifted = grow * z_f[None]
+    ending = jnp.exp(-decay * (tok_rows - 1.0)) * jnp.sum(lifted, axis=2)
     states = lax.all_to_all(
         jnp.broadcast_to(ending[None], (seq_count,) + ending.shape),
         "seq",
@@ -95,7 +95,7 @@
     incoming = jnp.sum(carry * states, axis=0)
     prefix = jnp.einsum(
         "mcs,st->mct",
-        grow * z_f[None],
+        lifted,
         upper,
         precision=lax.Precision.HIGH,
         preferred_element_type=jnp.float32,

time: 196 us -> 194 us (0.990)
  waiting for transfers between devices: 110 us -> 107 us
    all_to_all x1, waiting for transfers between devices: 11.5 us -> 8.36 us  [on_device(): lax.all_to_all(jnp.broadcast_to(ending[None], (seq_count,) + ending.shape...]
  transfers between devices with their start and end apart: 12 -> 12, of which waited for: 9 -> 9; matrix products, arithmetic and copies ran while one was open for 9% -> 11% of each run, Pallas kernels for 0% -> 0%
where the time goes in v9:
time: 194 us
  waiting for transfers between devices  107 us (55%)
  starting transfers between devices  38.1 us (20%)
  matrix products  24.3 us (13%)
  between operations  13.7 us (7%)
  other arithmetic  7.88 us (4%)
  local copies, waits for them, and re-layouts  2.52 us (1%)
    ppermute x9, waiting for transfers between devices, ring_shift(): lax.ppermute(value, axis, [(source, (source + steps) % count) for source...  72 us
    ppermute x9, starting transfers between devices, ring_shift(): lax.ppermute(value, axis, [(source, (source + steps) % count) for source...  24.1 us
    all_gather x1, waiting for transfers between devices, on_device(): w_full = lax.all_gather(w_in, 'seq', axis=2, tiled=True)  23.7 us
    dot_general x6, matrix products, on_device(): jnp.einsum('cgd,td->cgt', block_of(step, lo, hi), piece, preferred_elemen...  13.3 us
    all_to_all x1, starting transfers between devices, on_device(): lax.all_to_all(jnp.broadcast_to(ending[None], (seq_count,) + ending.shape...  8.38 us
    all_to_all x1, waiting for transfers between devices, on_device(): lax.all_to_all(jnp.broadcast_to(ending[None], (seq_count,) + ending.shape...  8.36 us
    dot_general x1, matrix products, on_device(): jnp.einsum('mcs,st->mct', lifted, upper, precision=lax.Precision.HIGH, pr...  5.61 us
    ppermute x1, starting transfers between devices, from_behind(): lax.ppermute(value, axis, [(source, source + steps) for source in range(l...  5.56 us
  transfers between devices with their start and end apart: 12, of which 9 were waited for; matrix products, arithmetic and copies ran while one was open for 11% of the time, Pallas kernels for 0%

profile of v9, /device:TPU:1, one launch (start us, length us, event | category | flops | bytes accessed | tf_op | source)
XLA Modules:
  0.0 193.6 jit_solution(14089702562619189459)
XLA Ops:
  6.5 0.0 copy-start.5
  6.5 0.0 all-gather.2.cloned.1.call-start
  6.5 0.7 all-gather.2.cloned.1.call-update
  7.3 1.5 fusion.76
  8.8 6.9 %collective-permute-start.1 = (bf16[384,1024]{1,0:T(8,128)(2,1)S(1)}, bf16[384,1024]{1,0:T(8,128)(2,1)}, u32[]{:S(2)}, u32[]{:S(2)}) collective-permute-start(bf16[384,1024]{1,0:T(8,128)(2,1)S(1)} %get-tuple-element.8), channel_id=1, source_target_pairs={{0,6},{2,0},{4,2},{6,4},{1,7},{3,1},{5,3},{7,5},{8,14},{10,8},{12,... | collective-permute-start | bytes 2359304 | tf_op jit(solution)/shard_map/ppermute | solution.py:15
  15.7 0.0 collective-permute-start
  15.7 1.3 collective-permute-start.2
  16.9 2.3 %collective-permute-start.3 = (bf16[384,1024]{1,0:T(8,128)(2,1)S(1)}, bf16[384,1024]{1,0:T(8,128)(2,1)}, u32[]{:S(2)}, u32[]{:S(2)}) collective-permute-start(bf16[384,1024]{1,0:T(8,128)(2,1)S(1)} %get-tuple-element.7), channel_id=1, source_target_pairs={{0,6},{2,0},{4,2},{6,4},{1,7},{3,1},{5,3},{7,5},{8,14},{10,8},{12,... | collective-permute-start | bytes 2359304 | tf_op jit(solution)/shard_map/ppermute | solution.py:15
  19.3 0.0 copy-done.5
  19.3 39.3 %collective-permute-done.1 = bf16[384,1024]{1,0:T(8,128)(2,1)} collective-permute-done((bf16[384,1024]{1,0:T(8,128)(2,1)S(1)}, bf16[384,1024]{1,0:T(8,128)(2,1)}, u32[]{:S(2)}, u32[]{:S(2)}) %collective-permute-start.1) | collective-permute-done | bytes 786464 | tf_op jit(solution)/shard_map/ppermute | solution.py:15
  58.6 6.0 %collective-permute-start.5 = (bf16[384,1024]{1,0:T(8,128)(2,1)}, bf16[384,1024]{1,0:T(8,128)(2,1)}, u32[]{:S(2)}, u32[]{:S(2)}) collective-permute-start(bf16[384,1024]{1,0:T(8,128)(2,1)} %collective-permute-done.1), channel_id=1, source_target_pairs={{0,6},{2,0},{4,2},{6,4},{1,7},{3,1},{5,3},{7,5},{8,14},{10,8},{12,... | collective-permute-start | bytes 2359304 | tf_op jit(solution)/shard_map/ppermute | solution.py:15
  64.6 0.0 collective-permute-done
  64.6 0.0 collective-permute-start.4
  64.6 23.7 %all-gather.2.cloned.1.call-done = bf16[256,3,8192]{2,0,1:T(8,128)(2,1)} async-done(((bf16[256,3,256]{2,0,1:T(8,128)(2,1)}), bf16[256,3,8192]{2,0,1:T(8,128)(2,1)}) %all-gather.2.cloned.1.call-update) | async-done | bytes 12582928 | tf_op jit(solution)/shard_map/all_gather | solution.py:48
  88.3 2.8 %fusion.15 = f32[256,3,384]{2,0,1:T(8,128)S(1)} fusion(bf16[256,3,8192]{2,0,1:T(8,128)(2,1)} %all-gather.2.cloned.1.call-done, s32[]{:T(128)S(6)} %select_n.75, bf16[384,1024]{1,0:T(8,128)(2,1)} %collective-permute-done.1), kind=kOutput, calls=%fused_computation.20 | convolution fusion | flops 603979776 | bytes 3538948 | tf_op jit(solution)/shard_map/cgd,td->cgt/dot_general | solution.py:56
  91.1 0.0 collective-permute-done.2
  91.1 3.2 %fusion.13 = f32[256,3,384]{2,0,1:T(8,128)S(1)} fusion(bf16[256,3,8192]{2,0,1:T(8,128)(2,1)} %all-gather.2.cloned.1.call-done, s32[]{:T(128)S(6)} %select_n.76, bf16[384,1024]{1,0:T(8,128)(2,1)} %collective-permute-done.2), kind=kOutput, calls=%fused_computation.18 | convolution fusion | flops 603979776 | bytes 3538948 | tf_op jit(solution)/shard_map/cgd,td->cgt/dot_general | solution.py:56
  94.3 0.0 copy-start.1
  94.3 3.1 %collective-permute-done.3 = bf16[384,1024]{1,0:T(8,128)(2,1)} collective-permute-done((bf16[384,1024]{1,0:T(8,128)(2,1)S(1)}, bf16[384,1024]{1,0:T(8,128)(2,1)}, u32[]{:S(2)}, u32[]{:S(2)}) %collective-permute-start.3) | collective-permute-done | bytes 786464 | tf_op jit(solution)/shard_map/ppermute | solution.py:15
  97.4 2.6 %fusion.11 = f32[256,3,384]{2,0,1:T(8,128)S(1)} fusion(bf16[256,3,8192]{2,0,1:T(8,128)(2,1)} %all-gather.2.cloned.1.call-done, s32[]{:T(128)S(6)} %select_n.77, bf16[384,1024]{1,0:T(8,128)(2,1)} %collective-permute-done.3), kind=kOutput, calls=%fused_computation.16 | convolution fusion | flops 603979776 | bytes 3538948 | tf_op jit(solution)/shard_map/cgd,td->cgt/dot_general | solution.py:56
  100.0 14.3 %collective-permute-done.5 = bf16[384,1024]{1,0:T(8,128)(2,1)} collective-permute-done((bf16[384,1024]{1,0:T(8,128)(2,1)}, bf16[384,1024]{1,0:T(8,128)(2,1)}, u32[]{:S(2)}, u32[]{:S(2)}) %collective-permute-start.5) | collective-permute-done | bytes 786464 | tf_op jit(solution)/shard_map/ppermute | solution.py:15
  114.3 2.6 %fusion.7 = f32[256,3,384]{2,0,1:T(8,128)S(1)} fusion(bf16[256,3,8192]{2,0,1:T(8,128)(2,1)} %all-gather.2.cloned.1.call-done, s32[]{:T(128)S(6)} %select_n.80, bf16[384,1024]{1,0:T(8,128)(2,1)} %collective-permute-done.5), kind=kOutput, calls=%fused_computation.12 | convolution fusion | flops 603979776 | bytes 3538948 | tf_op jit(solution)/shard_map/cgd,td->cgt/dot_general | solution.py:56
  116.9 0.0 copy-done.2
  116.9 0.0 copy-done.1
  116.9 1.8 fusion.4
  118.7 1.0 fusion.34
  119.8 1.2 collective-permute-done.4
  121.0 1.0 fusion.37
  122.1 0.1 slice.51
  122.2 5.6 %collective-permute-start.6 = (bf16[256,3,2]{2,0,1:T(8,128)(2,1)S(1)}, bf16[256,3,2]{2,0,1:T(8,128)(2,1)S(1)}, u32[]{:S(2)}, u32[]{:S(2)}) collective-permute-start(bf16[256,3,2]{2,0,1:T(8,128)(2,1)S(1)} %slice.51), channel_id=1, source_target_pairs={{0,8},{8,16},{16,24},{24,32},{32,40},{40,48},{48,56},{56,64},{64,7... | collective-permute-start | bytes 9224 | tf_op jit(solution)/shard_map/ppermute | solution.py:10
  127.8 2.4 %collective-permute-done.6 = bf16[256,3,2]{2,0,1:T(8,128)(2,1)S(1)} collective-permute-done((bf16[256,3,2]{2,0,1:T(8,128)(2,1)S(1)}, bf16[256,3,2]{2,0,1:T(8,128)(2,1)S(1)}, u32[]{:S(2)}, u32[]{:S(2)}) %collective-permute-start.6) | collective-permute-done | bytes 3104 | tf_op jit(solution)/shard_map/ppermute | solution.py:10
  130.2 0.4 pad_maximum_fusion
  130.6 0.2 convert_element_type.36
  130.8 0.0 copy-start.3
  130.8 1.1 fusion.40
  131.9 0.0 copy-done.3
  132.0 1.9 fusion
  133.8 0.9 broadcast_in_dim.12
  134.7 8.4 %all-to-all-start = ((f32[32,16,256]{2,1,0:T(8,128)}), f32[32,16,256]{2,1,0:T(8,128)S(1)}, u32[]{:S(2)}, u32[]{:S(2)}) async-start(f32[32,16,256]{2,1,0:T(8,128)} %broadcast_in_dim.12), calls=%async_computation | async-start | bytes 1048576 | tf_op jit(solution)/shard_map/all_to_all | solution.py:81
  143.1 0.0 copy-start.4
  143.2 3.2 %multiply_exponential_fusion = f32[16,256,384]{2,1,0:T(8,128)} fusion(f32[384]{0:T(512)S(1)} %iota_add_fusion, f32[16,256]{1,0:T(8,128)S(1)} %get-tuple-element.10), kind=kLoop, calls=%fused_computation.1 | loop fusion | flops 1572864 | bytes 6309376 | tf_op jit(solution)/shard_map/exp | solution.py:105
  146.3 8.4 %all-to-all-done = f32[32,16,256]{2,1,0:T(8,128)S(1)} async-done(((f32[32,16,256]{2,1,0:T(8,128)}), f32[32,16,256]{2,1,0:T(8,128)S(1)}, u32[]{:S(2)}, u32[]{:S(2)}) %all-to-all-start) | async-done | bytes 524320 | tf_op jit(solution)/shard_map/all_to_all | solution.py:81
  154.7 0.2 multiply_reduce_fusion.2
  154.9 0.0 copy-done.4
  154.9 0.0 slice-start.1
  154.9 5.6 %multiply_reduce_fusion.1 = f32[256,384]{1,0:T(8,128)S(1)} fusion(f32[16,256]{1,0:T(8,128)S(1)} %get-tuple-element.10, f32[16,256]{1,0:T(8,128)S(1)} %get-tuple-element.6, f32[256,384]{1,0:T(8,128)S(1)} %convert_element_type.39, f32[16,256]{1,0:T(8,128)S(1)} %copy-done.3), kind=kOutput, calls=%fused_computation.2 | convolution fusion | flops 3633364992 | bytes 835584 | tf_op jit(solution)/shard_map/mcs,st->mct/dot_general | solution.py:96
  160.5 0.0 slice-done
  160.5 0.0 slice-done.1
  160.5 0.0 copy-start.6
  160.6 0.0 copy-start
  160.6 0.7 multiply_reduce_fusion
  161.3 0.0 copy-done.6
  161.3 0.1 add_convert_fusion.1
  161.5 4.0 %collective-permute-start.7 = (bf16[256,384]{1,0:T(8,128)(2,1)S(1)}, bf16[256,384]{1,0:T(8,128)(2,1)S(1)}, u32[]{:S(2)}, u32[]{:S(2)}) collective-permute-start(bf16[256,384]{1,0:T(8,128)(2,1)S(1)} %fusion.62), channel_id=1, source_target_pairs={{0,4},{2,6},{4,0},{6,2},{1,5},{3,7},{5,1},{7,3},{8,12},{10,14},{12... | collective-permute-start | bytes 589832 | tf_op jit(solution)/shard_map/ppermute | solution.py:15
  165.6 2.4 %collective-permute-start.8 = (bf16[256,384]{1,0:T(8,128)(2,1)S(1)}, bf16[256,384]{1,0:T(8,128)(2,1)S(1)}, u32[]{:S(2)}, u32[]{:S(2)}) collective-permute-start(bf16[256,384]{1,0:T(8,128)(2,1)S(1)} %fusion.62), channel_id=1, source_target_pairs={{0,2},{2,4},{4,6},{6,0},{1,3},{3,5},{5,7},{7,1},{8,10},{10,12},{12... | collective-permute-start | bytes 589832 | tf_op jit(solution)/shard_map/ppermute | solution.py:15
  168.0 1.2 collective-permute-start.9
  169.1 0.0 copy-done
  169.1 0.6 fusion.50
  169.7 4.2 %collective-permute-done.7 = bf16[256,384]{1,0:T(8,128)(2,1)S(1)} collective-permute-done((bf16[256,384]{1,0:T(8,128)(2,1)S(1)}, bf16[256,384]{1,0:T(8,128)(2,1)S(1)}, u32[]{:S(2)}, u32[]{:S(2)}) %collective-permute-start.7) | collective-permute-done | bytes 196640 | tf_op jit(solution)/shard_map/ppermute | solution.py:15
  174.0 0.6 fusion.48
  174.6 9.8 %collective-permute-done.8 = bf16[256,384]{1,0:T(8,128)(2,1)S(1)} collective-permute-done((bf16[256,384]{1,0:T(8,128)(2,1)S(1)}, bf16[256,384]{1,0:T(8,128)(2,1)S(1)}, u32[]{:S(2)}, u32[]{:S(2)}) %collective-permute-start.8) | collective-permute-done | bytes 196640 | tf_op jit(solution)/shard_map/ppermute | solution.py:15
  184.4 0.6 fusion.46
  185.0 0.0 collective-permute-done.9
  185.0 1.8 add_convert_fusion
  (12 shorter events, 0.2 us)
Async XLA Ops:
  6.5 12.7 %copy-start.5 = (f32[3,3,256]{2,1,0:T(4,128)S(1)}, f32[3,3,256]{2,1,0:T(4,128)}, u32[]{:S(2)}) copy-start(f32[3,3,256]{2,1,0:T(4,128)} %param.9) | copy-start | bytes 27652
  6.5 81.8 %all-gather.2.cloned.1.call-start = ((), (), s32[]{:S(2)}) async-start(), calls=%async_computation.1 | async-start | bytes 12976128 | tf_op jit(solution)/shard_map/all_gather | solution.py:48
  8.8 49.8 %collective-permute-start.1 = (bf16[384,1024]{1,0:T(8,128)(2,1)S(1)}, bf16[384,1024]{1,0:T(8,128)(2,1)}, u32[]{:S(2)}, u32[]{:S(2)}) collective-permute-start(bf16[384,1024]{1,0:T(8,128)(2,1)S(1)} %get-tuple-element.8), channel_id=1, source_target_pairs={{0,6},{2,0},{4,2},{6,4},{1,7},{3,1},{5,3},{7,5},{8,14},{10,8},{12,... | collective-permute-start | bytes 2359304 | tf_op jit(solution)/shard_map/ppermute | solution.py:15
  15.7 48.9 %collective-permute-start = (bf16[384,1024]{1,0:T(8,128)(2,1)S(1)}, bf16[384,1024]{1,0:T(8,128)(2,1)S(1)}, u32[]{:S(2)}, u32[]{:S(2)}) collective-permute-start(bf16[384,1024]{1,0:T(8,128)(2,1)S(1)} %get-tuple-element.7), channel_id=1, source_target_pairs={{0,2},{2,4},{4,6},{6,0},{1,3},{3,5},{5,7},{7,1},{8,10},{10,12},{12... | collective-permute-start | bytes 2359304 | tf_op jit(solution)/shard_map/ppermute | solution.py:15
  15.7 75.4 %collective-permute-start.2 = (bf16[384,1024]{1,0:T(8,128)(2,1)S(1)}, bf16[384,1024]{1,0:T(8,128)(2,1)}, u32[]{:S(2)}, u32[]{:S(2)}) collective-permute-start(bf16[384,1024]{1,0:T(8,128)(2,1)S(1)} %get-tuple-element.8), channel_id=1, source_target_pairs={{0,2},{2,4},{4,6},{6,0},{1,3},{3,5},{5,7},{7,1},{8,10},{10,12},{12... | collective-permute-start | bytes 2359304 | tf_op jit(solution)/shard_map/ppermute | solution.py:15
  16.9 80.5 %collective-permute-start.3 = (bf16[384,1024]{1,0:T(8,128)(2,1)S(1)}, bf16[384,1024]{1,0:T(8,128)(2,1)}, u32[]{:S(2)}, u32[]{:S(2)}) collective-permute-start(bf16[384,1024]{1,0:T(8,128)(2,1)S(1)} %get-tuple-element.7), channel_id=1, source_target_pairs={{0,6},{2,0},{4,2},{6,4},{1,7},{3,1},{5,3},{7,5},{8,14},{10,8},{12,... | collective-permute-start | bytes 2359304 | tf_op jit(solution)/shard_map/ppermute | solution.py:15
  58.6 55.7 %collective-permute-start.5 = (bf16[384,1024]{1,0:T(8,128)(2,1)}, bf16[384,1024]{1,0:T(8,128)(2,1)}, u32[]{:S(2)}, u32[]{:S(2)}) collective-permute-start(bf16[384,1024]{1,0:T(8,128)(2,1)} %collective-permute-done.1), channel_id=1, source_target_pairs={{0,6},{2,0},{4,2},{6,4},{1,7},{3,1},{5,3},{7,5},{8,14},{10,8},{12,... | collective-permute-start | bytes 2359304 | tf_op jit(solution)/shard_map/ppermute | solution.py:15
  64.6 56.5 %collective-permute-start.4 = (bf16[384,1024]{1,0:T(8,128)(2,1)S(1)}, bf16[384,1024]{1,0:T(8,128)(2,1)S(1)}, u32[]{:S(2)}, u32[]{:S(2)}) collective-permute-start(bf16[384,1024]{1,0:T(8,128)(2,1)S(1)} %collective-permute-done), channel_id=1, source_target_pairs={{0,2},{2,4},{4,6},{6,0},{1,3},{3,5},{5,7},{7,1},{8,10},{10,12},{12... | collective-permute-start | bytes 2359304 | tf_op jit(solution)/shard_map/ppermute | solution.py:15
  88.3 28.6 %copy-start.2 = (bf16[256,3,8192]{2,0,1:T(8,128)(2,1)S(1)}, bf16[256,3,8192]{2,0,1:T(8,128)(2,1)}, u32[]{:S(2)}) copy-start(bf16[256,3,8192]{2,0,1:T(8,128)(2,1)} %all-gather.2.cloned.1.call-done) | copy-start | bytes 37748740
  94.3 22.6 %copy-start.1 = (bf16[384,2048]{1,0:T(8,128)(2,1)S(1)}, bf16[384,2048]{1,0:T(8,128)(2,1)}, u32[]{:S(2)}) copy-start(bf16[384,2048]{1,0:T(8,128)(2,1)} %param.7) | copy-start | bytes 4718596
  122.2 8.0 %collective-permute-start.6 = (bf16[256,3,2]{2,0,1:T(8,128)(2,1)S(1)}, bf16[256,3,2]{2,0,1:T(8,128)(2,1)S(1)}, u32[]{:S(2)}, u32[]{:S(2)}) collective-permute-start(bf16[256,3,2]{2,0,1:T(8,128)(2,1)S(1)} %slice.51), channel_id=1, source_target_pairs={{0,8},{8,16},{16,24},{24,32},{32,40},{40,48},{48,56},{56,64},{64,7... | collective-permute-start | bytes 9224 | tf_op jit(solution)/shard_map/ppermute | solution.py:10
  130.8 1.2 copy-start.3
  134.7 20.0 %all-to-all-start = ((f32[32,16,256]{2,1,0:T(8,128)}), f32[32,16,256]{2,1,0:T(8,128)S(1)}, u32[]{:S(2)}, u32[]{:S(2)}) async-start(f32[32,16,256]{2,1,0:T(8,128)} %broadcast_in_dim.12), calls=%async_computation | async-start | bytes 1048576 | tf_op jit(solution)/shard_map/all_to_all | solution.py:81
  143.1 11.7 %copy-start.4 = (f32[16,256]{1,0:T(8,128)S(1)}, f32[16,256]{1,0:T(8,128)}, u32[]{:S(2)}) copy-start(f32[16,256]{1,0:T(8,128)} %param.11) | copy-start | bytes 49156
  154.7 5.8 %slice-start = ((s8[6291456]{0:T(1024)(128)(4,1)}), s8[4194304]{0:T(1024)(128)(4,1)S(1)}, s32[]{:S(2)}) async-start(s8[6291456]{0:T(1024)(128)(4,1)} %bitcast.43), calls=%async_computation.2 | async-start | bytes 8388608
  154.9 5.6 %slice-start.1 = ((s8[6291456]{0:T(1024)(128)(4,1)}), s8[2097152]{0:T(1024)(128)(4,1)S(1)}, s32[]{:S(2)}) async-start(s8[6291456]{0:T(1024)(128)(4,1)} %bitcast.43), calls=%async_computation.3 | async-start | bytes 4194304
  160.5 0.8 copy-start.6
  160.6 8.6 %copy-start = (bf16[1024,2048]{1,0:T(8,128)(2,1)S(1)}, bf16[1024,2048]{1,0:T(8,128)(2,1)}, u32[]{:S(2)}) copy-start(bf16[1024,2048]{1,0:T(8,128)(2,1)} %param.13) | copy-start | bytes 12582916
  161.5 12.5 %collective-permute-start.7 = (bf16[256,384]{1,0:T(8,128)(2,1)S(1)}, bf16[256,384]{1,0:T(8,128)(2,1)S(1)}, u32[]{:S(2)}, u32[]{:S(2)}) collective-permute-start(bf16[256,384]{1,0:T(8,128)(2,1)S(1)} %fusion.62), channel_id=1, source_target_pairs={{0,4},{2,6},{4,0},{6,2},{1,5},{3,7},{5,1},{7,3},{8,12},{10,14},{12... | collective-permute-start | bytes 589832 | tf_op jit(solution)/shard_map/ppermute | solution.py:15
  165.6 18.8 %collective-permute-start.8 = (bf16[256,384]{1,0:T(8,128)(2,1)S(1)}, bf16[256,384]{1,0:T(8,128)(2,1)S(1)}, u32[]{:S(2)}, u32[]{:S(2)}) collective-permute-start(bf16[256,384]{1,0:T(8,128)(2,1)S(1)} %fusion.62), channel_id=1, source_target_pairs={{0,2},{2,4},{4,6},{6,0},{1,3},{3,5},{5,7},{7,1},{8,10},{10,12},{12... | collective-permute-start | bytes 589832 | tf_op jit(solution)/shard_map/ppermute | solution.py:15
  168.0 17.0 %collective-permute-start.9 = (bf16[256,384]{1,0:T(8,128)(2,1)S(1)}, bf16[256,384]{1,0:T(8,128)(2,1)S(1)}, u32[]{:S(2)}, u32[]{:S(2)}) collective-permute-start(bf16[256,384]{1,0:T(8,128)(2,1)S(1)} %fusion.62), channel_id=1, source_target_pairs={{0,6},{2,0},{4,2},{6,4},{1,7},{3,1},{5,3},{7,5},{8,14},{10,8},{12,... | collective-permute-start | bytes 589832 | tf_op jit(solution)/shard_map/ppermute | solution.py:15
Sparse Core Ops, SparseCore 0:
  9.8 78.4 all-gather.1

commit v10 on v9

--- a/solution.py
+++ b/solution.py
@@ -102,6 +102,7 @@
     )
     intra = fall * prefix
     near = jnp.sum(gains[:, :, None] * intra, axis=0)
+    near, incoming = lax.optimization_barrier((near, incoming))
     onward = lax.optimization_barrier(jnp.exp(-decay[:, :, None] * (tau + 1.0)))
     conv = near + jnp.sum((gains * incoming)[:, :, None] * onward, axis=0)
     longc = (conv + skip[:, None] * z_f).astype(jnp.bfloat16)

time: 194 us -> 191 us (0.985)
  waiting for transfers between devices: 107 us -> 102 us
  other arithmetic: 7.88 us -> 10.5 us
    all_to_all x1, waiting for transfers between devices: 8.36 us -> 2.86 us  [on_device(): lax.all_to_all(jnp.broadcast_to(ending[None], (seq_count,) + ending.shape...]
    reduce_sum x1, other arithmetic: 0.74 us -> 3.38 us  [on_device(): conv = near + jnp.sum((gains * incoming)[:, :, None] * onward, axis=0)]
  transfers between devices with their start and end apart: 12 -> 12, of which waited for: 9 -> 9; matrix products, arithmetic and copies ran while one was open for 11% -> 14% of each run, Pallas kernels for 0% -> 0%
where the time goes in v10:
time: 191 us
  waiting for transfers between devices  102 us (53%)
  starting transfers between devices  38.1 us (20%)
  matrix products  24.2 us (13%)
  between operations  13.8 us (7%)
  other arithmetic  10.5 us (5%)
  local copies, waits for them, and re-layouts  2.51 us (1%)
    ppermute x9, waiting for transfers between devices, ring_shift(): lax.ppermute(value, axis, [(source, (source + steps) % count) for source...  71.9 us
    ppermute x9, starting transfers between devices, ring_shift(): lax.ppermute(value, axis, [(source, (source + steps) % count) for source...  24.1 us
    all_gather x1, waiting for transfers between devices, on_device(): w_full = lax.all_gather(w_in, 'seq', axis=2, tiled=True)  23.7 us
    dot_general x6, matrix products, on_device(): jnp.einsum('cgd,td->cgt', block_of(step, lo, hi), piece, preferred_elemen...  13.3 us
    all_to_all x1, starting transfers between devices, on_device(): lax.all_to_all(jnp.broadcast_to(ending[None], (seq_count,) + ending.shape...  8.38 us
    dot_general x1, matrix products, on_device(): jnp.einsum('mcs,st->mct', lifted, upper, precision=lax.Precision.HIGH, pr...  5.58 us
    ppermute x1, starting transfers between devices, from_behind(): lax.ppermute(value, axis, [(source, source + steps) for source in range(l...  5.56 us
  transfers between devices with their start and end apart: 12, of which 9 were waited for; matrix products, arithmetic and copies ran while one was open for 14% of the time, Pallas kernels for 0%

profile of v10, /device:TPU:1, one launch (start us, length us, event | category | flops | bytes accessed | tf_op | source)
XLA Modules:
  0.0 190.6 jit_solution(11390387578874193677)
XLA Ops:
  6.5 0.0 copy-start.5
  6.5 0.0 all-gather.2.cloned.1.call-start
  6.5 0.7 all-gather.2.cloned.1.call-update
  7.3 1.5 fusion.75
  8.8 6.9 %collective-permute-start.1 = (bf16[384,1024]{1,0:T(8,128)(2,1)S(1)}, bf16[384,1024]{1,0:T(8,128)(2,1)}, u32[]{:S(2)}, u32[]{:S(2)}) collective-permute-start(bf16[384,1024]{1,0:T(8,128)(2,1)S(1)} %get-tuple-element.10), channel_id=1, source_target_pairs={{0,6},{2,0},{4,2},{6,4},{1,7},{3,1},{5,3},{7,5},{8,14},{10,8},{12,... | collective-permute-start | bytes 2359304 | tf_op jit(solution)/shard_map/ppermute | solution.py:15
  15.7 0.0 collective-permute-start
  15.7 1.3 collective-permute-start.2
  16.9 2.3 %collective-permute-start.3 = (bf16[384,1024]{1,0:T(8,128)(2,1)S(1)}, bf16[384,1024]{1,0:T(8,128)(2,1)}, u32[]{:S(2)}, u32[]{:S(2)}) collective-permute-start(bf16[384,1024]{1,0:T(8,128)(2,1)S(1)} %get-tuple-element.9), channel_id=1, source_target_pairs={{0,6},{2,0},{4,2},{6,4},{1,7},{3,1},{5,3},{7,5},{8,14},{10,8},{12,... | collective-permute-start | bytes 2359304 | tf_op jit(solution)/shard_map/ppermute | solution.py:15
  19.4 0.0 copy-done.5
  19.4 39.2 %collective-permute-done.1 = bf16[384,1024]{1,0:T(8,128)(2,1)} collective-permute-done((bf16[384,1024]{1,0:T(8,128)(2,1)S(1)}, bf16[384,1024]{1,0:T(8,128)(2,1)}, u32[]{:S(2)}, u32[]{:S(2)}) %collective-permute-start.1) | collective-permute-done | bytes 786464 | tf_op jit(solution)/shard_map/ppermute | solution.py:15
  58.6 6.0 %collective-permute-start.5 = (bf16[384,1024]{1,0:T(8,128)(2,1)}, bf16[384,1024]{1,0:T(8,128)(2,1)}, u32[]{:S(2)}, u32[]{:S(2)}) collective-permute-start(bf16[384,1024]{1,0:T(8,128)(2,1)} %collective-permute-done.1), channel_id=1, source_target_pairs={{0,6},{2,0},{4,2},{6,4},{1,7},{3,1},{5,3},{7,5},{8,14},{10,8},{12,... | collective-permute-start | bytes 2359304 | tf_op jit(solution)/shard_map/ppermute | solution.py:15
  64.6 0.0 collective-permute-done
  64.6 0.0 collective-permute-start.4
  64.6 23.7 %all-gather.2.cloned.1.call-done = bf16[256,3,8192]{2,0,1:T(8,128)(2,1)} async-done(((bf16[256,3,256]{2,0,1:T(8,128)(2,1)}), bf16[256,3,8192]{2,0,1:T(8,128)(2,1)}) %all-gather.2.cloned.1.call-update) | async-done | bytes 12582928 | tf_op jit(solution)/shard_map/all_gather | solution.py:48
  88.3 0.0 copy-start.2
  88.3 2.8 %fusion.15 = f32[256,3,384]{2,0,1:T(8,128)S(1)} fusion(bf16[256,3,8192]{2,0,1:T(8,128)(2,1)} %all-gather.2.cloned.1.call-done, s32[]{:T(128)S(6)} %select_n.75, bf16[384,1024]{1,0:T(8,128)(2,1)} %collective-permute-done.1), kind=kOutput, calls=%fused_computation.20 | convolution fusion | flops 603979776 | bytes 3538948 | tf_op jit(solution)/shard_map/cgd,td->cgt/dot_general | solution.py:56
  91.1 0.0 collective-permute-done.2
  91.1 3.2 %fusion.13 = f32[256,3,384]{2,0,1:T(8,128)S(1)} fusion(bf16[256,3,8192]{2,0,1:T(8,128)(2,1)} %all-gather.2.cloned.1.call-done, s32[]{:T(128)S(6)} %select_n.76, bf16[384,1024]{1,0:T(8,128)(2,1)} %collective-permute-done.2), kind=kOutput, calls=%fused_computation.18 | convolution fusion | flops 603979776 | bytes 3538948 | tf_op jit(solution)/shard_map/cgd,td->cgt/dot_general | solution.py:56
  94.3 0.0 copy-start.1
  94.3 3.1 %collective-permute-done.3 = bf16[384,1024]{1,0:T(8,128)(2,1)} collective-permute-done((bf16[384,1024]{1,0:T(8,128)(2,1)S(1)}, bf16[384,1024]{1,0:T(8,128)(2,1)}, u32[]{:S(2)}, u32[]{:S(2)}) %collective-permute-start.3) | collective-permute-done | bytes 786464 | tf_op jit(solution)/shard_map/ppermute | solution.py:15
  97.4 2.6 %fusion.11 = f32[256,3,384]{2,0,1:T(8,128)S(1)} fusion(bf16[256,3,8192]{2,0,1:T(8,128)(2,1)} %all-gather.2.cloned.1.call-done, s32[]{:T(128)S(6)} %select_n.77, bf16[384,1024]{1,0:T(8,128)(2,1)} %collective-permute-done.3), kind=kOutput, calls=%fused_computation.16 | convolution fusion | flops 603979776 | bytes 3538948 | tf_op jit(solution)/shard_map/cgd,td->cgt/dot_general | solution.py:56
  100.0 14.3 %collective-permute-done.5 = bf16[384,1024]{1,0:T(8,128)(2,1)} collective-permute-done((bf16[384,1024]{1,0:T(8,128)(2,1)}, bf16[384,1024]{1,0:T(8,128)(2,1)}, u32[]{:S(2)}, u32[]{:S(2)}) %collective-permute-start.5) | collective-permute-done | bytes 786464 | tf_op jit(solution)/shard_map/ppermute | solution.py:15
  114.3 2.6 %fusion.7 = f32[256,3,384]{2,0,1:T(8,128)S(1)} fusion(bf16[256,3,8192]{2,0,1:T(8,128)(2,1)} %all-gather.2.cloned.1.call-done, s32[]{:T(128)S(6)} %select_n.80, bf16[384,1024]{1,0:T(8,128)(2,1)} %collective-permute-done.5), kind=kOutput, calls=%fused_computation.12 | convolution fusion | flops 603979776 | bytes 3538948 | tf_op jit(solution)/shard_map/cgd,td->cgt/dot_general | solution.py:56
  116.9 0.0 copy-done.2
  116.9 0.0 copy-done.1
  116.9 1.8 fusion.4
  118.7 1.0 fusion.34
  119.8 1.2 collective-permute-done.4
  121.0 1.0 fusion.37
  122.1 0.1 slice.51
  122.2 5.6 %collective-permute-start.6 = (bf16[256,3,2]{2,0,1:T(8,128)(2,1)S(1)}, bf16[256,3,2]{2,0,1:T(8,128)(2,1)S(1)}, u32[]{:S(2)}, u32[]{:S(2)}) collective-permute-start(bf16[256,3,2]{2,0,1:T(8,128)(2,1)S(1)} %slice.51), channel_id=1, source_target_pairs={{0,8},{8,16},{16,24},{24,32},{32,40},{40,48},{48,56},{56,64},{64,7... | collective-permute-start | bytes 9224 | tf_op jit(solution)/shard_map/ppermute | solution.py:10
  127.8 2.4 %collective-permute-done.6 = bf16[256,3,2]{2,0,1:T(8,128)(2,1)S(1)} collective-permute-done((bf16[256,3,2]{2,0,1:T(8,128)(2,1)S(1)}, bf16[256,3,2]{2,0,1:T(8,128)(2,1)S(1)}, u32[]{:S(2)}, u32[]{:S(2)}) %collective-permute-start.6) | collective-permute-done | bytes 3104 | tf_op jit(solution)/shard_map/ppermute | solution.py:10
  130.2 0.4 pad_maximum_fusion
  130.6 0.2 convert_element_type.36
  130.8 0.0 copy-start.4
  130.8 1.1 fusion.40
  131.9 0.0 copy-start.3
  132.0 0.0 copy-done.4
  132.0 1.9 fusion
  133.8 0.0 copy-done.3
  133.9 0.9 broadcast_in_dim.12
  134.7 8.4 %all-to-all-start = ((f32[32,16,256]{2,1,0:T(8,128)}), f32[32,16,256]{2,1,0:T(8,128)S(1)}, u32[]{:S(2)}, u32[]{:S(2)}) async-start(f32[32,16,256]{2,1,0:T(8,128)} %broadcast_in_dim.12), calls=%async_computation | async-start | bytes 1048576 | tf_op jit(solution)/shard_map/all_to_all | solution.py:81
  143.1 3.1 %multiply_exponential_fusion = f32[16,256,384]{2,1,0:T(8,128)} fusion(f32[384]{0:T(512)S(1)} %iota_add_fusion, f32[16,256]{1,0:T(8,128)S(1)} %get-tuple-element.13), kind=kLoop, calls=%fused_computation.1 | loop fusion | flops 1572864 | bytes 6309376 | tf_op jit(solution)/shard_map/exp | solution.py:106
  146.3 5.6 %multiply_reduce_fusion.1 = f32[256,384]{1,0:T(8,128)S(1)} fusion(f32[16,256]{1,0:T(8,128)S(1)} %get-tuple-element.13, f32[16,256]{1,0:T(8,128)S(1)} %get-tuple-element.12, f32[256,384]{1,0:T(8,128)S(1)} %convert_element_type.39, f32[16,256]{1,0:T(8,128)S(1)} %copy-done.4), kind=kOutput, calls=%fused_computation.2 | convolution fusion | flops 3633364992 | bytes 835584 | tf_op jit(solution)/shard_map/mcs,st->mct/dot_general | solution.py:96
  151.9 2.9 %all-to-all-done = f32[32,16,256]{2,1,0:T(8,128)S(1)} async-done(((f32[32,16,256]{2,1,0:T(8,128)}), f32[32,16,256]{2,1,0:T(8,128)S(1)}, u32[]{:S(2)}, u32[]{:S(2)}) %all-to-all-start) | async-done | bytes 524320 | tf_op jit(solution)/shard_map/all_to_all | solution.py:81
  154.7 0.2 multiply_reduce_fusion.2
  154.9 0.0 copy-start.6
  154.9 0.0 copy-start
  154.9 3.4 %multiply_reduce_fusion = f32[256,384]{1,0:T(8,128)S(1)} fusion(f32[16,256,384]{2,1,0:T(8,128)} %multiply_exponential_fusion, f32[16,256]{1,0:T(8,128)S(1)} %mul.212), kind=kLoop, calls=%fused_computation | loop fusion | flops 3047424 | bytes 6701056 | tf_op jit(solution)/shard_map/reduce_sum | solution.py:107
  158.3 0.0 copy-done.6
  158.3 0.1 add_convert_fusion.1
  158.5 4.0 %collective-permute-start.7 = (bf16[256,384]{1,0:T(8,128)(2,1)S(1)}, bf16[256,384]{1,0:T(8,128)(2,1)S(1)}, u32[]{:S(2)}, u32[]{:S(2)}) collective-permute-start(bf16[256,384]{1,0:T(8,128)(2,1)S(1)} %fusion.62), channel_id=1, source_target_pairs={{0,4},{2,6},{4,0},{6,2},{1,5},{3,7},{5,1},{7,3},{8,12},{10,14},{12... | collective-permute-start | bytes 589832 | tf_op jit(solution)/shard_map/ppermute | solution.py:15
  162.5 2.4 %collective-permute-start.8 = (bf16[256,384]{1,0:T(8,128)(2,1)S(1)}, bf16[256,384]{1,0:T(8,128)(2,1)S(1)}, u32[]{:S(2)}, u32[]{:S(2)}) collective-permute-start(bf16[256,384]{1,0:T(8,128)(2,1)S(1)} %fusion.62), channel_id=1, source_target_pairs={{0,2},{2,4},{4,6},{6,0},{1,3},{3,5},{5,7},{7,1},{8,10},{10,12},{12... | collective-permute-start | bytes 589832 | tf_op jit(solution)/shard_map/ppermute | solution.py:15
  164.9 1.2 collective-permute-start.9
  166.1 0.0 copy-done
  166.1 0.6 fusion.50
  166.7 4.2 %collective-permute-done.7 = bf16[256,384]{1,0:T(8,128)(2,1)S(1)} collective-permute-done((bf16[256,384]{1,0:T(8,128)(2,1)S(1)}, bf16[256,384]{1,0:T(8,128)(2,1)S(1)}, u32[]{:S(2)}, u32[]{:S(2)}) %collective-permute-start.7) | collective-permute-done | bytes 196640 | tf_op jit(solution)/shard_map/ppermute | solution.py:15
  171.0 0.6 fusion.48
  171.6 9.8 %collective-permute-done.8 = bf16[256,384]{1,0:T(8,128)(2,1)S(1)} collective-permute-done((bf16[256,384]{1,0:T(8,128)(2,1)S(1)}, bf16[256,384]{1,0:T(8,128)(2,1)S(1)}, u32[]{:S(2)}, u32[]{:S(2)}) %collective-permute-start.8) | collective-permute-done | bytes 196640 | tf_op jit(solution)/shard_map/ppermute | solution.py:15
  181.4 0.6 fusion.46
  182.0 0.0 collective-permute-done.9
  182.0 1.8 add_convert_fusion
  (9 shorter events, 0.2 us)
Async XLA Ops:
  6.5 12.8 %copy-start.5 = (f32[3,3,256]{2,1,0:T(4,128)S(1)}, f32[3,3,256]{2,1,0:T(4,128)}, u32[]{:S(2)}) copy-start(f32[3,3,256]{2,1,0:T(4,128)} %param.9) | copy-start | bytes 27652
  6.5 81.8 %all-gather.2.cloned.1.call-start = ((), (), s32[]{:S(2)}) async-start(), calls=%async_computation.1 | async-start | bytes 12976128 | tf_op jit(solution)/shard_map/all_gather | solution.py:48
  8.8 49.8 %collective-permute-start.1 = (bf16[384,1024]{1,0:T(8,128)(2,1)S(1)}, bf16[384,1024]{1,0:T(8,128)(2,1)}, u32[]{:S(2)}, u32[]{:S(2)}) collective-permute-start(bf16[384,1024]{1,0:T(8,128)(2,1)S(1)} %get-tuple-element.10), channel_id=1, source_target_pairs={{0,6},{2,0},{4,2},{6,4},{1,7},{3,1},{5,3},{7,5},{8,14},{10,8},{12,... | collective-permute-start | bytes 2359304 | tf_op jit(solution)/shard_map/ppermute | solution.py:15
  15.7 48.9 %collective-permute-start = (bf16[384,1024]{1,0:T(8,128)(2,1)S(1)}, bf16[384,1024]{1,0:T(8,128)(2,1)S(1)}, u32[]{:S(2)}, u32[]{:S(2)}) collective-permute-start(bf16[384,1024]{1,0:T(8,128)(2,1)S(1)} %get-tuple-element.9), channel_id=1, source_target_pairs={{0,2},{2,4},{4,6},{6,0},{1,3},{3,5},{5,7},{7,1},{8,10},{10,12},{12... | collective-permute-start | bytes 2359304 | tf_op jit(solution)/shard_map/ppermute | solution.py:15
  15.7 75.4 %collective-permute-start.2 = (bf16[384,1024]{1,0:T(8,128)(2,1)S(1)}, bf16[384,1024]{1,0:T(8,128)(2,1)}, u32[]{:S(2)}, u32[]{:S(2)}) collective-permute-start(bf16[384,1024]{1,0:T(8,128)(2,1)S(1)} %get-tuple-element.10), channel_id=1, source_target_pairs={{0,2},{2,4},{4,6},{6,0},{1,3},{3,5},{5,7},{7,1},{8,10},{10,12},{12... | collective-permute-start | bytes 2359304 | tf_op jit(solution)/shard_map/ppermute | solution.py:15
  16.9 80.5 %collective-permute-start.3 = (bf16[384,1024]{1,0:T(8,128)(2,1)S(1)}, bf16[384,1024]{1,0:T(8,128)(2,1)}, u32[]{:S(2)}, u32[]{:S(2)}) collective-permute-start(bf16[384,1024]{1,0:T(8,128)(2,1)S(1)} %get-tuple-element.9), channel_id=1, source_target_pairs={{0,6},{2,0},{4,2},{6,4},{1,7},{3,1},{5,3},{7,5},{8,14},{10,8},{12,... | collective-permute-start | bytes 2359304 | tf_op jit(solution)/shard_map/ppermute | solution.py:15
  58.6 55.7 %collective-permute-start.5 = (bf16[384,1024]{1,0:T(8,128)(2,1)}, bf16[384,1024]{1,0:T(8,128)(2,1)}, u32[]{:S(2)}, u32[]{:S(2)}) collective-permute-start(bf16[384,1024]{1,0:T(8,128)(2,1)} %collective-permute-done.1), channel_id=1, source_target_pairs={{0,6},{2,0},{4,2},{6,4},{1,7},{3,1},{5,3},{7,5},{8,14},{10,8},{12,... | collective-permute-start | bytes 2359304 | tf_op jit(solution)/shard_map/ppermute | solution.py:15
  64.6 56.5 %collective-permute-start.4 = (bf16[384,1024]{1,0:T(8,128)(2,1)S(1)}, bf16[384,1024]{1,0:T(8,128)(2,1)S(1)}, u32[]{:S(2)}, u32[]{:S(2)}) collective-permute-start(bf16[384,1024]{1,0:T(8,128)(2,1)S(1)} %collective-permute-done), channel_id=1, source_target_pairs={{0,2},{2,4},{4,6},{6,0},{1,3},{3,5},{5,7},{7,1},{8,10},{10,12},{12... | collective-permute-start | bytes 2359304 | tf_op jit(solution)/shard_map/ppermute | solution.py:15
  88.3 28.6 %copy-start.2 = (bf16[256,3,8192]{2,0,1:T(8,128)(2,1)S(1)}, bf16[256,3,8192]{2,0,1:T(8,128)(2,1)}, u32[]{:S(2)}) copy-start(bf16[256,3,8192]{2,0,1:T(8,128)(2,1)} %all-gather.2.cloned.1.call-done) | copy-start | bytes 37748740
  94.3 22.6 %copy-start.1 = (bf16[384,2048]{1,0:T(8,128)(2,1)S(1)}, bf16[384,2048]{1,0:T(8,128)(2,1)}, u32[]{:S(2)}) copy-start(bf16[384,2048]{1,0:T(8,128)(2,1)} %param.7) | copy-start | bytes 4718596
  122.2 8.0 %collective-permute-start.6 = (bf16[256,3,2]{2,0,1:T(8,128)(2,1)S(1)}, bf16[256,3,2]{2,0,1:T(8,128)(2,1)S(1)}, u32[]{:S(2)}, u32[]{:S(2)}) collective-permute-start(bf16[256,3,2]{2,0,1:T(8,128)(2,1)S(1)} %slice.51), channel_id=1, source_target_pairs={{0,8},{8,16},{16,24},{24,32},{32,40},{40,48},{48,56},{56,64},{64,7... | collective-permute-start | bytes 9224 | tf_op jit(solution)/shard_map/ppermute | solution.py:10
  130.8 1.2 copy-start.4
  131.9 2.0 %copy-start.3 = (f32[16,256]{1,0:T(8,128)S(1)}, f32[16,256]{1,0:T(8,128)}, u32[]{:S(2)}) copy-start(f32[16,256]{1,0:T(8,128)} %param.11) | copy-start | bytes 49156
  134.7 20.0 %all-to-all-start = ((f32[32,16,256]{2,1,0:T(8,128)}), f32[32,16,256]{2,1,0:T(8,128)S(1)}, u32[]{:S(2)}, u32[]{:S(2)}) async-start(f32[32,16,256]{2,1,0:T(8,128)} %broadcast_in_dim.12), calls=%async_computation | async-start | bytes 1048576 | tf_op jit(solution)/shard_map/all_to_all | solution.py:81
  154.9 3.4 %copy-start.6 = (f32[256]{0:T(256)S(1)}, f32[256]{0:T(256)}, u32[]{:S(2)}) copy-start(f32[256]{0:T(256)} %param.12) | copy-start | bytes 3076
  154.9 11.2 %copy-start = (bf16[1024,2048]{1,0:T(8,128)(2,1)S(1)}, bf16[1024,2048]{1,0:T(8,128)(2,1)}, u32[]{:S(2)}) copy-start(bf16[1024,2048]{1,0:T(8,128)(2,1)} %param.13) | copy-start | bytes 12582916
  158.5 12.5 %collective-permute-start.7 = (bf16[256,384]{1,0:T(8,128)(2,1)S(1)}, bf16[256,384]{1,0:T(8,128)(2,1)S(1)}, u32[]{:S(2)}, u32[]{:S(2)}) collective-permute-start(bf16[256,384]{1,0:T(8,128)(2,1)S(1)} %fusion.62), channel_id=1, source_target_pairs={{0,4},{2,6},{4,0},{6,2},{1,5},{3,7},{5,1},{7,3},{8,12},{10,14},{12... | collective-permute-start | bytes 589832 | tf_op jit(solution)/shard_map/ppermute | solution.py:15
  162.5 18.8 %collective-permute-start.8 = (bf16[256,384]{1,0:T(8,128)(2,1)S(1)}, bf16[256,384]{1,0:T(8,128)(2,1)S(1)}, u32[]{:S(2)}, u32[]{:S(2)}) collective-permute-start(bf16[256,384]{1,0:T(8,128)(2,1)S(1)} %fusion.62), channel_id=1, source_target_pairs={{0,2},{2,4},{4,6},{6,0},{1,3},{3,5},{5,7},{7,1},{8,10},{10,12},{12... | collective-permute-start | bytes 589832 | tf_op jit(solution)/shard_map/ppermute | solution.py:15
  164.9 17.0 %collective-permute-start.9 = (bf16[256,384]{1,0:T(8,128)(2,1)S(1)}, bf16[256,384]{1,0:T(8,128)(2,1)S(1)}, u32[]{:S(2)}, u32[]{:S(2)}) collective-permute-start(bf16[256,384]{1,0:T(8,128)(2,1)S(1)} %fusion.62), channel_id=1, source_target_pairs={{0,6},{2,0},{4,2},{6,4},{1,7},{3,1},{5,3},{7,5},{8,14},{10,8},{12,... | collective-permute-start | bytes 589832 | tf_op jit(solution)/shard_map/ppermute | solution.py:15
Sparse Core Ops, SparseCore 0:
  9.8 78.4 all-gather.1
